TPU v7x, 256 devices: a whole 4x4x8 slice. The times are simulated.
256 devices in a mesh: expert: 128 (over x, z, y), tensor: 2 (over core).
Axes of the slice: x: 4, y: 4, z: 8, core: 2. Of those that a mesh axis runs over, the one named last changes fastest.
Arguments:
- features: bfloat16 [16384, 3584], P('expert', 'tensor'), may hold values from -6 to 6
- cotangent: bfloat16 [16384, 3584], P('expert', 'tensor'), may hold values from -6 to 6
- expert_ids: int32 [16384, 2], P('expert'), may hold values from 0 to 127, all different within a row; in each aligned block of 128 rows (0 to 127, 128 to 255, ...) at most 3 rows name the same one
- route_weight: bfloat16 [16384, 2], P('expert'), may hold values from 0.099609375 to 1
- gate_weight: bfloat16 [128, 3584, 1024], P('expert', None, 'tensor'), may hold values from -0.09375 to 0.09375
- up_weight: bfloat16 [128, 3584, 1024], P('expert', None, 'tensor'), may hold values from -0.09375 to 0.09375
- down_weight: bfloat16 [128, 1024, 3584], P('expert', 'tensor'), may hold values from -0.1875 to 0.1875
Outputs:
- input_grad: bfloat16 [16384, 3584], P('expert', 'tensor')
Inputs may be any that keep to these rules, and one draw needn't show every extreme that they name: `expert_ids`: each token names 2 different experts. Among the 128 tokens of one device (aligned blocks of rows) no expert is named by more than 3 tokens, a bound that some block reaches.
All inputs are finite; a program needn't handle non-finite values.
Results may differ from a plain program's by a relative error of at most 0.0058.
Values may be sent and summed in bfloat16 or wider, within the bound.
No kernel may reach another device: no remote copies, remote signals or barrier semaphores. Data moves between devices by JAX's collectives and lax.ppermute only.
A program may use at most 128 MiB of HBM per device.

v0:
```python
import jax
import jax.numpy as jnp
from jax import lax
from jax.sharding import PartitionSpec as P


def expert_rows(inputs, cotan_rows, weights, gate_w, up_w, down_w):
    gate_pre = jnp.dot(inputs, gate_w, preferred_element_type=jnp.float32)
    up_pre = jnp.dot(inputs, up_w, preferred_element_type=jnp.float32)
    hidden_grad = lax.dot_general(
        cotan_rows, down_w, (((1,), (1,)), ((), ())), preferred_element_type=jnp.float32
    )
    hidden_grad = hidden_grad * weights.astype(jnp.float32)[:, None]
    sigmoid_gate = jax.nn.sigmoid(gate_pre)
    gate_grad = (
        hidden_grad * up_pre * sigmoid_gate * (1.0 + gate_pre * (1.0 - sigmoid_gate))
    ).astype(jnp.bfloat16)
    up_grad = (hidden_grad * gate_pre * sigmoid_gate).astype(jnp.bfloat16)
    first = lax.dot_general(
        gate_grad, gate_w, (((1,), (1,)), ((), ())), preferred_element_type=jnp.float32
    )
    second = lax.dot_general(
        up_grad, up_w, (((1,), (1,)), ((), ())), preferred_element_type=jnp.float32
    )
    return first + second


def per_device(features, cotangent, expert_ids, route_weight, gate_weight, up_weight, down_weight):
    experts = lax.axis_size("expert")
    tok_rows, top = expert_ids.shape
    routes = tok_rows * top
    capacity = 3 * tok_rows * top // (2 * experts)
    total = experts * capacity
    flat_ids = expert_ids.reshape(routes)
    onehot = (flat_ids[:, None] == jnp.arange(experts, dtype=jnp.int32)[None, :]).astype(jnp.int32)
    ranks = jnp.sum((jnp.cumsum(onehot, axis=0) - 1) * onehot, axis=1)
    destination = flat_ids * capacity + ranks
    source = (
        jnp.full((total,), -1, jnp.int32).at[destination].set(jnp.arange(routes, dtype=jnp.int32))
    )
    filled = source >= 0
    safe_source = jnp.maximum(source, 0)
    token_of = safe_source // top
    slot_weight = jnp.where(
        filled, route_weight.reshape(routes)[safe_source], jnp.zeros((), jnp.bfloat16)
    )
    slot_weight = slot_weight.reshape(experts, capacity)

    def packed_rows(rows):
        picked = jnp.where(filled[:, None], rows[token_of], jnp.zeros((), rows.dtype))
        return picked.reshape(experts, capacity, rows.shape[1])

    whole_x, whole_dy = (
        lax.all_gather(features, "tensor", axis=1, tiled=True),
        lax.all_gather(cotangent, "tensor", axis=1, tiled=True),
    )
    recv_x, recv_dy, recv_w = (
        lax.all_to_all(packed_rows(whole_x), "expert", split_axis=0, concat_axis=0, tiled=True),
        lax.all_to_all(packed_rows(whole_dy), "expert", split_axis=0, concat_axis=0, tiled=True),
        lax.all_to_all(slot_weight, "expert", split_axis=0, concat_axis=0, tiled=True),
    )
    width = recv_x.shape[2]
    rows_x = recv_x.reshape(total, width)
    rows_dy = recv_dy.reshape(total, width)
    rows_w = recv_w.reshape(total)
    gate_w = gate_weight[0]
    up_w = up_weight[0]
    down_w = down_weight[0]
    partial_grad = expert_rows(rows_x, rows_dy, rows_w, gate_w, up_w, down_w)
    half_width = width // lax.axis_size("tensor")
    summed = lax.psum(partial_grad, "tensor")
    my_share = lax.dynamic_slice_in_dim(
        summed, lax.axis_index("tensor") * half_width, half_width, 1
    )
    outgoing = my_share.astype(jnp.bfloat16).reshape(experts, capacity, half_width)
    returned = lax.all_to_all(outgoing, "expert", split_axis=0, concat_axis=0, tiled=True)
    per_route = returned.reshape(total, half_width)[destination].astype(jnp.float32)
    per_route = per_route.reshape(tok_rows, top, half_width)
    return jnp.sum(per_route, axis=1).astype(jnp.bfloat16)


def solution(mesh):
    in_specs = (
        P("expert", "tensor"),
        P("expert", "tensor"),
        P("expert", None),
        P("expert", None),
        P("expert", None, "tensor"),
        P("expert", None, "tensor"),
        P("expert", "tensor", None),
    )
    out_specs = P("expert", "tensor")
    return jax.shard_map(
        per_device, mesh=mesh, in_specs=in_specs, out_specs=out_specs, check_vma=False
    )
```

profile of v0, /device:TPU:32, one launch (start us, length us, event | category | flops | bytes accessed | tf_op | source)
XLA Modules:
  0.0 365.3 jit_solution(13094932849750307494)
XLA Ops:
  2.7 1.4 scatter_custom_fusion
  5.0 2.7 gather_fusion.1
  8.6 15.0 %all-to-all-start.1 = ((bf16[128,1,3]{2,1,0:T(2,128)(2,1)}), bf16[128,1,3]{2,1,0:T(2,128)(2,1)S(1)}, u32[]{:S(2)}, u32[]{:S(2)}) async-start(bf16[128,1,3]{2,1,0:T(2,128)(2,1)} %all_to_all.20), calls=%async_computation.1 | async-start | bytes 131072 | tf_op jit(solution)/shard_map/all_to_all | solution.py:60
  23.9 2.7 all_gather.6
  26.6 3.9 %gather_fusion = bf16[384,3584]{1,0:T(8,128)(2,1)} fusion(bf16[128,3584]{1,0:T(8,128)(2,1)S(1)} %all_gather.6, s32[1024]{0:T(1024)S(1)} %pad_clamp_fusion.2), kind=kCustom, calls=%fused_computation | custom fusion | bytes 5506560 | tf_op jit(solution)/shard_map/gather | solution.py:50
  30.5 6.7 %gather.19 = bf16[128,3,3584]{2,1,0:T(4,128)(2,1)} reshape(bf16[384,3584]{1,0:T(8,128)(2,1)} %gather_fusion) | data formatting | bytes 5505024 | tf_op jit(solution)/shard_map/gather | solution.py:50
  37.2 2.5 all_gather.7
  39.6 3.9 %gather_fusion.2 = bf16[384,3584]{1,0:T(8,128)(2,1)} fusion(bf16[128,3584]{1,0:T(8,128)(2,1)S(1)} %all_gather.7, s32[1024]{0:T(1024)S(1)} %pad_clamp_fusion.2), kind=kCustom, calls=%fused_computation.2 | custom fusion | bytes 5506560 | tf_op jit(solution)/shard_map/gather | solution.py:50
  43.5 6.7 %gather.22 = bf16[128,3,3584]{2,1,0:T(4,128)(2,1)} reshape(bf16[384,3584]{1,0:T(8,128)(2,1)} %gather_fusion.2) | data formatting | bytes 5505024 | tf_op jit(solution)/shard_map/gather | solution.py:50
  50.2 8.1 %broadcast_select_fusion = (bf16[128,3,3584]{2,1,0:T(4,128)(2,1)}, bf16[128,3,3584]{2,1,0:T(4,128)(2,1)}) fusion(bf16[128,3,3584]{2,1,0:T(4,128)(2,1)} %gather.22, pred[128,3]{1,0:T(8,128)(4,1)S(1)} %broadcast_in_dim.39, bf16[128,3,3584]{2,1,0:T(4,128)(2,1)} %gather.19), kind=kLoop, calls=%fused_computation.15 | loop fusion | flops 2752512 | bytes 11010432 | tf_op jit(solution)/shard_map/jit(_where)/select_n | solution.py:50
  58.3 100.3 %all_to_all.25 = bf16[128,3,3584]{2,1,0:T(4,128)(2,1)} all-to-all(bf16[128,3,3584]{2,1,0:T(4,128)(2,1)} %get-tuple-element.7), channel_id=1, replica_groups=mesh['expert'=128,'tensor'=2] {'expert'}, dimensions={0} | all-to-all | bytes 5505024 | tf_op jit(solution)/shard_map/all_to_all | solution.py:58
  158.6 7.7 %all-to-all-start = ((bf16[128,3,3584]{2,1,0:T(4,128)(2,1)}), bf16[128,3,3584]{2,1,0:T(4,128)(2,1)}, u32[]{:S(2)}, u32[]{:S(2)}) async-start(bf16[128,3,3584]{2,1,0:T(4,128)(2,1)} %get-tuple-element.8), calls=%async_computation | async-start | bytes 7340032 | tf_op jit(solution)/shard_map/all_to_all | solution.py:59
  166.7 5.6 %reshape.95 = bf16[384,3584]{1,0:T(8,128)(2,1)S(1)} reshape(bf16[128,3,3584]{2,1,0:T(4,128)(2,1)} %all_to_all.25) | data formatting | bytes 5505024 | tf_op jit(solution)/shard_map/reshape | solution.py:63
  172.3 3.6 fusion.2
  176.0 75.9 %all-to-all-done = bf16[128,3,3584]{2,1,0:T(4,128)(2,1)} async-done(((bf16[128,3,3584]{2,1,0:T(4,128)(2,1)}), bf16[128,3,3584]{2,1,0:T(4,128)(2,1)}, u32[]{:S(2)}, u32[]{:S(2)}) %all-to-all-start) | async-done | bytes 2752544 | tf_op jit(solution)/shard_map/all_to_all | solution.py:59
  251.9 7.0 %reshape.93 = bf16[384,3584]{1,0:T(8,128)(2,1)} reshape(bf16[128,3,3584]{2,1,0:T(4,128)(2,1)} %all-to-all-done) | data formatting | bytes 5505024 | tf_op jit(solution)/shard_map/reshape | solution.py:64
  258.9 5.4 %fusion.9 = f32[384,512]{1,0:T(8,128)} fusion(bf16[384,3584]{1,0:T(8,128)(2,1)} %reshape.93, bf16[1,512,3584]{2,1,0:T(8,128)(2,1)} %param.13, f32[384]{0:T(512)S(1)} %reshape.98), kind=kOutput, calls=%fused_computation.18 | convolution fusion | flops 1409482752 | bytes 7210496 | tf_op jit(solution)/shard_map/dot_general | solution.py:10
  264.3 9.0 %fusion = f32[384,3584]{1,0:T(8,128)} fusion(bf16[1,3584,512]{2,1,0:T(8,128)(2,1)} %param.11, f32[384,512]{1,0:T(8,128)} %fusion.9, bf16[384,3584]{1,0:T(8,128)(2,1)S(1)} %reshape.95, bf16[1,3584,512]{2,1,0:T(8,128)(2,1)} %param.12, f32[384,512]{1,0:T(8,128)S(1)} %fusion.2), kind=kOutput, calls=%fused_computation.6 | convolution fusion | flops 2820538368 | bytes 17170432 | tf_op jit(solution)/shard_map/dot_general | solution.py:19
  273.3 7.9 %convolution_add_fusion = f32[384,3584]{1,0:T(8,128)} fusion(f32[384,3584]{1,0:T(8,128)} %fusion, bf16[1,3584,512]{2,1,0:T(8,128)(2,1)} %param.12, f32[384,512]{1,0:T(8,128)} %fusion.9, f32[384,512]{1,0:T(8,128)S(1)} %fusion.2), kind=kOutput, calls=%fused_computation.5 | convolution fusion | flops 1411842048 | bytes 16252928 | tf_op jit(solution)/shard_map/dot_general | solution.py:22
  281.2 18.2 %all-reduce.1 = bf16[384,3584]{1,0:T(8,128)(2,1)S(1)} all-reduce(f32[384,3584]{1,0:T(8,128)} %convolution_add_fusion), channel_id=1, replica_groups=mesh['expert'=128,'tensor'=2] {'tensor'}, use_global_device_ids=true, to_apply=%region_4.5 | all-reduce | flops 1376256 | bytes 8257536 | tf_op jit(solution)/shard_map/psum | solution.py:71
  300.6 3.9 %reshape.96 = bf16[128,3,1792]{2,1,0:T(4,128)(2,1)} reshape(bf16[384,1792]{1,0:T(8,128)(2,1)} %dynamic-slice_convert_fusion) | data formatting | bytes 2752512 | tf_op jit(solution)/shard_map/reshape | solution.py:75
  304.5 7.3 %all-to-all-start.3 = ((bf16[128,3,1792]{2,1,0:T(4,128)(2,1)}), bf16[128,3,1792]{2,1,0:T(4,128)(2,1)S(1)}, u32[]{:S(2)}, u32[]{:S(2)}) async-start(bf16[128,3,1792]{2,1,0:T(4,128)(2,1)} %reshape.96), calls=%async_computation.3 | async-start | bytes 3670016 | tf_op jit(solution)/shard_map/all_to_all | solution.py:76
  311.8 47.3 %all-to-all-done.3 = bf16[128,3,1792]{2,1,0:T(4,128)(2,1)S(1)} async-done(((bf16[128,3,1792]{2,1,0:T(4,128)(2,1)}), bf16[128,3,1792]{2,1,0:T(4,128)(2,1)S(1)}, u32[]{:S(2)}, u32[]{:S(2)}) %all-to-all-start.3) | async-done | bytes 1376288 | tf_op jit(solution)/shard_map/all_to_all | solution.py:76
  362.0 3.2 reduce_sum.25
  (34 shorter events, 9.2 us)
Async XLA Ops:
  8.6 49.7 %all-to-all-start.1 = ((bf16[128,1,3]{2,1,0:T(2,128)(2,1)}), bf16[128,1,3]{2,1,0:T(2,128)(2,1)S(1)}, u32[]{:S(2)}, u32[]{:S(2)}) async-start(bf16[128,1,3]{2,1,0:T(2,128)(2,1)} %all_to_all.20), calls=%async_computation.1 | async-start | bytes 131072 | tf_op jit(solution)/shard_map/all_to_all | solution.py:60
  30.5 6.7 %copy-start = (bf16[128,1792]{1,0:T(8,128)(2,1)S(1)}, bf16[128,1792]{1,0:T(8,128)(2,1)}, u32[]{:S(2)}) copy-start(bf16[128,1792]{1,0:T(8,128)(2,1)} %param.7) | copy-start | bytes 1376260
  158.6 93.2 %all-to-all-start = ((bf16[128,3,3584]{2,1,0:T(4,128)(2,1)}), bf16[128,3,3584]{2,1,0:T(4,128)(2,1)}, u32[]{:S(2)}, u32[]{:S(2)}) async-start(bf16[128,3,3584]{2,1,0:T(4,128)(2,1)} %get-tuple-element.8), calls=%async_computation | async-start | bytes 7340032 | tf_op jit(solution)/shard_map/all_to_all | solution.py:59
  304.5 54.6 %all-to-all-start.3 = ((bf16[128,3,1792]{2,1,0:T(4,128)(2,1)}), bf16[128,3,1792]{2,1,0:T(4,128)(2,1)S(1)}, u32[]{:S(2)}, u32[]{:S(2)}) async-start(bf16[128,3,1792]{2,1,0:T(4,128)(2,1)} %reshape.96), calls=%async_computation.3 | async-start | bytes 3670016 | tf_op jit(solution)/shard_map/all_to_all | solution.py:76
where the time goes:
time: 366 us; the launch traced here: 365 us
  blocking collectives  124 us (34%)
  waiting for transfers between devices  123 us (34%)
  local copies, waits for them, and re-layouts  49.6 us (14%)
  starting transfers between devices  29.9 us (8%)
  matrix products  26 us (7%)
  other arithmetic  12.7 us (3%)
    all_to_all x1, blocking collectives, per_device(): lax.all_to_all(packed_rows(whole_x), 'expert', split_axis=0, concat_axis=...  100 us
    all_to_all x1, waiting for transfers between devices, per_device(): lax.all_to_all(packed_rows(whole_dy), 'expert', split_axis=0, concat_axis...  75.9 us
    all_to_all x1, waiting for transfers between devices, per_device(): lax.all_to_all(outgoing, 'expert', split_axis=0, concat_axis=0, tiled=True)  47.3 us
    gather x4, local copies, waits for them, and re-layouts, packed_rows(): rows[token_of]  21.2 us
    psum x1, blocking collectives, per_device(): summed = lax.psum(partial_grad, 'tensor')  18.2 us
    all_to_all x1, starting transfers between devices, per_device(): lax.all_to_all(slot_weight, 'expert', split_axis=0, concat_axis=0, tiled=...  15 us
    dot_general x1, matrix products, expert_rows(): lax.dot_general(gate_grad, gate_w, (((1,), (1,)), ((), ())), preferred_el...  8.98 us
    select_n x1, other arithmetic, packed_rows(): jnp.where(filled[:, None], rows[token_of], jnp.zeros((), rows.dtype))  8.13 us
  transfers between devices with their start and end apart: 3, of which 2 were waited for; matrix products, arithmetic and copies ran while one was open for 11% of the time, Pallas kernels for 0%

commit v1 on v0

v1 whole, which is shorter than its diff:
```python
import jax
import jax.numpy as jnp
from jax import lax
from jax.sharding import PartitionSpec as P


def expert_rows(xs, dys, weights, gate_w, up_w, down_w):
    parts, _, width = xs.shape
    ffh = gate_w.shape[1]
    gate_p = gate_w.reshape(parts, width, ffh)
    up_p = up_w.reshape(parts, width, ffh)
    down_p = down_w.reshape(ffh, parts, width)
    gate_pre = jnp.einsum("pnd,pdf->nf", xs, gate_p, preferred_element_type=jnp.float32)
    up_pre = jnp.einsum("pnd,pdf->nf", xs, up_p, preferred_element_type=jnp.float32)
    hidden_grad = jnp.einsum("pnd,fpd->nf", dys, down_p, preferred_element_type=jnp.float32)
    hidden_grad = hidden_grad * weights.astype(jnp.float32)[:, None]
    sigmoid_gate = jax.nn.sigmoid(gate_pre)
    gate_grad = (
        hidden_grad * up_pre * sigmoid_gate * (1.0 + gate_pre * (1.0 - sigmoid_gate))
    ).astype(jnp.bfloat16)
    up_grad = (hidden_grad * gate_pre * sigmoid_gate).astype(jnp.bfloat16)
    first = lax.dot_general(
        gate_grad, gate_w, (((1,), (1,)), ((), ())), preferred_element_type=jnp.float32
    )
    second = lax.dot_general(
        up_grad, up_w, (((1,), (1,)), ((), ())), preferred_element_type=jnp.float32
    )
    return first + second


def per_device(features, cotangent, expert_ids, route_weight, gate_weight, up_weight, down_weight):
    experts = lax.axis_size("expert")
    parts = lax.axis_size("tensor")
    tok_rows, top = expert_ids.shape
    half = features.shape[1]
    routes = tok_rows * top
    capacity = 3 * tok_rows * top // (2 * experts)
    total = experts * capacity
    flat_ids = expert_ids.reshape(routes)
    onehot = (flat_ids[:, None] == jnp.arange(experts, dtype=jnp.int32)[None, :]).astype(jnp.int32)
    ranks = jnp.sum((jnp.cumsum(onehot, axis=0) - 1) * onehot, axis=1)
    destination = flat_ids * capacity + ranks
    route_slot = destination[:, None] == jnp.arange(total, dtype=jnp.int32)[None, :]
    token_slot = jnp.sum(route_slot.reshape(tok_rows, top, total).astype(jnp.int32), axis=1)
    token_slot = token_slot.astype(jnp.bfloat16)
    slot_weight = jnp.sum(
        jnp.where(route_slot, route_weight.reshape(routes).astype(jnp.float32)[:, None], 0.0),
        axis=0,
    ).astype(jnp.bfloat16)

    token_rows = jnp.concatenate([features, cotangent], axis=1)
    packed = lax.dot_general(
        token_slot, token_rows, (((0,), (0,)), ((), ())), preferred_element_type=jnp.float32
    ).astype(jnp.bfloat16)
    lane = jnp.arange(128, dtype=jnp.int32)[None, :]
    weight_block = jnp.where(lane == 0, slot_weight[:, None], jnp.zeros((), jnp.bfloat16))
    outgoing = jnp.concatenate([packed, weight_block], axis=1)
    width = outgoing.shape[1]
    received = lax.all_to_all(
        outgoing.reshape(experts, capacity, width), "expert", split_axis=0, concat_axis=0, tiled=True
    ).reshape(total, width)
    both = lax.all_gather(received, "tensor", axis=0, tiled=False)
    xs = both[:, :, :half]
    dys = both[:, :, half : 2 * half]
    weights = received[:, 2 * half]
    partial_grad = expert_rows(xs, dys, weights, gate_weight[0], up_weight[0], down_weight[0])
    my_share = lax.psum_scatter(partial_grad, "tensor", scatter_dimension=1, tiled=True)
    back = my_share.astype(jnp.bfloat16).reshape(experts, capacity, half)
    returned = lax.all_to_all(back, "expert", split_axis=0, concat_axis=0, tiled=True)
    summed = jnp.dot(token_slot, returned.reshape(total, half), preferred_element_type=jnp.float32)
    return summed.astype(jnp.bfloat16)


def solution(mesh):
    in_specs = (
        P("expert", "tensor"),
        P("expert", "tensor"),
        P("expert", None),
        P("expert", None),
        P("expert", None, "tensor"),
        P("expert", None, "tensor"),
        P("expert", "tensor", None),
    )
    out_specs = P("expert", "tensor")
    return jax.shard_map(
        per_device, mesh=mesh, in_specs=in_specs, out_specs=out_specs, check_vma=False
    )
```

time: 366 us -> 264 us (0.72)
  waiting for transfers between devices: 123 us -> 21.5 us
  blocking collectives: 124 us -> 165 us
  starting transfers between devices: 29.9 us -> 0.22 us
  local copies, waits for them, and re-layouts: 49.6 us -> 32.6 us
  between operations: 0.21 us -> 13.5 us
  other arithmetic: 12.7 us -> 3.8 us
    all_to_all x3 -> x0, waiting for transfers between devices: 123 us -> none  [the longest x1 75.9 us: per_device(): lax.all_to_all(packed_rows(whole_dy), 'expert', split_axis=0, concat_axis...]
    all_to_all x1 -> x2, blocking collectives: 100 us -> 165 us  [the longest x1 104 us: per_device(): lax.all_to_all(outgoing.reshape(experts, capacity, width), 'expert', spli...]
    all_to_all x3 -> x0, starting transfers between devices: 29.9 us -> none  [the longest x1 15 us: per_device(): lax.all_to_all(slot_weight, 'expert', split_axis=0, concat_axis=0, tiled=...]
    gather x7 -> x0, local copies, waits for them, and re-layouts: 25.6 us -> none  [the longest x4 21.2 us: packed_rows(): rows[token_of]]
    reduce_scatter x0 -> x1, waiting for transfers between devices: none -> 20.1 us  [per_device(): lax.psum_scatter(partial_grad, 'tensor', scatter_dimension=1, tiled=True)]
    psum x1 -> x0, blocking collectives: 18.2 us -> none  [per_device(): summed = lax.psum(partial_grad, 'tensor')]
    another operation x2 -> x4, local copies, waits for them, and re-layouts: 0.01 us -> 15.7 us  [the longest x1 8.46 us: expert_rows(): down_p = down_w.reshape(ffh, parts, width)]
    select_n x3 -> x1, other arithmetic: 8.14 us -> 0.12 us  [per_device(): jnp.where(lane == 0, slot_weight[:, None], jnp.zeros((), jnp.bfloat16))]
  transfers between devices with their start and end apart: 3 -> 2, of which waited for: 2 -> 2; matrix products, arithmetic and copies ran while one was open for 11% -> 6% of each run, Pallas kernels for 0% -> 0%
where the time goes in v1:
time: 264 us; the launch traced here: 263 us
  blocking collectives  165 us (62%)
  local copies, waits for them, and re-layouts  32.6 us (12%)
  matrix products  26.8 us (10%)
  waiting for transfers between devices  21.5 us (8%)
  between operations  13.5 us (5%)
  other arithmetic  3.8 us (1%)
    all_to_all x1, blocking collectives, per_device(): lax.all_to_all(outgoing.reshape(experts, capacity, width), 'expert', spli...  104 us
    all_to_all x1, blocking collectives, per_device(): lax.all_to_all(back, 'expert', split_axis=0, concat_axis=0, tiled=True)  60.7 us
    reduce_scatter x1, waiting for transfers between devices, per_device(): lax.psum_scatter(partial_grad, 'tensor', scatter_dimension=1, tiled=True)  20.1 us
    dot_general x1, matrix products, expert_rows(): lax.dot_general(gate_grad, gate_w, (((1,), (1,)), ((), ())), preferred_el...  9.63 us
    another operation x1, local copies, waits for them, and re-layouts, expert_rows(): down_p = down_w.reshape(ffh, parts, width)  8.46 us
    dot_general x1, matrix products, expert_rows(): lax.dot_general(up_grad, up_w, (((1,), (1,)), ((), ())), preferred_elemen...  7.78 us
    another operation x1, local copies, waits for them, and re-layouts, per_device(): both = lax.all_gather(received, 'tensor', axis=0, tiled=False)  7.2 us
    reshape x1, local copies, waits for them, and re-layouts, per_device(): received = lax.all_to_all(outgoing.reshape(experts, capacity, width), 'ex...  6.03 us
  transfers between devices with their start and end apart: 2, of which 2 were waited for; matrix products, arithmetic and copies ran while one was open for 6% of the time, Pallas kernels for 0%

profile of v1, /device:TPU:32, one launch (start us, length us, event | category | flops | bytes accessed | tf_op | source)
XLA Modules:
  0.0 263.2 jit_solution(18330837398755425765)
XLA Ops:
  6.5 0.8 copy.35
  7.7 0.2 fusion.48
  8.5 0.7 multiply_add_fusion.1
  9.2 0.8 copy.40
  10.5 2.1 convolution_convert_fusion
  12.5 0.2 pad_maximum_fusion
  12.7 4.0 %reshape.67 = bf16[128,3,3712]{2,1,0:T(4,128)(2,1)} reshape(bf16[384,3712]{1,0:T(8,128)(2,1)S(1)} %pad_maximum_fusion) | data formatting | bytes 5701632 | tf_op jit(solution)/shard_map/reshape | solution.py:60
  16.7 103.9 %all_to_all.10 = bf16[128,3,3712]{2,1,0:T(4,128)(2,1)} all-to-all(bf16[128,3,3712]{2,1,0:T(4,128)(2,1)} %reshape.67), channel_id=1, replica_groups=mesh['expert'=128,'tensor'=2] {'expert'}, dimensions={0} | all-to-all | bytes 5701632 | tf_op jit(solution)/shard_map/all_to_all | solution.py:59
  120.7 7.2 %all_gather_reshape.3 = bf16[1,384,3712]{2,1,0:T(8,128)(2,1)} reshape(bf16[128,3,3712]{2,1,0:T(4,128)(2,1)} %all_to_all.10) | data formatting | bytes 5701632 | tf_op jit(solution)/shard_map/all_gather;reshape | solution.py:62
  127.9 0.2 reduce-scatter.2.cloned.1.call-start
  128.1 8.5 %reshape_squeeze.9 = bf16[512,2,1792]{2,1,0:T(2,128)(2,1)} reshape(bf16[1,512,3584]{2,1,0:T(8,128)(2,1)} %param.13) | data formatting | bytes 7340032 | tf_op jit(solution)/shard_map/reshape;squeeze | solution.py:12
  136.6 6.0 %reshape.68 = bf16[384,3712]{1,0:T(8,128)(2,1)S(1)} reshape(bf16[128,3,3712]{2,1,0:T(4,128)(2,1)} %all_to_all.10) | data formatting | bytes 5701632 | tf_op jit(solution)/shard_map/reshape | solution.py:61
  142.7 1.4 all-gather.2.cloned.1.call-done
  144.2 4.6 %fusion.13 = f32[384,512]{1,0:T(8,128)S(1)} fusion(bf16[2,1792,512]{2,1,0:T(8,128)(2,1)} %bitcast.38, bf16[2,384,3712]{2,1,0:T(8,128)(2,1)} %all-gather.2.cloned.1.call-done), kind=kOutput, calls=%fused_computation.15 | convolution fusion | flops 1409286144 | bytes 7208960 | tf_op jit(solution)/shard_map/pnd,pdf->nf/dot_general | solution.py:13
  148.8 1.0 copy-done.1
  149.8 1.6 fusion.30
  151.4 9.6 %fusion.1 = f32[384,3584]{1,0:T(8,128)} fusion(bf16[1,3584,512]{2,1,0:T(8,128)(2,1)} %param.11, f32[384,512]{1,0:T(8,128)S(1)} %fusion.30, bf16[2,1792,512]{2,1,0:T(8,128)(2,1)} %bitcast.37, bf16[2,384,3712]{2,1,0:T(8,128)(2,1)} %all-gather.2.cloned.1.call-done, f32[384,512]{1,0:T(8,128)S(1)} %fusion.13), kind=kOutput, calls=%fused_computation.3 | convolution fusion | flops 2820538368 | bytes 17170432 | tf_op jit(solution)/shard_map/dot_general | solution.py:22
  161.0 7.8 %convolution_add_fusion = f32[384,3584]{1,0:T(8,128)} fusion(f32[384,3584]{1,0:T(8,128)} %fusion.1, bf16[1,3584,512]{2,1,0:T(8,128)(2,1)} %param.12, f32[384,512]{1,0:T(8,128)S(1)} %fusion.30, f32[384,512]{1,0:T(8,128)S(1)} %fusion.13), kind=kOutput, calls=%fused_computation | convolution fusion | flops 1411842048 | bytes 16252928 | tf_op jit(solution)/shard_map/dot_general | solution.py:25
  168.8 20.1 %reduce-scatter.2.cloned.1.call-done = f32[384,1792]{1,0:T(8,128)} async-done(((f32[384,3584]{1,0:T(8,128)}), f32[384,1792]{1,0:T(8,128)}) %reduce-scatter.2.cloned.1.call-update) | async-done | bytes 2752528 | tf_op jit(solution)/shard_map/reduce_scatter | solution.py:67
  188.9 1.9 convert_element_type.54
  190.8 0.7 reshape.69
  191.5 60.7 %all_to_all.11 = bf16[128,3,1792]{2,1,0:T(4,128)(2,1)} all-to-all(bf16[128,3,1792]{2,1,0:T(4,128)(2,1)S(1)} %reshape.69), channel_id=1, replica_groups=mesh['expert'=128,'tensor'=2] {'expert'}, dimensions={0} | all-to-all | bytes 2752512 | tf_op jit(solution)/shard_map/all_to_all | solution.py:69
  252.2 3.0 %reshape.70 = bf16[384,1792]{1,0:T(8,128)(2,1)S(1)} reshape(bf16[128,3,1792]{2,1,0:T(4,128)(2,1)} %all_to_all.11) | data formatting | bytes 2752512 | tf_op jit(solution)/shard_map/reshape | solution.py:70
  255.2 1.2 convolution_convert_fusion.1
  (24 shorter events, 1.6 us)
Async XLA Ops:
  6.5 137.6 %all-gather.2.cloned.1.call-start = ((), (), s32[]{:S(2)}) async-start(), calls=%async_computation.3 | async-start | bytes 8552448 | tf_op jit(solution)/shard_map/all_gather | solution.py:62
  127.9 61.0 %reduce-scatter.2.cloned.1.call-start = ((), (), s32[]{:S(2)}) async-start(), calls=%async_computation.4 | async-start | bytes 8257536 | tf_op jit(solution)/shard_map/reduce_scatter | solution.py:67
  144.2 4.6 %copy-start = (bf16[512,2,1792]{2,1,0:T(2,128)(2,1)S(1)}, bf16[512,2,1792]{2,1,0:T(2,128)(2,1)}, u32[]{:S(2)}) copy-start(bf16[512,2,1792]{2,1,0:T(2,128)(2,1)} %reshape_squeeze.9) | copy-start | bytes 11010052
  144.2 5.6 %copy-start.1 = (bf16[2,384,3712]{2,1,0:T(8,128)(2,1)S(1)}, bf16[2,384,3712]{2,1,0:T(8,128)(2,1)}, u32[]{:S(2)}) copy-start(bf16[2,384,3712]{2,1,0:T(8,128)(2,1)} %all-gather.2.cloned.1.call-done) | copy-start | bytes 17104900
Sparse Core Ops, SparseCore 0:
  128.0 16.1 all-gather.1
  169.0 19.8 reduce-scatter.1

commit v2 on v1

v2 whole, which is shorter than its diff:
```python
import jax
import jax.numpy as jnp
from jax import lax
from jax.sharding import PartitionSpec as P


def fold_rows(rows, experts, lanes):
    per_expert = rows.size // experts
    return rows.reshape(experts, 4, per_expert // 4)


def per_device(features, cotangent, expert_ids, route_weight, gate_weight, up_weight, down_weight):
    experts = lax.axis_size("expert")
    parts = lax.axis_size("tensor")
    me = lax.axis_index("tensor")
    swap = [(i, (i + 1) % parts) for i in range(parts)]
    tok_rows, top = expert_ids.shape
    half = features.shape[1]
    routes = tok_rows * top
    capacity = 3 * tok_rows * top // (2 * experts)
    total = experts * capacity
    gate_w = gate_weight[0]
    up_w = up_weight[0]
    down_w = down_weight[0]
    ffh = gate_w.shape[1]

    other_rows = (me + 1) % parts * half
    sent_w = jnp.stack(
        [
            lax.dynamic_slice_in_dim(gate_w, other_rows, half, axis=0),
            lax.dynamic_slice_in_dim(up_w, other_rows, half, axis=0),
        ]
    )
    got_w = lax.ppermute(sent_w, "tensor", swap)
    own_gate = lax.dynamic_slice_in_dim(gate_w, me * half, half, axis=0)
    own_up = lax.dynamic_slice_in_dim(up_w, me * half, half, axis=0)

    flat_ids = expert_ids.reshape(routes)
    onehot = (flat_ids[:, None] == jnp.arange(experts, dtype=jnp.int32)[None, :]).astype(jnp.int32)
    ranks = jnp.sum((jnp.cumsum(onehot, axis=0) - 1) * onehot, axis=1)
    destination = flat_ids * capacity + ranks
    route_slot = destination[:, None] == jnp.arange(total, dtype=jnp.int32)[None, :]
    token_slot = jnp.sum(route_slot.reshape(tok_rows, top, total).astype(jnp.int32), axis=1)
    token_slot = token_slot.astype(jnp.bfloat16)
    slot_weight = jnp.sum(
        jnp.where(route_slot, route_weight.reshape(routes).astype(jnp.float32)[:, None], 0.0),
        axis=0,
    ).astype(jnp.bfloat16)

    token_rows = jnp.concatenate([features, cotangent], axis=1)
    packed = lax.dot_general(
        token_slot, token_rows, (((0,), (0,)), ((), ())), preferred_element_type=jnp.float32
    ).astype(jnp.bfloat16)
    row_part = fold_rows(packed, experts, 128)
    weight4 = jnp.pad(slot_weight.reshape(experts, capacity), ((0, 0), (0, 4 - capacity)))
    lane = jnp.arange(128, dtype=jnp.int32)[None, None, :]
    weight_part = jnp.where(lane == 0, weight4[:, :, None], jnp.zeros((), jnp.bfloat16))
    outgoing = jnp.concatenate([row_part, weight_part], axis=2)
    fold = row_part.shape[2]
    received = lax.all_to_all(outgoing, "expert", split_axis=0, concat_axis=0, tiled=True)
    weights = received[:, :capacity, fold].reshape(total)
    both = lax.all_gather(received, "tensor", axis=0, tiled=False)
    rows = both[:, :, :, :fold].reshape(parts, total, 2 * half)
    xs = rows[:, :, :half]
    dys = rows[:, :, half:]

    gate_pre = jnp.einsum(
        "pnd,pdf->nf", xs, gate_w.reshape(parts, half, ffh), preferred_element_type=jnp.float32
    )
    up_pre = jnp.einsum(
        "pnd,pdf->nf", xs, up_w.reshape(parts, half, ffh), preferred_element_type=jnp.float32
    )
    hidden_grad = None
    for p in range(parts):
        term = lax.dot_general(
            dys[p],
            lax.slice_in_dim(down_w, p * half, (p + 1) * half, axis=1),
            (((1,), (1,)), ((), ())),
            preferred_element_type=jnp.float32,
        )
        hidden_grad = term if hidden_grad is None else hidden_grad + term
    hidden_grad = hidden_grad * weights.astype(jnp.float32)[:, None]
    sigmoid_gate = jax.nn.sigmoid(gate_pre)
    gate_grad = (
        hidden_grad * up_pre * sigmoid_gate * (1.0 + gate_pre * (1.0 - sigmoid_gate))
    ).astype(jnp.bfloat16)
    up_grad = (hidden_grad * gate_pre * sigmoid_gate).astype(jnp.bfloat16)
    got_grad = lax.ppermute(jnp.concatenate([gate_grad, up_grad], axis=1), "tensor", swap)

    def back(grad, weight):
        return lax.dot_general(
            grad, weight, (((1,), (1,)), ((), ())), preferred_element_type=jnp.float32
        )

    share = (
        back(gate_grad, own_gate)
        + back(up_grad, own_up)
        + back(got_grad[:, :ffh], got_w[0])
        + back(got_grad[:, ffh:], got_w[1])
    )
    outgoing_back = fold_rows(share.astype(jnp.bfloat16), experts, 128)
    returned = lax.all_to_all(outgoing_back, "expert", split_axis=0, concat_axis=0, tiled=True)
    summed = jnp.dot(
        token_slot, returned.reshape(total, half), preferred_element_type=jnp.float32
    )
    return summed.astype(jnp.bfloat16)


def solution(mesh):
    in_specs = (
        P("expert", "tensor"),
        P("expert", "tensor"),
        P("expert", None),
        P("expert", None),
        P("expert", None, "tensor"),
        P("expert", None, "tensor"),
        P("expert", "tensor", None),
    )
    out_specs = P("expert", "tensor")
    return jax.shard_map(
        per_device, mesh=mesh, in_specs=in_specs, out_specs=out_specs, check_vma=False
    )
```

time: 264 us -> 221 us (0.84)
  blocking collectives: 165 us -> 137 us
  waiting for transfers between devices: 21.5 us -> 10 us
  matrix products: 26.8 us -> 21.1 us
  other arithmetic: 3.8 us -> 8.09 us
    all_to_all x2, blocking collectives: 165 us -> 137 us  [the longest x1 84.3 us: per_device(): lax.all_to_all(outgoing, 'expert', split_axis=0, concat_axis=0, tiled=True)]
    reduce_scatter x1 -> x0, waiting for transfers between devices: 20.1 us -> none  [per_device(): lax.psum_scatter(partial_grad, 'tensor', scatter_dimension=1, tiled=True)]
    another operation x4 -> x2, local copies, waits for them, and re-layouts: 15.7 us -> 0.01 us  [the longest x1 8.46 us: expert_rows(): down_p = down_w.reshape(ffh, parts, width)]
    all_gather x1, waiting for transfers between devices: 1.43 us -> 10 us  [per_device(): both = lax.all_gather(received, 'tensor', axis=0, tiled=False)]
    slice x0 -> x1, local copies, waits for them, and re-layouts: none -> 6.89 us  [per_device(): rows = both[:, :, :, :fold].reshape(parts, total, 2 * half)]
    dot_general x4 -> x8, matrix products: 23.6 us -> 17.9 us  [the longest x4 8.41 us: back(): lax.dot_general(grad, weight, (((1,), (1,)), ((), ())), preferred_element...]
    concatenate x1 -> x2, other arithmetic: 0.2 us -> 3.19 us  [the longest x1 3.09 us: per_device(): outgoing = jnp.concatenate([row_part, weight_part], axis=2)]
    reshape x3, local copies, waits for them, and re-layouts: 10.7 us -> 13.7 us  [the longest x1 8.48 us: per_device(): rows = both[:, :, :, :fold].reshape(parts, total, 2 * half)]
  transfers between devices with their start and end apart: 2 -> 3, of which waited for: 2 -> 1; matrix products, arithmetic and copies ran while one was open for 6% -> 15% of each run, Pallas kernels for 0% -> 0%
where the time goes in v2:
time: 221 us
  blocking collectives  137 us (62%)
  local copies, waits for them, and re-layouts  30.7 us (14%)
  matrix products  21.1 us (10%)
  between operations  13.6 us (6%)
  waiting for transfers between devices  10 us (5%)
  other arithmetic  8.09 us (4%)
    all_to_all x1, blocking collectives, per_device(): lax.all_to_all(outgoing, 'expert', split_axis=0, concat_axis=0, tiled=True)  84.3 us
    all_to_all x1, blocking collectives, per_device(): lax.all_to_all(outgoing_back, 'expert', split_axis=0, concat_axis=0, tile...  52.4 us
    all_gather x1, waiting for transfers between devices, per_device(): both = lax.all_gather(received, 'tensor', axis=0, tiled=False)  10 us
    reshape x1, local copies, waits for them, and re-layouts, per_device(): rows = both[:, :, :, :fold].reshape(parts, total, 2 * half)  8.48 us
    dot_general x4, matrix products, back(): lax.dot_general(grad, weight, (((1,), (1,)), ((), ())), preferred_element...  8.41 us
    slice x1, local copies, waits for them, and re-layouts, per_device(): rows = both[:, :, :, :fold].reshape(parts, total, 2 * half)  6.89 us
    reshape x2, local copies, waits for them, and re-layouts, fold_rows(): return rows.reshape(experts, 4, per_expert // 4)  5.19 us
  transfers between devices with their start and end apart: 3, of which 1 were waited for; matrix products, arithmetic and copies ran while one was open for 15% of the time, Pallas kernels for 0%

profile of v2, /device:TPU:32, one launch (start us, length us, event | category | flops | bytes accessed | tf_op | source)
XLA Modules:
  0.0 220.5 jit_solution(5076561510272648710)
XLA Ops:
  10.6 2.1 convolution_convert_fusion
  12.7 2.9 %reshape.81 = bf16[128,4,2688]{2,1,0:T(4,128)(2,1)} reshape(bf16[384,3584]{1,0:T(8,128)(2,1)S(1)} %convolution_convert_fusion) | data formatting | bytes 5505024 | tf_op jit(solution)/shard_map/reshape | solution.py:9
  15.8 3.1 %pad_maximum_fusion.1 = bf16[128,4,2816]{2,1,0:T(4,128)(2,1)S(1)} fusion(bf16[128,4,128]{2,1,0:T(4,128)(2,1)S(1)} %broadcast_select_fusion, bf16[128,4,2688]{2,1,0:T(4,128)(2,1)} %reshape.81), kind=kLoop, calls=%fused_computation.5 | loop fusion | flops 5767168 | bytes 5767168 | tf_op jit(solution)/shard_map/concatenate | solution.py:58
  18.9 84.3 %all_to_all.10 = bf16[128,4,2816]{2,1,0:T(4,128)(2,1)} all-to-all(bf16[128,4,2816]{2,1,0:T(4,128)(2,1)S(1)} %pad_maximum_fusion.1), channel_id=1, replica_groups=mesh['expert'=128,'tensor'=2] {'expert'}, dimensions={0} | all-to-all | bytes 5767168 | tf_op jit(solution)/shard_map/all_to_all | solution.py:60
  103.2 1.8 constant_dynamic-slice_fusion
  105.9 2.1 pad_maximum_fusion
  108.1 1.1 convert_reduce_fusion.1
  109.4 10.0 %all-gather.3.cloned.1.call-done = bf16[256,4,2816]{2,1,0:T(4,128)(2,1)} async-done(((bf16[128,4,2816]{2,1,0:T(4,128)(2,1)}), bf16[256,4,2816]{2,1,0:T(4,128)(2,1)}) %all-gather.3.cloned.1.call-update) | async-done | bytes 5767184 | tf_op jit(solution)/shard_map/all_gather | solution.py:62
  119.4 6.9 %slice.56 = bf16[2,128,4,2688]{3,2,1,0:T(4,128)(2,1)} slice(bf16[2,128,4,2816]{3,2,1,0:T(4,128)(2,1)} %bitcast.53), slice={[0:2], [0:128], [0:4], [0:2688]} | slice | bytes 11010048 | tf_op jit(solution)/shard_map/slice | solution.py:63
  126.3 8.5 %reshape.82 = bf16[2,384,3584]{2,1,0:T(8,128)(2,1)} reshape(bf16[2,128,4,2688]{3,2,1,0:T(4,128)(2,1)} %slice.56) | data formatting | bytes 11010048 | tf_op jit(solution)/shard_map/reshape | solution.py:63
  134.8 3.0 %fusion.7 = f32[384,512]{1,0:T(8,128)S(1)} fusion(bf16[512,3584]{1,0:T(8,128)(2,1)} %bitcast.56, bf16[2,384,3584]{2,1,0:T(8,128)(2,1)} %reshape.82), kind=kOutput, calls=%fused_computation.15 | convolution fusion | flops 704643072 | bytes 3997696 | tf_op jit(solution)/shard_map/dot_general | solution.py:75
  138.3 3.8 %fusion.19 = f32[384,512]{1,0:T(8,128)S(1)} fusion(bf16[2,1792,512]{2,1,0:T(8,128)(2,1)} %bitcast.54, bf16[2,384,3584]{2,1,0:T(8,128)(2,1)S(1)} %copy-done), kind=kOutput, calls=%fused_computation.27 | convolution fusion | flops 1409286144 | bytes 7208960 | tf_op jit(solution)/shard_map/pnd,pdf->nf/dot_general | solution.py:67
  142.1 1.0 multiply_convert_fusion
  143.1 1.0 copy-done.2
  144.1 1.7 fusion.37
  146.3 2.5 %fusion.12 = f32[384,1792]{1,0:T(8,128)S(1)} fusion(bf16[384,512]{1,0:T(8,128)(2,1)S(1)} %fusion.37, bf16[1,3584,512]{2,1,0:T(8,128)(2,1)} %param.11, s32[]{:T(128)S(6)} %select_n.25), kind=kOutput, calls=%fused_computation.20 | convolution fusion | flops 704643072 | bytes 4980740 | tf_op jit(solution)/shard_map/dot_general | solution.py:91
  148.9 0.9 convolution_add_fusion.1
  149.9 0.9 copy-done.4
  150.7 2.4 %fusion.6 = f32[384,1792]{1,0:T(8,128)S(1)} fusion(bf16[2,1792,512]{2,1,0:T(8,128)(2,1)} %collective-permute-done.1, bf16[384,1024]{1,0:T(8,128)(2,1)S(1)} %collective-permute-done), kind=kOutput, calls=%fused_computation.13 | convolution fusion | flops 704643072 | bytes 4980736 | tf_op jit(solution)/shard_map/dot_general | solution.py:91
  153.2 2.6 %fusion.1 = bf16[384,1792]{1,0:T(8,128)(2,1)S(1)} fusion(f32[384,1792]{1,0:T(8,128)S(1)} %fusion.6, f32[384,1792]{1,0:T(8,128)S(1)} %convolution_add_fusion.1, bf16[2,1792,512]{2,1,0:T(8,128)(2,1)} %collective-permute-done.1, bf16[384,1024]{1,0:T(8,128)(2,1)} %copy-done.4), kind=kOutput, calls=%fused_computation.6 | convolution fusion | flops 706707456 | bytes 9109504 | tf_op jit(solution)/shard_map/dot_general | solution.py:91
  155.7 2.3 %reshape.83 = bf16[128,4,1344]{2,1,0:T(4,128)(2,1)S(1)} reshape(bf16[384,1792]{1,0:T(8,128)(2,1)S(1)} %fusion.1) | data formatting | bytes 2752512 | tf_op jit(solution)/shard_map/reshape | solution.py:9
  158.0 52.4 %all_to_all.11 = bf16[128,4,1344]{2,1,0:T(4,128)(2,1)S(1)} all-to-all(bf16[128,4,1344]{2,1,0:T(4,128)(2,1)S(1)} %reshape.83), channel_id=1, replica_groups=mesh['expert'=128,'tensor'=2] {'expert'}, dimensions={0} | all-to-all | bytes 2752512 | tf_op jit(solution)/shard_map/all_to_all | solution.py:102
  210.3 2.2 reshape.84
  212.5 1.2 convolution_convert_fusion.1
  (42 shorter events, 6.4 us)
Async XLA Ops:
  6.5 112.9 %all-gather.3.cloned.1.call-start = ((), (), s32[]{:S(2)}) async-start(), calls=%async_computation.2 | async-start | bytes 8650752 | tf_op jit(solution)/shard_map/all_gather | solution.py:62
  103.2 2.6 %copy-start.1 = (bf16[1,3584,512]{2,1,0:T(8,128)(2,1)S(1)}, bf16[1,3584,512]{2,1,0:T(8,128)(2,1)}, u32[]{:S(2)}) copy-start(bf16[1,3584,512]{2,1,0:T(8,128)(2,1)} %param.12) | copy-start | bytes 11010052
  108.1 41.8 %collective-permute-start.1 = (bf16[2,1792,512]{2,1,0:T(8,128)(2,1)}, bf16[2,1792,512]{2,1,0:T(8,128)(2,1)}, u32[]{:S(2)}, u32[]{:S(2)}) collective-permute-start(bf16[2,1792,512]{2,1,0:T(8,128)(2,1)} %pad_maximum_fusion), channel_id=1, source_target_pairs={{0,1},{1,0},{2,3},{3,2},{4,5},{5,4},{6,7},{7,6},{8,9},{9,8},{10,11... | collective-permute-start | bytes 11010056 | tf_op jit(solution)/shard_map/ppermute | solution.py:34
  134.8 3.5 %copy-start = (bf16[2,384,3584]{2,1,0:T(8,128)(2,1)S(1)}, bf16[2,384,3584]{2,1,0:T(8,128)(2,1)}, u32[]{:S(2)}) copy-start(bf16[2,384,3584]{2,1,0:T(8,128)(2,1)} %reshape.82) | copy-start | bytes 16515076
  138.3 3.8 %copy-start.5 = (bf16[1,512,3584]{2,1,0:T(8,128)(2,1)S(1)}, bf16[1,512,3584]{2,1,0:T(8,128)(2,1)}, u32[]{:S(2)}) copy-start(bf16[1,512,3584]{2,1,0:T(8,128)(2,1)} %param.13) | copy-start | bytes 11010052
  142.1 2.0 copy-start.2
  146.0 3.9 %collective-permute-start = (bf16[384,1024]{1,0:T(8,128)(2,1)S(1)}, bf16[384,1024]{1,0:T(8,128)(2,1)S(1)}, u32[]{:S(2)}, u32[]{:S(2)}) collective-permute-start(bf16[384,1024]{1,0:T(8,128)(2,1)S(1)} %pad_maximum_fusion.2), channel_id=1, source_target_pairs={{0,1},{1,0},{2,3},{3,2},{4,5},{5,4},{6,7},{7,6},{8,9},{9,8},{10,11... | collective-permute-start | bytes 2359304 | tf_op jit(solution)/shard_map/ppermute | solution.py:88
  146.3 2.6 %copy-start.3 = (bf16[1,3584,512]{2,1,0:T(8,128)(2,1)S(1)}, bf16[1,3584,512]{2,1,0:T(8,128)(2,1)}, u32[]{:S(2)}) copy-start(bf16[1,3584,512]{2,1,0:T(8,128)(2,1)} %param.12) | copy-start | bytes 11010052
  149.9 0.9 copy-start.4
Sparse Core Ops, SparseCore 0:
  103.3 16.0 all-gather.2

commit v3 on v2

--- a/solution.py
+++ b/solution.py
@@ -59,26 +59,23 @@
     fold = row_part.shape[2]
     received = lax.all_to_all(outgoing, "expert", split_axis=0, concat_axis=0, tiled=True)
     weights = received[:, :capacity, fold].reshape(total)
-    both = lax.all_gather(received, "tensor", axis=0, tiled=False)
-    rows = both[:, :, :, :fold].reshape(parts, total, 2 * half)
-    xs = rows[:, :, :half]
-    dys = rows[:, :, half:]
+    own_rows = received[:, :, :fold].reshape(total, 2 * half)
+    got_rows = lax.ppermute(own_rows, "tensor", swap)
+    other_cols = (me + 1) % parts * half
+    own_down = lax.dynamic_slice_in_dim(down_w, me * half, half, axis=1)
+    other_down = lax.dynamic_slice_in_dim(down_w, other_cols, half, axis=1)
 
-    gate_pre = jnp.einsum(
-        "pnd,pdf->nf", xs, gate_w.reshape(parts, half, ffh), preferred_element_type=jnp.float32
-    )
-    up_pre = jnp.einsum(
-        "pnd,pdf->nf", xs, up_w.reshape(parts, half, ffh), preferred_element_type=jnp.float32
-    )
-    hidden_grad = None
-    for p in range(parts):
-        term = lax.dot_general(
-            dys[p],
-            lax.slice_in_dim(down_w, p * half, (p + 1) * half, axis=1),
-            (((1,), (1,)), ((), ())),
-            preferred_element_type=jnp.float32,
+    def fwd(rows, weight):
+        return jnp.dot(rows, weight, preferred_element_type=jnp.float32)
+
+    def fwd_t(rows, weight):
+        return lax.dot_general(
+            rows, weight, (((1,), (1,)), ((), ())), preferred_element_type=jnp.float32
         )
-        hidden_grad = term if hidden_grad is None else hidden_grad + term
+
+    gate_pre = fwd(own_rows[:, :half], own_gate) + fwd(got_rows[:, :half], sent_w[0])
+    up_pre = fwd(own_rows[:, :half], own_up) + fwd(got_rows[:, :half], sent_w[1])
+    hidden_grad = fwd_t(own_rows[:, half:], own_down) + fwd_t(got_rows[:, half:], other_down)
     hidden_grad = hidden_grad * weights.astype(jnp.float32)[:, None]
     sigmoid_gate = jax.nn.sigmoid(gate_pre)
     gate_grad = (

time: 221 us -> 185 us (0.84)
  between operations: 13.6 us -> 0.3 us
  local copies, waits for them, and re-layouts: 30.7 us -> 20.7 us
  waiting for transfers between devices: 10 us -> 0.39 us
  blocking collectives: 137 us -> 130 us
  matrix products: 21.1 us -> 25.1 us
    all_gather x1 -> x0, waiting for transfers between devices: 10 us -> none  [per_device(): both = lax.all_gather(received, 'tensor', axis=0, tiled=False)]
    all_to_all x1, blocking collectives: 52.4 us -> 45.7 us  [per_device(): lax.all_to_all(outgoing_back, 'expert', split_axis=0, concat_axis=0, tile...]
    dot_general x4 -> x6, matrix products: 9.46 us -> 15.2 us  [the longest x4 10.2 us: fwd(): return jnp.dot(rows, weight, preferred_element_type=jnp.float32)]
    slice x1, local copies, waits for them, and re-layouts: 6.89 us -> 2.5 us  [per_device(): own_rows = received[:, :, :fold].reshape(total, 2 * half)]
    reshape x1, local copies, waits for them, and re-layouts: 8.48 us -> 4.82 us  [per_device(): own_rows = received[:, :, :fold].reshape(total, 2 * half)]
  transfers between devices with their start and end apart: 3 -> 3, of which waited for: 1 -> 1; matrix products, arithmetic and copies ran while one was open for 15% -> 12% of each run, Pallas kernels for 0% -> 0%
where the time goes in v3:
time: 185 us; the launch traced here: 184 us
  blocking collectives  130 us (70%)
  matrix products  25.1 us (14%)
  local copies, waits for them, and re-layouts  20.7 us (11%)
  other arithmetic  7.46 us (4%)
    all_to_all x1, blocking collectives, per_device(): lax.all_to_all(outgoing, 'expert', split_axis=0, concat_axis=0, tiled=True)  84.2 us
    all_to_all x1, blocking collectives, per_device(): lax.all_to_all(outgoing_back, 'expert', split_axis=0, concat_axis=0, tile...  45.7 us
    dot_general x4, matrix products, fwd(): return jnp.dot(rows, weight, preferred_element_type=jnp.float32)  10.2 us
    dot_general x4, matrix products, back(): lax.dot_general(grad, weight, (((1,), (1,)), ((), ())), preferred_element...  6.68 us
    reshape x2, local copies, waits for them, and re-layouts, fold_rows(): return rows.reshape(experts, 4, per_expert // 4)  5.19 us
    dot_general x2, matrix products, fwd_t(): lax.dot_general(rows, weight, (((1,), (1,)), ((), ())), preferred_element...  5.02 us
    reshape x1, local copies, waits for them, and re-layouts, per_device(): own_rows = received[:, :, :fold].reshape(total, 2 * half)  4.82 us
  transfers between devices with their start and end apart: 3, of which 1 were waited for; matrix products, arithmetic and copies ran while one was open for 12% of the time, Pallas kernels for 0%

profile of v3, /device:TPU:32, one launch (start us, length us, event | category | flops | bytes accessed | tf_op | source)
XLA Modules:
  0.0 184.4 jit_solution(13604582449897069145)
XLA Ops:
  0.0 0.8 copy.44
  4.1 2.1 %convolution_convert_fusion = bf16[384,3584]{1,0:T(8,128)(2,1)S(1)} fusion(bf16[128,1792]{1,0:T(8,128)(2,1)} %param.8, bf16[128,1792]{1,0:T(8,128)(2,1)} %param.7, s32[128,384]{1,0:T(8,128)S(1)} %convert_reduce_fusion), kind=kOutput, calls=%fused_computation | convolution fusion | flops 355581952 | bytes 3866624 | tf_op jit(solution)/shard_map/dot_general | solution.py:51
  6.1 2.9 %reshape.83 = bf16[128,4,2688]{2,1,0:T(4,128)(2,1)} reshape(bf16[384,3584]{1,0:T(8,128)(2,1)S(1)} %convolution_convert_fusion) | data formatting | bytes 5505024 | tf_op jit(solution)/shard_map/reshape | solution.py:9
  9.3 3.1 %pad_maximum_fusion.1 = bf16[128,4,2816]{2,1,0:T(4,128)(2,1)S(1)} fusion(bf16[128,4,128]{2,1,0:T(4,128)(2,1)S(1)} %broadcast_select_fusion, bf16[128,4,2688]{2,1,0:T(4,128)(2,1)} %reshape.83), kind=kLoop, calls=%fused_computation.5 | loop fusion | flops 5767168 | bytes 5767168 | tf_op jit(solution)/shard_map/concatenate | solution.py:58
  12.4 84.2 %all_to_all.10 = bf16[128,4,2816]{2,1,0:T(4,128)(2,1)S(1)} all-to-all(bf16[128,4,2816]{2,1,0:T(4,128)(2,1)S(1)} %pad_maximum_fusion.1), channel_id=1, replica_groups=mesh['expert'=128,'tensor'=2] {'expert'}, dimensions={0} | all-to-all | bytes 5767168 | tf_op jit(solution)/shard_map/all_to_all | solution.py:60
  96.5 2.5 %slice.51 = bf16[128,4,2688]{2,1,0:T(4,128)(2,1)} slice(bf16[128,4,2816]{2,1,0:T(4,128)(2,1)S(1)} %all_to_all.10), slice={[0:128], [0:4], [0:2688]} | slice | bytes 5505024 | tf_op jit(solution)/shard_map/slice | solution.py:62
  99.0 4.8 %reshape.84 = bf16[384,3584]{1,0:T(8,128)(2,1)} reshape(bf16[128,4,2688]{2,1,0:T(4,128)(2,1)} %slice.51) | data formatting | bytes 5505024 | tf_op jit(solution)/shard_map/reshape | solution.py:62
  103.9 1.8 constant_dynamic-slice_fusion
  105.6 0.8 copy-done.5
  106.6 2.4 %pad_maximum_fusion = bf16[2,1792,512]{2,1,0:T(8,128)(2,1)} fusion(bf16[1,1792,512]{2,1,0:T(8,128)(2,1)S(1)} %constant_dynamic-slice_fusion.1, bf16[1,1792,512]{2,1,0:T(8,128)(2,1)S(1)} %constant_dynamic-slice_fusion), kind=kLoop, calls=%fused_computation.1 | loop fusion | flops 1835008 | bytes 7340032 | tf_op jit(solution)/shard_map/stack | solution.py:28
  110.4 2.9 %fusion.7 = f32[384,512]{1,0:T(8,128)S(1)} fusion(bf16[1,3584,512]{2,1,0:T(8,128)(2,1)} %param.11, s32[]{:T(128)S(6)} %select_n.29, bf16[384,3584]{1,0:T(8,128)(2,1)} %reshape.84), kind=kOutput, calls=%fused_computation.15 | convolution fusion | flops 704643072 | bytes 3997700 | tf_op jit(solution)/shard_map/dot_general | solution.py:69
  113.4 2.4 %fusion.12 = f32[384,512]{1,0:T(8,128)S(1)} fusion(bf16[1,3584,512]{2,1,0:T(8,128)(2,1)S(1)} %copy-done.6, s32[]{:T(128)S(6)} %select_n.29, bf16[384,3584]{1,0:T(8,128)(2,1)} %reshape.84), kind=kOutput, calls=%fused_computation.20 | convolution fusion | flops 704643072 | bytes 3997700 | tf_op jit(solution)/shard_map/dot_general | solution.py:69
  115.7 2.5 %fusion.16 = f32[384,512]{1,0:T(8,128)S(1)} fusion(bf16[1,512,3584]{2,1,0:T(8,128)(2,1)} %param.13, s32[]{:T(128)S(6)} %select_n.29, bf16[384,3584]{1,0:T(8,128)(2,1)S(1)} %copy-done.7), kind=kOutput, calls=%fused_computation.24 | convolution fusion | flops 704643072 | bytes 3997700 | tf_op jit(solution)/shard_map/dot_general | solution.py:72
  118.3 2.4 %fusion.43 = f32[384,512]{1,0:T(8,128)S(1)} fusion(f32[384,512]{1,0:T(8,128)S(1)} %fusion.7, bf16[1,1792,512]{2,1,0:T(8,128)(2,1)S(1)} %copy-done.3, bf16[384,3584]{1,0:T(8,128)(2,1)} %collective-permute-done), kind=kOutput, calls=%fused_computation.39 | convolution fusion | flops 704839680 | bytes 4784128 | tf_op jit(solution)/shard_map/dot_general | solution.py:69
  120.7 2.5 %multiply_convert_fusion = (bf16[384,512]{1,0:T(8,128)(2,1)S(1)}, f32[384,512]{1,0:T(8,128)S(1)}) fusion(f32[384,512]{1,0:T(8,128)S(1)} %fusion.43, f32[384]{0:T(512)S(1)} %reshape.88, f32[384,512]{1,0:T(8,128)S(1)} %fusion.16, bf16[1,512,3584]{2,1,0:T(8,128)(2,1)S(1)} %copy-done.8, s32[]{:T(128)S(6)} %select_n.31, bf16[384,3584]{1,0:T(8,128)(2,1)} %collective-permute-done), kind=kOutput, calls=%fused_computation.50 | convolution fusion | flops 706215936 | bytes 5965828 | tf_op jit(solution)/shard_map/dot_general | solution.py:72
  123.3 2.6 %fusion.51 = bf16[384,512]{1,0:T(8,128)(2,1)S(1)} fusion(f32[384,512]{1,0:T(8,128)S(1)} %get-tuple-element.6, f32[384,512]{1,0:T(8,128)S(1)} %fusion.12, bf16[1,1792,512]{2,1,0:T(8,128)(2,1)S(1)} %copy-done.1, bf16[384,3584]{1,0:T(8,128)(2,1)} %collective-permute-done, f32[384,512]{1,0:T(8,128)S(1)} %fusion.43), kind=kOutput, calls=%fused_computation.41 | convolution fusion | flops 706805760 | bytes 5963776 | tf_op jit(solution)/shard_map/dot_general | solution.py:69
  126.0 0.9 fusion.5
  127.0 0.9 convolution_add_fusion.1
  128.3 2.4 %fusion.2 = f32[384,1792]{1,0:T(8,128)S(1)} fusion(bf16[2,1792,512]{2,1,0:T(8,128)(2,1)} %collective-permute-done.2, bf16[384,1024]{1,0:T(8,128)(2,1)S(1)} %collective-permute-done.1), kind=kOutput, calls=%fused_computation.9 | convolution fusion | flops 704643072 | bytes 4980736 | tf_op jit(solution)/shard_map/dot_general | solution.py:88
  130.7 2.4 %fusion.1 = bf16[384,1792]{1,0:T(8,128)(2,1)S(1)} fusion(f32[384,1792]{1,0:T(8,128)S(1)} %fusion.2, f32[384,1792]{1,0:T(8,128)S(1)} %convolution_add_fusion.1, bf16[2,1792,512]{2,1,0:T(8,128)(2,1)} %collective-permute-done.2, bf16[384,1024]{1,0:T(8,128)(2,1)S(1)} %collective-permute-done.1), kind=kOutput, calls=%fused_computation.6 | convolution fusion | flops 706707456 | bytes 9109504 | tf_op jit(solution)/shard_map/dot_general | solution.py:88
  133.1 2.3 %reshape.85 = bf16[128,4,1344]{2,1,0:T(4,128)(2,1)S(1)} reshape(bf16[384,1792]{1,0:T(8,128)(2,1)S(1)} %fusion.1) | data formatting | bytes 2752512 | tf_op jit(solution)/shard_map/reshape | solution.py:9
  135.4 45.7 %all_to_all.11 = bf16[128,4,1344]{2,1,0:T(4,128)(2,1)S(1)} all-to-all(bf16[128,4,1344]{2,1,0:T(4,128)(2,1)S(1)} %reshape.85), channel_id=1, replica_groups=mesh['expert'=128,'tensor'=2] {'expert'}, dimensions={0} | all-to-all | bytes 2752512 | tf_op jit(solution)/shard_map/all_to_all | solution.py:99
  181.0 2.2 %reshape.86 = bf16[384,1792]{1,0:T(8,128)(2,1)S(1)} reshape(bf16[128,4,1344]{2,1,0:T(4,128)(2,1)S(1)} %all_to_all.11) | data formatting | bytes 2752512 | tf_op jit(solution)/shard_map/reshape | solution.py:101
  183.2 1.2 convolution_convert_fusion.1
  (49 shorter events, 5.6 us)
Async XLA Ops:
  103.9 14.4 %collective-permute-start = (bf16[384,3584]{1,0:T(8,128)(2,1)}, bf16[384,3584]{1,0:T(8,128)(2,1)}, u32[]{:S(2)}, u32[]{:S(2)}) collective-permute-start(bf16[384,3584]{1,0:T(8,128)(2,1)} %reshape.84), channel_id=1, source_target_pairs={{0,1},{1,0},{2,3},{3,2},{4,5},{5,4},{6,7},{7,6},{8,9},{9,8},{10,11... | collective-permute-start | bytes 8257544 | tf_op jit(solution)/shard_map/ppermute | solution.py:63
  103.9 2.6 %copy-start.5 = (bf16[1,3584,512]{2,1,0:T(8,128)(2,1)S(1)}, bf16[1,3584,512]{2,1,0:T(8,128)(2,1)}, u32[]{:S(2)}) copy-start(bf16[1,3584,512]{2,1,0:T(8,128)(2,1)} %param.12) | copy-start | bytes 11010052
  106.4 2.5 %copy-start.2 = (bf16[1,1792,512]{2,1,0:T(8,128)(2,1)}, bf16[1,1792,512]{2,1,0:T(8,128)(2,1)S(1)}, u32[]{:S(2)}) copy-start(bf16[1,1792,512]{2,1,0:T(8,128)(2,1)S(1)} %constant_dynamic-slice_fusion) | copy-start | bytes 5505028
  106.6 2.8 %copy-start = (bf16[1,1792,512]{2,1,0:T(8,128)(2,1)}, bf16[1,1792,512]{2,1,0:T(8,128)(2,1)S(1)}, u32[]{:S(2)}) copy-start(bf16[1,1792,512]{2,1,0:T(8,128)(2,1)S(1)} %constant_dynamic-slice_fusion.1) | copy-start | bytes 5505028
  109.4 18.5 %collective-permute-start.2 = (bf16[2,1792,512]{2,1,0:T(8,128)(2,1)}, bf16[2,1792,512]{2,1,0:T(8,128)(2,1)}, u32[]{:S(2)}, u32[]{:S(2)}) collective-permute-start(bf16[2,1792,512]{2,1,0:T(8,128)(2,1)} %pad_maximum_fusion), channel_id=1, source_target_pairs={{0,1},{1,0},{2,3},{3,2},{4,5},{5,4},{6,7},{7,6},{8,9},{9,8},{10,11... | collective-permute-start | bytes 11010056 | tf_op jit(solution)/shard_map/ppermute | solution.py:34
  110.3 3.0 %copy-start.6 = (bf16[1,3584,512]{2,1,0:T(8,128)(2,1)S(1)}, bf16[1,3584,512]{2,1,0:T(8,128)(2,1)}, u32[]{:S(2)}) copy-start(bf16[1,3584,512]{2,1,0:T(8,128)(2,1)} %param.12) | copy-start | bytes 11010052
  113.4 2.4 %copy-start.7 = (bf16[384,3584]{1,0:T(8,128)(2,1)S(1)}, bf16[384,3584]{1,0:T(8,128)(2,1)}, u32[]{:S(2)}) copy-start(bf16[384,3584]{1,0:T(8,128)(2,1)} %reshape.84) | copy-start | bytes 8257540
  115.7 2.6 %copy-start.3 = (bf16[1,1792,512]{2,1,0:T(8,128)(2,1)S(1)}, bf16[1,1792,512]{2,1,0:T(8,128)(2,1)}, u32[]{:S(2)}) copy-start(bf16[1,1792,512]{2,1,0:T(8,128)(2,1)} %copy-done.2) | copy-start | bytes 5505028
  118.3 2.5 %copy-start.8 = (bf16[1,512,3584]{2,1,0:T(8,128)(2,1)S(1)}, bf16[1,512,3584]{2,1,0:T(8,128)(2,1)}, u32[]{:S(2)}) copy-start(bf16[1,512,3584]{2,1,0:T(8,128)(2,1)} %param.13) | copy-start | bytes 11010052
  120.7 2.5 %copy-start.1 = (bf16[1,1792,512]{2,1,0:T(8,128)(2,1)S(1)}, bf16[1,1792,512]{2,1,0:T(8,128)(2,1)}, u32[]{:S(2)}) copy-start(bf16[1,1792,512]{2,1,0:T(8,128)(2,1)} %copy-done) | copy-start | bytes 5505028
  123.2 2.8 %copy-start.4 = (bf16[1,3584,512]{2,1,0:T(8,128)(2,1)S(1)}, bf16[1,3584,512]{2,1,0:T(8,128)(2,1)}, u32[]{:S(2)}) copy-start(bf16[1,3584,512]{2,1,0:T(8,128)(2,1)} %param.11) | copy-start | bytes 11010052
  125.9 2.4 %collective-permute-start.1 = (bf16[384,1024]{1,0:T(8,128)(2,1)S(1)}, bf16[384,1024]{1,0:T(8,128)(2,1)S(1)}, u32[]{:S(2)}, u32[]{:S(2)}) collective-permute-start(bf16[384,1024]{1,0:T(8,128)(2,1)S(1)} %pad_maximum_fusion.2), channel_id=1, source_target_pairs={{0,1},{1,0},{2,3},{3,2},{4,5},{5,4},{6,7},{7,6},{8,9},{9,8},{10,11... | collective-permute-start | bytes 2359304 | tf_op jit(solution)/shard_map/ppermute | solution.py:85

commit v4 on v3

v4 whole, which is shorter than its diff:
```python
import jax
import jax.numpy as jnp
from jax import lax
from jax.sharding import PartitionSpec as P


def fold_rows(rows, experts):
    per_expert = rows.size // experts
    return rows.reshape(experts, 4, per_expert // 4)


def slot_ranks(ids, experts):
    onehot = (ids[:, None] == jnp.arange(experts, dtype=jnp.int32)[None, :]).astype(jnp.int32)
    return jnp.sum((jnp.cumsum(onehot, axis=0) - 1) * onehot, axis=1)


def device_body(features, cotangent, expert_ids, route_weight, gate_weight, up_weight, down_weight):
    experts = lax.axis_size("expert")
    parts = lax.axis_size("tensor")
    me = lax.axis_index("tensor")
    my_expert = lax.axis_index("expert")
    swap = [(i, (i + 1) % parts) for i in range(parts)]
    tok_rows, top = expert_ids.shape
    half = features.shape[1]
    routes = tok_rows * top
    capacity = 3 * tok_rows * top // (2 * experts)
    total = experts * capacity
    gate_w = gate_weight[0]
    up_w = up_weight[0]
    down_w = down_weight[0]

    coded = expert_ids * 4096 + (route_weight.astype(jnp.float32) * 2048.0).astype(jnp.int32)
    all_coded = lax.all_gather(coded, "expert", axis=0, tiled=True)
    all_coded = all_coded.reshape(experts, routes)
    all_ids = all_coded // 4096
    all_weights = (all_coded % 4096).astype(jnp.float32) * (1.0 / 2048.0)

    other_rows = (me + 1) % parts * half

    def rows_of(start):
        return jnp.concatenate(
            [
                lax.dynamic_slice_in_dim(gate_w, start, half, axis=0),
                lax.dynamic_slice_in_dim(up_w, start, half, axis=0),
            ],
            axis=1,
        )

    sent_gu = rows_of(other_rows)
    got_gu = lax.ppermute(sent_gu, "tensor", swap)
    own_gu = rows_of(me * half)

    flat_ids = expert_ids.reshape(routes)
    destination = flat_ids * capacity + slot_ranks(flat_ids, experts)
    route_slot = destination[:, None] == jnp.arange(total, dtype=jnp.int32)[None, :]
    token_slot = jnp.sum(route_slot.reshape(tok_rows, top, total).astype(jnp.int32), axis=1)
    token_slot = token_slot.astype(jnp.bfloat16)

    token_rows = jnp.concatenate([features, cotangent], axis=1)
    packed = lax.dot_general(
        token_slot, token_rows, (((0,), (0,)), ((), ())), preferred_element_type=jnp.float32
    ).astype(jnp.bfloat16)
    received = lax.all_to_all(
        fold_rows(packed, experts), "expert", split_axis=0, concat_axis=0, tiled=True
    )
    own_rows = received.reshape(total, 2 * half)
    got_rows = lax.ppermute(own_rows, "tensor", swap)

    mine = all_ids == my_expert
    rank = jnp.cumsum(mine.astype(jnp.int32), axis=1) - 1
    slot_of = jnp.where(mine, rank, capacity)
    weights = jnp.stack(
        [
            jnp.sum(jnp.where(slot_of == c, all_weights, 0.0), axis=1)
            for c in range(capacity)
        ],
        axis=1,
    ).reshape(total)

    other_cols = (me + 1) % parts * half
    own_down = lax.dynamic_slice_in_dim(down_w, me * half, half, axis=1)
    other_down = lax.dynamic_slice_in_dim(down_w, other_cols, half, axis=1)

    def fwd(rows, weight):
        return jnp.dot(rows, weight, preferred_element_type=jnp.float32)

    def fwd_t(rows, weight):
        return lax.dot_general(
            rows, weight, (((1,), (1,)), ((), ())), preferred_element_type=jnp.float32
        )

    ffh = gate_w.shape[1]
    gate_up = fwd(own_rows[:, :half], own_gu) + fwd(got_rows[:, :half], sent_gu)
    gate_pre = gate_up[:, :ffh]
    up_pre = gate_up[:, ffh:]
    hidden_grad = fwd_t(own_rows[:, half:], own_down) + fwd_t(got_rows[:, half:], other_down)
    hidden_grad = hidden_grad * weights[:, None]
    sigmoid_gate = jax.nn.sigmoid(gate_pre)
    gate_grad = (
        hidden_grad * up_pre * sigmoid_gate * (1.0 + gate_pre * (1.0 - sigmoid_gate))
    ).astype(jnp.bfloat16)
    up_grad = (hidden_grad * gate_pre * sigmoid_gate).astype(jnp.bfloat16)
    grads = jnp.concatenate([gate_grad, up_grad], axis=1)
    got_grads = lax.ppermute(grads, "tensor", swap)
    share = fwd_t(grads, own_gu) + fwd_t(got_grads, got_gu)
    returned = lax.all_to_all(
        fold_rows(share.astype(jnp.bfloat16), experts), "expert", split_axis=0, concat_axis=0, tiled=True
    )
    summed = jnp.dot(
        token_slot, returned.reshape(total, half), preferred_element_type=jnp.float32
    )
    return summed.astype(jnp.bfloat16)


def solution(mesh):
    in_specs = (
        P("expert", "tensor"),
        P("expert", "tensor"),
        P("expert", None),
        P("expert", None),
        P("expert", None, "tensor"),
        P("expert", None, "tensor"),
        P("expert", "tensor", None),
    )
    out_specs = P("expert", "tensor")
    return jax.shard_map(
        device_body, mesh=mesh, in_specs=in_specs, out_specs=out_specs, check_vma=False
    )
```

time: 185 us -> 539 us (2.91)
  blocking collectives: 130 us -> 384 us
  waiting for transfers between devices: 0.39 us -> 67.1 us
  local copies, waits for them, and re-layouts: 20.7 us -> 45.3 us
  starting transfers between devices: 0.6 us -> 15.8 us
    all_gather x0 -> x1, blocking collectives: none -> 330 us  [device_body(): all_coded = lax.all_gather(coded, 'expert', axis=0, tiled=True)]
    all_to_all x2 -> x1, blocking collectives: 130 us -> 54.6 us  [device_body(): lax.all_to_all(fold_rows(share.astype(jnp.bfloat16), experts), 'expert',...]
    all_to_all x0 -> x1, waiting for transfers between devices: none -> 66.5 us  [device_body(): lax.all_to_all(fold_rows(packed, experts), 'expert', split_axis=0, concat...]
    sub x1 -> x4, local copies, waits for them, and re-layouts: 0.01 us -> 15.5 us  [the longest x3 15.4 us: device_body(): rank = jnp.cumsum(mine.astype(jnp.int32), axis=1) - 1]
    all_to_all x0 -> x1, starting transfers between devices: none -> 15 us  [device_body(): lax.all_to_all(fold_rows(packed, experts), 'expert', split_axis=0, concat...]
    dot_general x6 -> x2, matrix products: 9.91 us -> 3.22 us  [the longest x1 2.05 us: device_body(): lax.dot_general(token_slot, token_rows, (((0,), (0,)), ((), ())), preferr...]
    dot_general x2 -> x4, matrix products: 5.02 us -> 11 us  [fwd_t(): lax.dot_general(rows, weight, (((1,), (1,)), ((), ())), preferred_element...]
    reshape x2 -> x4, local copies, waits for them, and re-layouts: 6.98 us -> 12.3 us  [the longest x2 7.16 us: device_body(): all_coded = all_coded.reshape(experts, routes)]
  transfers between devices with their start and end apart: 3 -> 4, of which waited for: 1 -> 2; matrix products, arithmetic and copies ran while one was open for 12% -> 9% of each run, Pallas kernels for 0% -> 0%
where the time goes in v4:
time: 539 us
  blocking collectives  384 us (71%)
  waiting for transfers between devices  67.1 us (12%)
  local copies, waits for them, and re-layouts  45.3 us (8%)
  matrix products  20.5 us (4%)
  starting transfers between devices  15.8 us (3%)
  other arithmetic  5.7 us (1%)
    all_gather x1, blocking collectives, device_body(): all_coded = lax.all_gather(coded, 'expert', axis=0, tiled=True)  330 us
    all_to_all x1, waiting for transfers between devices, device_body(): lax.all_to_all(fold_rows(packed, experts), 'expert', split_axis=0, concat...  66.5 us
    all_to_all x1, blocking collectives, device_body(): lax.all_to_all(fold_rows(share.astype(jnp.bfloat16), experts), 'expert',...  54.6 us
    sub x3, local copies, waits for them, and re-layouts, device_body(): rank = jnp.cumsum(mine.astype(jnp.int32), axis=1) - 1  15.4 us
    all_to_all x1, starting transfers between devices, device_body(): lax.all_to_all(fold_rows(packed, experts), 'expert', split_axis=0, concat...  15 us
    dot_general x4, matrix products, fwd_t(): lax.dot_general(rows, weight, (((1,), (1,)), ((), ())), preferred_element...  11 us
  transfers between devices with their start and end apart: 4, of which 2 were waited for; matrix products, arithmetic and copies ran while one was open for 9% of the time, Pallas kernels for 0%

profile of v4, /device:TPU:32, one launch (start us, length us, event | category | flops | bytes accessed | tf_op | source)
XLA Modules:
  0.0 539.1 jit_solution(10342919052675396747)
XLA Ops:
  0.0 0.8 copy.42
  2.8 2.1 convolution_convert_fusion
  4.8 2.9 reshape.88
  7.7 15.0 %all-to-all-start = ((bf16[128,4,2688]{2,1,0:T(4,128)(2,1)}), bf16[128,4,2688]{2,1,0:T(4,128)(2,1)S(1)}, u32[]{:S(2)}, u32[]{:S(2)}) async-start(bf16[128,4,2688]{2,1,0:T(4,128)(2,1)} %reshape.88), calls=%async_computation | async-start | bytes 5505024 | tf_op jit(solution)/shard_map/all_to_all | solution.py:63
  22.8 66.5 %all-to-all-done = bf16[128,4,2688]{2,1,0:T(4,128)(2,1)S(1)} async-done(((bf16[128,4,2688]{2,1,0:T(4,128)(2,1)}), bf16[128,4,2688]{2,1,0:T(4,128)(2,1)S(1)}, u32[]{:S(2)}, u32[]{:S(2)}) %all-to-all-start) | async-done | bytes 2752544 | tf_op jit(solution)/shard_map/all_to_all | solution.py:63
  89.3 3.0 reshape.89
  92.3 5.4 %dynamic-slice_bitcast_fusion = (bf16[1792,512]{1,0:T(8,128)(2,1)S(1)}, bf16[1792,512]{1,0:T(8,128)(2,1)}, bf16[1792,512]{1,0:T(8,128)(2,1)}, bf16[1792,512]{1,0:T(8,128)(2,1)S(1)}) fusion(bf16[1,3584,512]{2,1,0:T(8,128)(2,1)} %param.12, s32[]{:T(128)S(6)} %select_n.61, s32[]{:T(128)S(6)} %select_n.59, bf16[1,3584,512]{2,1,0:T(8,128)(2,1)} %param.11), kind=kLoop, calls=%fused_computation.12 | loop fusion | bytes 14680072 | tf_op jit(solution)/shard_map/dynamic_slice | solution.py:44
  97.7 2.6 pad_maximum_fusion.1
  100.8 329.8 %all_gather.3 = s32[16384,2]{0,1:T(2,128)S(1)} all-gather(s32[128,2]{0,1:T(2,128)S(1)} %get-tuple-element.14), channel_id=1, replica_groups=mesh['expert'=128,'tensor'=2] {'expert'}, dimensions={0}, use_global_device_ids=true | all-gather | bytes 132096 | tf_op jit(solution)/shard_map/all_gather | solution.py:33
  430.5 4.9 copy.47
  435.4 7.1 %reshape.90 = s32[128,2,128]{2,1,0:T(2,128)S(1)} reshape(s32[16384,2]{1,0:T(8,128)} %copy.47) | data formatting | bytes 262144 | tf_op jit(solution)/shard_map/reshape | solution.py:34
  443.2 10.0 %sub.30 = s32[16384,2]{1,0:T(8,128)} reshape(s32[128,2,128]{2,1,0:T(2,128)S(1)} %copy.52) | data formatting | bytes 262144 | tf_op jit(solution)/shard_map/sub | solution.py:70
  453.2 5.3 copy.53
  458.5 1.1 fusion.31
  460.2 3.0 fusion.5
  463.5 3.2 fusion.2
  466.7 3.1 convolution_add_fusion.1
  469.8 2.6 fusion.28
  472.9 1.6 fusion.1
  475.2 3.7 fusion
  478.9 2.3 reshape.92
  481.2 54.6 %all_to_all.10 = bf16[128,4,1344]{2,1,0:T(4,128)(2,1)S(1)} all-to-all(bf16[128,4,1344]{2,1,0:T(4,128)(2,1)S(1)} %reshape.92), channel_id=1, replica_groups=mesh['expert'=128,'tensor'=2] {'expert'}, dimensions={0} | all-to-all | bytes 2752512 | tf_op jit(solution)/shard_map/all_to_all | solution.py:106
  535.7 2.2 reshape.93
  537.9 1.2 convolution_convert_fusion.1
  (45 shorter events, 5.0 us)
Async XLA Ops:
  7.7 81.5 %all-to-all-start = ((bf16[128,4,2688]{2,1,0:T(4,128)(2,1)}), bf16[128,4,2688]{2,1,0:T(4,128)(2,1)S(1)}, u32[]{:S(2)}, u32[]{:S(2)}) async-start(bf16[128,4,2688]{2,1,0:T(4,128)(2,1)} %reshape.88), calls=%async_computation | async-start | bytes 5505024 | tf_op jit(solution)/shard_map/all_to_all | solution.py:63
  92.3 374.5 %collective-permute-start = (bf16[384,3584]{1,0:T(8,128)(2,1)}, bf16[384,3584]{1,0:T(8,128)(2,1)}, u32[]{:S(2)}, u32[]{:S(2)}) collective-permute-start(bf16[384,3584]{1,0:T(8,128)(2,1)} %reshape.89), channel_id=1, source_target_pairs={{0,1},{1,0},{2,3},{3,2},{4,5},{5,4},{6,7},{7,6},{8,9},{9,8},{10,11... | collective-permute-start | bytes 8257544 | tf_op jit(solution)/shard_map/ppermute | solution.py:67
  97.7 2.6 copy-start
  100.3 374.3 %collective-permute-start.2 = (bf16[1792,1024]{1,0:T(8,128)(2,1)}, bf16[1792,1024]{1,0:T(8,128)(2,1)}, u32[]{:S(2)}, u32[]{:S(2)}) collective-permute-start(bf16[1792,1024]{1,0:T(8,128)(2,1)} %pad_maximum_fusion.1), channel_id=1, source_target_pairs={{0,1},{1,0},{2,3},{3,2},{4,5},{5,4},{6,7},{7,6},{8,9},{9,8},{10,11... | collective-permute-start | bytes 11010056 | tf_op jit(solution)/shard_map/ppermute | solution.py:50
  460.2 3.0 copy-start.2
  460.2 3.3 copy-start.3
  463.5 3.2 copy-start.1
  466.7 3.1 copy-start.5
  469.8 3.1 copy-start.4
  472.6 2.6 collective-permute-start.1

commit v5 on v3

--- a/solution.py
+++ b/solution.py
@@ -25,15 +25,19 @@
     ffh = gate_w.shape[1]
 
     other_rows = (me + 1) % parts * half
-    sent_w = jnp.stack(
-        [
-            lax.dynamic_slice_in_dim(gate_w, other_rows, half, axis=0),
-            lax.dynamic_slice_in_dim(up_w, other_rows, half, axis=0),
-        ]
-    )
-    got_w = lax.ppermute(sent_w, "tensor", swap)
-    own_gate = lax.dynamic_slice_in_dim(gate_w, me * half, half, axis=0)
-    own_up = lax.dynamic_slice_in_dim(up_w, me * half, half, axis=0)
+
+    def rows_of(start):
+        return jnp.concatenate(
+            [
+                lax.dynamic_slice_in_dim(gate_w, start, half, axis=0),
+                lax.dynamic_slice_in_dim(up_w, start, half, axis=0),
+            ],
+            axis=1,
+        )
+
+    sent_gu = rows_of(other_rows)
+    got_gu = lax.ppermute(sent_gu, "tensor", swap)
+    own_gu = rows_of(me * half)
 
     flat_ids = expert_ids.reshape(routes)
     onehot = (flat_ids[:, None] == jnp.arange(experts, dtype=jnp.int32)[None, :]).astype(jnp.int32)
@@ -73,8 +77,9 @@
             rows, weight, (((1,), (1,)), ((), ())), preferred_element_type=jnp.float32
         )
 
-    gate_pre = fwd(own_rows[:, :half], own_gate) + fwd(got_rows[:, :half], sent_w[0])
-    up_pre = fwd(own_rows[:, :half], own_up) + fwd(got_rows[:, :half], sent_w[1])
+    gate_up = fwd(own_rows[:, :half], own_gu) + fwd(got_rows[:, :half], sent_gu)
+    gate_pre = gate_up[:, :ffh]
+    up_pre = gate_up[:, ffh:]
     hidden_grad = fwd_t(own_rows[:, half:], own_down) + fwd_t(got_rows[:, half:], other_down)
     hidden_grad = hidden_grad * weights.astype(jnp.float32)[:, None]
     sigmoid_gate = jax.nn.sigmoid(gate_pre)
@@ -82,19 +87,9 @@
         hidden_grad * up_pre * sigmoid_gate * (1.0 + gate_pre * (1.0 - sigmoid_gate))
     ).astype(jnp.bfloat16)
     up_grad = (hidden_grad * gate_pre * sigmoid_gate).astype(jnp.bfloat16)
-    got_grad = lax.ppermute(jnp.concatenate([gate_grad, up_grad], axis=1), "tensor", swap)
-
-    def back(grad, weight):
-        return lax.dot_general(
-            grad, weight, (((1,), (1,)), ((), ())), preferred_element_type=jnp.float32
-        )
-
-    share = (
-        back(gate_grad, own_gate)
-        + back(up_grad, own_up)
-        + back(got_grad[:, :ffh], got_w[0])
-        + back(got_grad[:, ffh:], got_w[1])
-    )
+    grads = jnp.concatenate([gate_grad, up_grad], axis=1)
+    got_grads = lax.ppermute(grads, "tensor", swap)
+    share = fwd_t(grads, own_gu) + fwd_t(got_grads, got_gu)
     outgoing_back = fold_rows(share.astype(jnp.bfloat16), experts, 128)
     returned = lax.all_to_all(outgoing_back, "expert", split_axis=0, concat_axis=0, tiled=True)
     summed = jnp.dot(

time: 185 us -> 184 us (level)
  matrix products: 25.1 us -> 21.3 us
  local copies, waits for them, and re-layouts: 20.7 us -> 23.2 us
    dot_general x4 -> x0, matrix products: 6.68 us -> none  [back(): lax.dot_general(grad, weight, (((1,), (1,)), ((), ())), preferred_element...]
    dot_general x2 -> x4, matrix products: 5.02 us -> 10.8 us  [fwd_t(): lax.dot_general(rows, weight, (((1,), (1,)), ((), ())), preferred_element...]
    dynamic_slice x2 -> x1, local copies, waits for them, and re-layouts: 1.89 us -> 5.41 us  [rows_of(): lax.dynamic_slice_in_dim(up_w, start, half, axis=0)]
    dot_general x4 -> x2, matrix products: 10.2 us -> 7.27 us  [fwd(): return jnp.dot(rows, weight, preferred_element_type=jnp.float32)]
    concatenate x1 -> x2, other arithmetic: 0.09 us -> 2.7 us  [the longest x1 2.6 us: rows_of(): jnp.concatenate([lax.dynamic_slice_in_dim(gate_w, start, half, axis=0), l...]
    another operation x3 -> x2, other arithmetic: 2.65 us -> 0.24 us  [the longest x1 2.4 us: per_device(): jnp.stack([lax.dynamic_slice_in_dim(gate_w, other_rows, half, axis=0), la...]
where the time goes in v5:
time: 184 us; the launch traced here: 183 us
  blocking collectives  130 us (71%)
  local copies, waits for them, and re-layouts  23.2 us (13%)
  matrix products  21.3 us (12%)
  other arithmetic  7.66 us (4%)
    all_to_all x1, blocking collectives, per_device(): lax.all_to_all(outgoing, 'expert', split_axis=0, concat_axis=0, tiled=True)  84.2 us
    all_to_all x1, blocking collectives, per_device(): lax.all_to_all(outgoing_back, 'expert', split_axis=0, concat_axis=0, tile...  45.6 us
    dot_general x4, matrix products, fwd_t(): lax.dot_general(rows, weight, (((1,), (1,)), ((), ())), preferred_element...  10.8 us
    dot_general x2, matrix products, fwd(): return jnp.dot(rows, weight, preferred_element_type=jnp.float32)  7.27 us
    dynamic_slice x1, local copies, waits for them, and re-layouts, rows_of(): lax.dynamic_slice_in_dim(up_w, start, half, axis=0)  5.41 us
    reshape x2, local copies, waits for them, and re-layouts, fold_rows(): return rows.reshape(experts, 4, per_expert // 4)  5.19 us
    reshape x1, local copies, waits for them, and re-layouts, per_device(): own_rows = received[:, :, :fold].reshape(total, 2 * half)  4.82 us
  transfers between devices with their start and end apart: 3, of which 1 were waited for; matrix products, arithmetic and copies ran while one was open for 12% of the time, Pallas kernels for 0%

profile of v5, /device:TPU:32, one launch (start us, length us, event | category | flops | bytes accessed | tf_op | source)
XLA Modules:
  0.0 183.4 jit_solution(228810932589566191)
XLA Ops:
  0.0 0.8 copy.44
  1.9 0.7 multiply_add_fusion.1
  2.6 0.8 copy.49
  4.1 2.1 %convolution_convert_fusion = bf16[384,3584]{1,0:T(8,128)(2,1)S(1)} fusion(bf16[128,1792]{1,0:T(8,128)(2,1)} %param.8, bf16[128,1792]{1,0:T(8,128)(2,1)} %param.7, s32[128,384]{1,0:T(8,128)S(1)} %convert_reduce_fusion), kind=kOutput, calls=%fused_computation | convolution fusion | flops 355581952 | bytes 3866624 | tf_op jit(solution)/shard_map/dot_general | solution.py:55
  6.1 2.9 %reshape.81 = bf16[128,4,2688]{2,1,0:T(4,128)(2,1)} reshape(bf16[384,3584]{1,0:T(8,128)(2,1)S(1)} %convolution_convert_fusion) | data formatting | bytes 5505024 | tf_op jit(solution)/shard_map/reshape | solution.py:9
  9.3 3.1 %pad_maximum_fusion.2 = bf16[128,4,2816]{2,1,0:T(4,128)(2,1)S(1)} fusion(bf16[128,4,128]{2,1,0:T(4,128)(2,1)S(1)} %broadcast_select_fusion, bf16[128,4,2688]{2,1,0:T(4,128)(2,1)} %reshape.81), kind=kLoop, calls=%fused_computation.4 | loop fusion | flops 5767168 | bytes 5767168 | tf_op jit(solution)/shard_map/concatenate | solution.py:62
  12.4 84.2 %all_to_all.10 = bf16[128,4,2816]{2,1,0:T(4,128)(2,1)S(1)} all-to-all(bf16[128,4,2816]{2,1,0:T(4,128)(2,1)S(1)} %pad_maximum_fusion.2), channel_id=1, replica_groups=mesh['expert'=128,'tensor'=2] {'expert'}, dimensions={0} | all-to-all | bytes 5767168 | tf_op jit(solution)/shard_map/all_to_all | solution.py:64
  96.5 2.5 %slice.41 = bf16[128,4,2688]{2,1,0:T(4,128)(2,1)} slice(bf16[128,4,2816]{2,1,0:T(4,128)(2,1)S(1)} %all_to_all.10), slice={[0:128], [0:4], [0:2688]} | slice | bytes 5505024 | tf_op jit(solution)/shard_map/slice | solution.py:66
  99.0 4.8 %reshape.82 = bf16[384,3584]{1,0:T(8,128)(2,1)} reshape(bf16[128,4,2688]{2,1,0:T(4,128)(2,1)} %slice.41) | data formatting | bytes 5505024 | tf_op jit(solution)/shard_map/reshape | solution.py:66
  103.9 5.4 %dynamic-slice_bitcast_fusion = (bf16[1792,512]{1,0:T(8,128)(2,1)S(1)}, bf16[1792,512]{1,0:T(8,128)(2,1)}, bf16[1792,512]{1,0:T(8,128)(2,1)}, bf16[1792,512]{1,0:T(8,128)(2,1)S(1)}) fusion(bf16[1,3584,512]{2,1,0:T(8,128)(2,1)} %param.12, s32[]{:T(128)S(6)} %select_n.31, s32[]{:T(128)S(6)} %select_n.29, bf16[1,3584,512]{2,1,0:T(8,128)(2,1)} %param.11), kind=kLoop, calls=%fused_computation.13 | loop fusion | bytes 14680072 | tf_op jit(solution)/shard_map/dynamic_slice | solution.py:33
  109.3 2.6 %pad_maximum_fusion.1 = bf16[1792,1024]{1,0:T(8,128)(2,1)} fusion(bf16[1792,512]{1,0:T(8,128)(2,1)S(1)} %get-tuple-element.7, bf16[1792,512]{1,0:T(8,128)(2,1)S(1)} %get-tuple-element.12), kind=kLoop, calls=%fused_computation.2 | loop fusion | flops 7340032 | bytes 7340032 | tf_op jit(solution)/shard_map/concatenate | solution.py:30
  111.9 0.3 copy-done.2
  112.2 0.5 collective-permute-start.2
  113.1 2.8 %fusion.5 = f32[384,512]{1,0:T(8,128)S(1)} fusion(bf16[1,512,3584]{2,1,0:T(8,128)(2,1)} %param.13, s32[]{:T(128)S(6)} %select_n.29, bf16[384,3584]{1,0:T(8,128)(2,1)} %reshape.82), kind=kOutput, calls=%fused_computation.11 | convolution fusion | flops 704643072 | bytes 3997700 | tf_op jit(solution)/shard_map/dot_general | solution.py:76
  116.0 4.2 %fusion.2 = f32[384,1024]{1,0:T(8,128)S(1)} fusion(bf16[1792,512]{1,0:T(8,128)(2,1)} %get-tuple-element.8, bf16[1792,512]{1,0:T(8,128)(2,1)} %get-tuple-element.11, bf16[384,3584]{1,0:T(8,128)(2,1)} %reshape.82), kind=kOutput, calls=%fused_computation.8 | convolution fusion | flops 1416626176 | bytes 6619136 | tf_op jit(solution)/shard_map/dot_general | solution.py:73
  120.2 3.1 %convolution_add_fusion.1 = f32[384,1024]{1,0:T(8,128)S(1)} fusion(f32[384,1024]{1,0:T(8,128)S(1)} %fusion.2, bf16[384,3584]{1,0:T(8,128)(2,1)} %collective-permute-done, bf16[1792,512]{1,0:T(8,128)(2,1)S(1)} %copy-done.1, bf16[1792,512]{1,0:T(8,128)(2,1)S(1)} %copy-done.3), kind=kOutput, calls=%fused_computation.19 | convolution fusion | flops 1417019392 | bytes 8192000 | tf_op jit(solution)/shard_map/dot_general | solution.py:73
  123.4 2.7 %fusion.28 = (bf16[384,512]{1,0:T(8,128)(2,1)S(1)}, bf16[384,512]{1,0:T(8,128)(2,1)S(1)}) fusion(f32[384,1024]{1,0:T(8,128)S(1)} %convolution_add_fusion.1, f32[384]{0:T(512)S(1)} %reshape.86, f32[384,512]{1,0:T(8,128)S(1)} %fusion.5, bf16[1,512,3584]{2,1,0:T(8,128)(2,1)S(1)} %copy-done.6, s32[]{:T(128)S(6)} %select_n.31, ...), kind=kOutput, calls=%fused_computation.32 | convolution fusion | flops 707592192 | bytes 6359044 | tf_op jit(solution)/shard_map/dot_general | solution.py:76
  126.3 1.6 fusion.1
  127.9 0.6 collective-permute-done.1
  128.5 3.7 %fusion = bf16[384,1792]{1,0:T(8,128)(2,1)S(1)} fusion(f32[384,1792]{1,0:T(8,128)S(1)} %fusion.1, bf16[384,1024]{1,0:T(8,128)(2,1)S(1)} %collective-permute-done.1, bf16[1792,1024]{1,0:T(8,128)(2,1)} %collective-permute-done.2), kind=kOutput, calls=%fused_computation.5 | convolution fusion | flops 1410662400 | bytes 8585216 | tf_op jit(solution)/shard_map/dot_general | solution.py:76
  132.2 2.3 %reshape.83 = bf16[128,4,1344]{2,1,0:T(4,128)(2,1)S(1)} reshape(bf16[384,1792]{1,0:T(8,128)(2,1)S(1)} %fusion) | data formatting | bytes 2752512 | tf_op jit(solution)/shard_map/reshape | solution.py:9
  134.4 45.6 %all_to_all.11 = bf16[128,4,1344]{2,1,0:T(4,128)(2,1)S(1)} all-to-all(bf16[128,4,1344]{2,1,0:T(4,128)(2,1)S(1)} %reshape.83), channel_id=1, replica_groups=mesh['expert'=128,'tensor'=2] {'expert'}, dimensions={0} | all-to-all | bytes 2752512 | tf_op jit(solution)/shard_map/all_to_all | solution.py:94
  180.1 2.2 %reshape.84 = bf16[384,1792]{1,0:T(8,128)(2,1)S(1)} reshape(bf16[128,4,1344]{2,1,0:T(4,128)(2,1)S(1)} %all_to_all.11) | data formatting | bytes 2752512 | tf_op jit(solution)/shard_map/reshape | solution.py:96
  182.3 1.2 convolution_convert_fusion.1
  (40 shorter events, 2.6 us)
Async XLA Ops:
  103.9 16.4 %collective-permute-start = (bf16[384,3584]{1,0:T(8,128)(2,1)}, bf16[384,3584]{1,0:T(8,128)(2,1)}, u32[]{:S(2)}, u32[]{:S(2)}) collective-permute-start(bf16[384,3584]{1,0:T(8,128)(2,1)} %reshape.82), channel_id=1, source_target_pairs={{0,1},{1,0},{2,3},{3,2},{4,5},{5,4},{6,7},{7,6},{8,9},{9,8},{10,11... | collective-permute-start | bytes 8257544 | tf_op jit(solution)/shard_map/ppermute | solution.py:67
  109.3 2.6 %copy-start = (bf16[1792,512]{1,0:T(8,128)(2,1)}, bf16[1792,512]{1,0:T(8,128)(2,1)S(1)}, u32[]{:S(2)}) copy-start(bf16[1792,512]{1,0:T(8,128)(2,1)S(1)} %get-tuple-element.7) | copy-start | bytes 5505028
  109.3 2.9 %copy-start.2 = (bf16[1792,512]{1,0:T(8,128)(2,1)}, bf16[1792,512]{1,0:T(8,128)(2,1)S(1)}, u32[]{:S(2)}) copy-start(bf16[1792,512]{1,0:T(8,128)(2,1)S(1)} %get-tuple-element.12) | copy-start | bytes 5505028
  112.2 15.7 %collective-permute-start.2 = (bf16[1792,1024]{1,0:T(8,128)(2,1)}, bf16[1792,1024]{1,0:T(8,128)(2,1)}, u32[]{:S(2)}, u32[]{:S(2)}) collective-permute-start(bf16[1792,1024]{1,0:T(8,128)(2,1)} %pad_maximum_fusion.1), channel_id=1, source_target_pairs={{0,1},{1,0},{2,3},{3,2},{4,5},{5,4},{6,7},{7,6},{8,9},{9,8},{10,11... | collective-permute-start | bytes 11010056 | tf_op jit(solution)/shard_map/ppermute | solution.py:39
  116.0 4.2 %copy-start.1 = (bf16[1792,512]{1,0:T(8,128)(2,1)S(1)}, bf16[1792,512]{1,0:T(8,128)(2,1)}, u32[]{:S(2)}) copy-start(bf16[1792,512]{1,0:T(8,128)(2,1)} %copy-done) | copy-start | bytes 5505028
  116.0 4.2 %copy-start.3 = (bf16[1792,512]{1,0:T(8,128)(2,1)S(1)}, bf16[1792,512]{1,0:T(8,128)(2,1)}, u32[]{:S(2)}) copy-start(bf16[1792,512]{1,0:T(8,128)(2,1)} %copy-done.2) | copy-start | bytes 5505028
  120.2 3.1 %copy-start.6 = (bf16[1,512,3584]{2,1,0:T(8,128)(2,1)S(1)}, bf16[1,512,3584]{2,1,0:T(8,128)(2,1)}, u32[]{:S(2)}) copy-start(bf16[1,512,3584]{2,1,0:T(8,128)(2,1)} %param.13) | copy-start | bytes 11010052
  123.3 2.9 %copy-start.4 = (bf16[1792,512]{1,0:T(8,128)(2,1)S(1)}, bf16[1792,512]{1,0:T(8,128)(2,1)}, u32[]{:S(2)}) copy-start(bf16[1792,512]{1,0:T(8,128)(2,1)} %get-tuple-element.8) | copy-start | bytes 5505028
  123.3 2.9 %copy-start.5 = (bf16[1792,512]{1,0:T(8,128)(2,1)S(1)}, bf16[1792,512]{1,0:T(8,128)(2,1)}, u32[]{:S(2)}) copy-start(bf16[1792,512]{1,0:T(8,128)(2,1)} %get-tuple-element.11) | copy-start | bytes 5505028
  126.1 2.4 %collective-permute-start.1 = (bf16[384,1024]{1,0:T(8,128)(2,1)S(1)}, bf16[384,1024]{1,0:T(8,128)(2,1)S(1)}, u32[]{:S(2)}, u32[]{:S(2)}) collective-permute-start(bf16[384,1024]{1,0:T(8,128)(2,1)S(1)} %pad_maximum_fusion.5), channel_id=1, source_target_pairs={{0,1},{1,0},{2,3},{3,2},{4,5},{5,4},{6,7},{7,6},{8,9},{9,8},{10,11... | collective-permute-start | bytes 2359304 | tf_op jit(solution)/shard_map/ppermute | solution.py:91

commit v6 on v3

--- a/solution.py
+++ b/solution.py
@@ -42,24 +42,20 @@
     route_slot = destination[:, None] == jnp.arange(total, dtype=jnp.int32)[None, :]
     token_slot = jnp.sum(route_slot.reshape(tok_rows, top, total).astype(jnp.int32), axis=1)
     token_slot = token_slot.astype(jnp.bfloat16)
-    slot_weight = jnp.sum(
-        jnp.where(route_slot, route_weight.reshape(routes).astype(jnp.float32)[:, None], 0.0),
-        axis=0,
+    route_weight_slot = jnp.sum(
+        jnp.where(route_slot, route_weight.reshape(routes).astype(jnp.float32)[:, None], 0.0)
+        .reshape(tok_rows, top, total),
+        axis=1,
     ).astype(jnp.bfloat16)
 
     token_rows = jnp.concatenate([features, cotangent], axis=1)
     packed = lax.dot_general(
         token_slot, token_rows, (((0,), (0,)), ((), ())), preferred_element_type=jnp.float32
     ).astype(jnp.bfloat16)
-    row_part = fold_rows(packed, experts, 128)
-    weight4 = jnp.pad(slot_weight.reshape(experts, capacity), ((0, 0), (0, 4 - capacity)))
-    lane = jnp.arange(128, dtype=jnp.int32)[None, None, :]
-    weight_part = jnp.where(lane == 0, weight4[:, :, None], jnp.zeros((), jnp.bfloat16))
-    outgoing = jnp.concatenate([row_part, weight_part], axis=2)
-    fold = row_part.shape[2]
-    received = lax.all_to_all(outgoing, "expert", split_axis=0, concat_axis=0, tiled=True)
-    weights = received[:, :capacity, fold].reshape(total)
-    own_rows = received[:, :, :fold].reshape(total, 2 * half)
+    received = lax.all_to_all(
+        fold_rows(packed, experts, 128), "expert", split_axis=0, concat_axis=0, tiled=True
+    )
+    own_rows = received.reshape(total, 2 * half)
     got_rows = lax.ppermute(own_rows, "tensor", swap)
     other_cols = (me + 1) % parts * half
     own_down = lax.dynamic_slice_in_dim(down_w, me * half, half, axis=1)
@@ -76,7 +72,6 @@
     gate_pre = fwd(own_rows[:, :half], own_gate) + fwd(got_rows[:, :half], sent_w[0])
     up_pre = fwd(own_rows[:, :half], own_up) + fwd(got_rows[:, :half], sent_w[1])
     hidden_grad = fwd_t(own_rows[:, half:], own_down) + fwd_t(got_rows[:, half:], other_down)
-    hidden_grad = hidden_grad * weights.astype(jnp.float32)[:, None]
     sigmoid_gate = jax.nn.sigmoid(gate_pre)
     gate_grad = (
         hidden_grad * up_pre * sigmoid_gate * (1.0 + gate_pre * (1.0 - sigmoid_gate))
@@ -98,7 +93,7 @@
     outgoing_back = fold_rows(share.astype(jnp.bfloat16), experts, 128)
     returned = lax.all_to_all(outgoing_back, "expert", split_axis=0, concat_axis=0, tiled=True)
     summed = jnp.dot(
-        token_slot, returned.reshape(total, half), preferred_element_type=jnp.float32
+        route_weight_slot, returned.reshape(total, half), preferred_element_type=jnp.float32
     )
     return summed.astype(jnp.bfloat16)
 

time: 185 us -> 173 us (0.935)
  blocking collectives: 130 us -> 81.5 us
  waiting for transfers between devices: 0.39 us -> 39 us
  starting transfers between devices: 0.6 us -> 7.93 us
  local copies, waits for them, and re-layouts: 20.7 us -> 15.1 us
  other arithmetic: 7.46 us -> 3.86 us
    all_to_all x2 -> x1, blocking collectives: 130 us -> 81.5 us  [per_device(): lax.all_to_all(fold_rows(packed, experts, 128), 'expert', split_axis=0, c...]
    all_to_all x0 -> x1, waiting for transfers between devices: none -> 38.6 us  [per_device(): lax.all_to_all(outgoing_back, 'expert', split_axis=0, concat_axis=0, tile...]
    all_to_all x0 -> x1, starting transfers between devices: none -> 7.15 us  [per_device(): lax.all_to_all(outgoing_back, 'expert', split_axis=0, concat_axis=0, tile...]
    concatenate x1 -> x0, other arithmetic: 3.09 us -> none  [per_device(): outgoing = jnp.concatenate([row_part, weight_part], axis=2)]
    slice x1 -> x0, local copies, waits for them, and re-layouts: 2.5 us -> none  [per_device(): own_rows = received[:, :, :fold].reshape(total, 2 * half)]
  transfers between devices with their start and end apart: 3 -> 4, of which waited for: 1 -> 2; matrix products, arithmetic and copies ran while one was open for 12% -> 13% of each run, Pallas kernels for 0% -> 0%
where the time goes in v6:
time: 173 us
  blocking collectives  81.5 us (47%)
  waiting for transfers between devices  39 us (23%)
  matrix products  25 us (14%)
  local copies, waits for them, and re-layouts  15.1 us (9%)
  starting transfers between devices  7.93 us (5%)
  other arithmetic  3.86 us (2%)
    all_to_all x1, blocking collectives, per_device(): lax.all_to_all(fold_rows(packed, experts, 128), 'expert', split_axis=0, c...  81.5 us
    all_to_all x1, waiting for transfers between devices, per_device(): lax.all_to_all(outgoing_back, 'expert', split_axis=0, concat_axis=0, tile...  38.6 us
    dot_general x4, matrix products, fwd(): return jnp.dot(rows, weight, preferred_element_type=jnp.float32)  10.2 us
    all_to_all x1, starting transfers between devices, per_device(): lax.all_to_all(outgoing_back, 'expert', split_axis=0, concat_axis=0, tile...  7.15 us
    dot_general x4, matrix products, back(): lax.dot_general(grad, weight, (((1,), (1,)), ((), ())), preferred_element...  6.68 us
    reshape x2, local copies, waits for them, and re-layouts, fold_rows(): return rows.reshape(experts, 4, per_expert // 4)  6.05 us
    dot_general x2, matrix products, fwd_t(): lax.dot_general(rows, weight, (((1,), (1,)), ((), ())), preferred_element...  4.87 us
  transfers between devices with their start and end apart: 4, of which 2 were waited for; matrix products, arithmetic and copies ran while one was open for 13% of the time, Pallas kernels for 0%

profile of v6, /device:TPU:32, one launch (start us, length us, event | category | flops | bytes accessed | tf_op | source)
XLA Modules:
  0.0 172.6 jit_solution(12965754980228286558)
XLA Ops:
  0.0 0.8 copy.24
  1.9 0.7 multiply_add_fusion
  2.7 2.1 %convolution_convert_fusion = bf16[384,3584]{1,0:T(8,128)(2,1)S(1)} fusion(bf16[128,1792]{1,0:T(8,128)(2,1)} %param.8, bf16[128,1792]{1,0:T(8,128)(2,1)} %param.7, s32[128,384]{1,0:T(8,128)S(1)} %convert_reduce_fusion), kind=kOutput, calls=%fused_computation | convolution fusion | flops 355581952 | bytes 3866624 | tf_op jit(solution)/shard_map/dot_general | solution.py:52
  4.8 2.9 %reshape.77 = bf16[128,4,2688]{2,1,0:T(4,128)(2,1)} reshape(bf16[384,3584]{1,0:T(8,128)(2,1)S(1)} %convolution_convert_fusion) | data formatting | bytes 5505024 | tf_op jit(solution)/shard_map/reshape | solution.py:9
  7.7 81.5 %all_to_all.10 = bf16[128,4,2688]{2,1,0:T(4,128)(2,1)S(1)} all-to-all(bf16[128,4,2688]{2,1,0:T(4,128)(2,1)} %reshape.77), channel_id=1, replica_groups=mesh['expert'=128,'tensor'=2] {'expert'}, dimensions={0} | all-to-all | bytes 5505024 | tf_op jit(solution)/shard_map/all_to_all | solution.py:55
  89.2 3.0 %reshape.78 = bf16[384,3584]{1,0:T(8,128)(2,1)} reshape(bf16[128,4,2688]{2,1,0:T(4,128)(2,1)S(1)} %all_to_all.10) | data formatting | bytes 5505024 | tf_op jit(solution)/shard_map/reshape | solution.py:58
  92.3 2.3 %constant_dynamic-slice_fusion = (bf16[1,1792,512]{2,1,0:T(8,128)(2,1)S(1)}, bf16[1,1792,512]{2,1,0:T(8,128)(2,1)S(1)}) fusion(bf16[1,3584,512]{2,1,0:T(8,128)(2,1)} %param.11, s32[]{:T(128)S(6)} %select_n.27, bf16[1,3584,512]{2,1,0:T(8,128)(2,1)} %param.12), kind=kLoop, calls=%fused_computation.66 | loop fusion | bytes 7340036 | tf_op jit(solution)/shard_map/dynamic_slice | solution.py:30
  94.6 2.3 %pad_maximum_fusion = bf16[2,1792,512]{2,1,0:T(8,128)(2,1)} fusion(bf16[1,1792,512]{2,1,0:T(8,128)(2,1)S(1)} %get-tuple-element.8, bf16[1,1792,512]{2,1,0:T(8,128)(2,1)S(1)} %get-tuple-element.7), kind=kLoop, calls=%fused_computation.1 | loop fusion | flops 1835008 | bytes 7340032 | tf_op jit(solution)/shard_map/stack | solution.py:28
  97.0 0.5 collective-permute-start.2
  97.5 2.9 %fusion.7 = f32[384,512]{1,0:T(8,128)S(1)} fusion(bf16[1,3584,512]{2,1,0:T(8,128)(2,1)} %param.11, s32[]{:T(128)S(6)} %select_n.25, bf16[384,3584]{1,0:T(8,128)(2,1)} %reshape.78), kind=kOutput, calls=%fused_computation.14 | convolution fusion | flops 704643072 | bytes 3997700 | tf_op jit(solution)/shard_map/dot_general | solution.py:65
  100.5 2.4 %fusion.12 = f32[384,512]{1,0:T(8,128)S(1)} fusion(bf16[1,3584,512]{2,1,0:T(8,128)(2,1)S(1)} %copy-done.3, s32[]{:T(128)S(6)} %select_n.25, bf16[384,3584]{1,0:T(8,128)(2,1)} %reshape.78), kind=kOutput, calls=%fused_computation.19 | convolution fusion | flops 704643072 | bytes 3997700 | tf_op jit(solution)/shard_map/dot_general | solution.py:65
  102.9 2.5 %fusion.16 = f32[384,512]{1,0:T(8,128)S(1)} fusion(bf16[1,512,3584]{2,1,0:T(8,128)(2,1)} %param.13, s32[]{:T(128)S(6)} %select_n.25, bf16[384,3584]{1,0:T(8,128)(2,1)S(1)} %copy-done.4), kind=kOutput, calls=%fused_computation.23 | convolution fusion | flops 704643072 | bytes 3997700 | tf_op jit(solution)/shard_map/dot_general | solution.py:68
  105.4 2.4 %fusion.43 = f32[384,512]{1,0:T(8,128)S(1)} fusion(f32[384,512]{1,0:T(8,128)S(1)} %fusion.7, bf16[1,1792,512]{2,1,0:T(8,128)(2,1)S(1)} %copy-done.1, bf16[384,3584]{1,0:T(8,128)(2,1)} %collective-permute-done), kind=kOutput, calls=%fused_computation.38 | convolution fusion | flops 704839680 | bytes 4784128 | tf_op jit(solution)/shard_map/dot_general | solution.py:65
  107.9 2.3 %multiply_convert_fusion = (bf16[384,512]{1,0:T(8,128)(2,1)S(1)}, f32[384,512]{1,0:T(8,128)S(1)}) fusion(f32[384,512]{1,0:T(8,128)S(1)} %fusion.43, f32[384,512]{1,0:T(8,128)S(1)} %fusion.16, bf16[1,512,3584]{2,1,0:T(8,128)(2,1)S(1)} %copy-done.5, s32[]{:T(128)S(6)} %select_n.27, bf16[384,3584]{1,0:T(8,128)(2,1)} %collective-permute-done), kind=kOutput, calls=%fused_computation.48 | convolution fusion | flops 706019328 | bytes 5963780 | tf_op jit(solution)/shard_map/dot_general | solution.py:68
  110.2 2.5 %fusion.46 = bf16[384,512]{1,0:T(8,128)(2,1)S(1)} fusion(f32[384,512]{1,0:T(8,128)S(1)} %get-tuple-element.6, f32[384,512]{1,0:T(8,128)S(1)} %fusion.12, bf16[1,1792,512]{2,1,0:T(8,128)(2,1)S(1)} %get-tuple-element.8, bf16[384,3584]{1,0:T(8,128)(2,1)} %collective-permute-done, f32[384,512]{1,0:T(8,128)S(1)} %fusion.43), kind=kOutput, calls=%fused_computation.39 | convolution fusion | flops 706805760 | bytes 5963776 | tf_op jit(solution)/shard_map/dot_general | solution.py:65
  113.2 0.9 fusion.5
  114.1 0.9 convolution_add_fusion.1
  115.4 2.4 %fusion.2 = f32[384,1792]{1,0:T(8,128)S(1)} fusion(bf16[2,1792,512]{2,1,0:T(8,128)(2,1)} %collective-permute-done.2, bf16[384,1024]{1,0:T(8,128)(2,1)S(1)} %collective-permute-done.1), kind=kOutput, calls=%fused_computation.8 | convolution fusion | flops 704643072 | bytes 4980736 | tf_op jit(solution)/shard_map/dot_general | solution.py:83
  117.8 2.4 %fusion.1 = bf16[384,1792]{1,0:T(8,128)(2,1)S(1)} fusion(f32[384,1792]{1,0:T(8,128)S(1)} %fusion.2, f32[384,1792]{1,0:T(8,128)S(1)} %convolution_add_fusion.1, bf16[2,1792,512]{2,1,0:T(8,128)(2,1)} %collective-permute-done.2, bf16[384,1024]{1,0:T(8,128)(2,1)S(1)} %collective-permute-done.1), kind=kOutput, calls=%fused_computation.5 | convolution fusion | flops 706707456 | bytes 9109504 | tf_op jit(solution)/shard_map/dot_general | solution.py:83
  120.3 3.1 %reshape.79 = bf16[128,4,1344]{2,1,0:T(4,128)(2,1)} reshape(bf16[384,1792]{1,0:T(8,128)(2,1)S(1)} %fusion.1) | data formatting | bytes 2752512 | tf_op jit(solution)/shard_map/reshape | solution.py:9
  123.4 7.2 %all-to-all-start.1 = ((bf16[128,4,1344]{2,1,0:T(4,128)(2,1)}), bf16[128,4,1344]{2,1,0:T(4,128)(2,1)S(1)}, u32[]{:S(2)}, u32[]{:S(2)}) async-start(bf16[128,4,1344]{2,1,0:T(4,128)(2,1)} %reshape.79), calls=%async_computation.1 | async-start | bytes 2883584 | tf_op jit(solution)/shard_map/all_to_all | solution.py:94
  130.7 38.6 %all-to-all-done.1 = bf16[128,4,1344]{2,1,0:T(4,128)(2,1)S(1)} async-done(((bf16[128,4,1344]{2,1,0:T(4,128)(2,1)}), bf16[128,4,1344]{2,1,0:T(4,128)(2,1)S(1)}, u32[]{:S(2)}, u32[]{:S(2)}) %all-to-all-start.1) | async-done | bytes 1376288 | tf_op jit(solution)/shard_map/all_to_all | solution.py:94
  169.3 2.2 %reshape.80 = bf16[384,1792]{1,0:T(8,128)(2,1)S(1)} reshape(bf16[128,4,1344]{2,1,0:T(4,128)(2,1)S(1)} %all-to-all-done.1) | data formatting | bytes 2752512 | tf_op jit(solution)/shard_map/reshape | solution.py:96
  171.5 1.2 convolution_convert_fusion.1
  (35 shorter events, 2.3 us)
Async XLA Ops:
  92.3 13.2 %collective-permute-start = (bf16[384,3584]{1,0:T(8,128)(2,1)}, bf16[384,3584]{1,0:T(8,128)(2,1)}, u32[]{:S(2)}, u32[]{:S(2)}) collective-permute-start(bf16[384,3584]{1,0:T(8,128)(2,1)} %reshape.78), channel_id=1, source_target_pairs={{0,1},{1,0},{2,3},{3,2},{4,5},{5,4},{6,7},{7,6},{8,9},{9,8},{10,11... | collective-permute-start | bytes 8257544 | tf_op jit(solution)/shard_map/ppermute | solution.py:59
  94.5 2.4 %copy-start = (bf16[1,1792,512]{2,1,0:T(8,128)(2,1)}, bf16[1,1792,512]{2,1,0:T(8,128)(2,1)S(1)}, u32[]{:S(2)}) copy-start(bf16[1,1792,512]{2,1,0:T(8,128)(2,1)S(1)} %get-tuple-element.7) | copy-start | bytes 5505028
  97.0 18.1 %collective-permute-start.2 = (bf16[2,1792,512]{2,1,0:T(8,128)(2,1)}, bf16[2,1792,512]{2,1,0:T(8,128)(2,1)}, u32[]{:S(2)}, u32[]{:S(2)}) collective-permute-start(bf16[2,1792,512]{2,1,0:T(8,128)(2,1)} %pad_maximum_fusion), channel_id=1, source_target_pairs={{0,1},{1,0},{2,3},{3,2},{4,5},{5,4},{6,7},{7,6},{8,9},{9,8},{10,11... | collective-permute-start | bytes 11010056 | tf_op jit(solution)/shard_map/ppermute | solution.py:34
  97.5 3.0 %copy-start.3 = (bf16[1,3584,512]{2,1,0:T(8,128)(2,1)S(1)}, bf16[1,3584,512]{2,1,0:T(8,128)(2,1)}, u32[]{:S(2)}) copy-start(bf16[1,3584,512]{2,1,0:T(8,128)(2,1)} %param.12) | copy-start | bytes 11010052
  100.5 2.4 %copy-start.4 = (bf16[384,3584]{1,0:T(8,128)(2,1)S(1)}, bf16[384,3584]{1,0:T(8,128)(2,1)}, u32[]{:S(2)}) copy-start(bf16[384,3584]{1,0:T(8,128)(2,1)} %reshape.78) | copy-start | bytes 8257540
  102.8 2.6 %copy-start.1 = (bf16[1,1792,512]{2,1,0:T(8,128)(2,1)S(1)}, bf16[1,1792,512]{2,1,0:T(8,128)(2,1)}, u32[]{:S(2)}) copy-start(bf16[1,1792,512]{2,1,0:T(8,128)(2,1)} %copy-done) | copy-start | bytes 5505028
  105.4 2.5 %copy-start.5 = (bf16[1,512,3584]{2,1,0:T(8,128)(2,1)S(1)}, bf16[1,512,3584]{2,1,0:T(8,128)(2,1)}, u32[]{:S(2)}) copy-start(bf16[1,512,3584]{2,1,0:T(8,128)(2,1)} %param.13) | copy-start | bytes 11010052
  110.2 2.9 %copy-start.2 = (bf16[1,3584,512]{2,1,0:T(8,128)(2,1)S(1)}, bf16[1,3584,512]{2,1,0:T(8,128)(2,1)}, u32[]{:S(2)}) copy-start(bf16[1,3584,512]{2,1,0:T(8,128)(2,1)} %param.11) | copy-start | bytes 11010052
  112.9 2.6 %collective-permute-start.1 = (bf16[384,1024]{1,0:T(8,128)(2,1)S(1)}, bf16[384,1024]{1,0:T(8,128)(2,1)S(1)}, u32[]{:S(2)}, u32[]{:S(2)}) collective-permute-start(bf16[384,1024]{1,0:T(8,128)(2,1)S(1)} %pad_maximum_fusion.1), channel_id=1, source_target_pairs={{0,1},{1,0},{2,3},{3,2},{4,5},{5,4},{6,7},{7,6},{8,9},{9,8},{10,11... | collective-permute-start | bytes 2359304 | tf_op jit(solution)/shard_map/ppermute | solution.py:80
  120.3 10.3 %copy-start.6 = (bf16[128,2]{0,1:T(2,128)(2,1)S(1)}, bf16[128,2]{0,1:T(2,128)(2,1)}, u32[]{:S(2)}) copy-start(bf16[128,2]{0,1:T(2,128)(2,1)} %param.10) | copy-start | bytes 1540
  123.4 45.9 %all-to-all-start.1 = ((bf16[128,4,1344]{2,1,0:T(4,128)(2,1)}), bf16[128,4,1344]{2,1,0:T(4,128)(2,1)S(1)}, u32[]{:S(2)}, u32[]{:S(2)}) async-start(bf16[128,4,1344]{2,1,0:T(4,128)(2,1)} %reshape.79), calls=%async_computation.1 | async-start | bytes 2883584 | tf_op jit(solution)/shard_map/all_to_all | solution.py:94

commit v7 on v6

--- a/solution.py
+++ b/solution.py
@@ -4,12 +4,12 @@
 from jax.sharding import PartitionSpec as P
 
 
-def fold_rows(rows, experts, lanes):
+def fold_rows(rows, experts):
     per_expert = rows.size // experts
     return rows.reshape(experts, 4, per_expert // 4)
 
 
-def per_device(features, cotangent, expert_ids, route_weight, gate_weight, up_weight, down_weight):
+def device_body(features, cotangent, expert_ids, route_weight, gate_weight, up_weight, down_weight):
     experts = lax.axis_size("expert")
     parts = lax.axis_size("tensor")
     me = lax.axis_index("tensor")
@@ -53,7 +53,7 @@
         token_slot, token_rows, (((0,), (0,)), ((), ())), preferred_element_type=jnp.float32
     ).astype(jnp.bfloat16)
     received = lax.all_to_all(
-        fold_rows(packed, experts, 128), "expert", split_axis=0, concat_axis=0, tiled=True
+        fold_rows(packed, experts), "expert", split_axis=0, concat_axis=0, tiled=True
     )
     own_rows = received.reshape(total, 2 * half)
     got_rows = lax.ppermute(own_rows, "tensor", swap)
@@ -90,7 +90,7 @@
         + back(got_grad[:, :ffh], got_w[0])
         + back(got_grad[:, ffh:], got_w[1])
     )
-    outgoing_back = fold_rows(share.astype(jnp.bfloat16), experts, 128)
+    outgoing_back = fold_rows(share.astype(jnp.bfloat16), experts)
     returned = lax.all_to_all(outgoing_back, "expert", split_axis=0, concat_axis=0, tiled=True)
     summed = jnp.dot(
         route_weight_slot, returned.reshape(total, half), preferred_element_type=jnp.float32
@@ -110,5 +110,5 @@
     )
     out_specs = P("expert", "tensor")
     return jax.shard_map(
-        per_device, mesh=mesh, in_specs=in_specs, out_specs=out_specs, check_vma=False
+        device_body, mesh=mesh, in_specs=in_specs, out_specs=out_specs, check_vma=False
     )

time: 173 us -> 173 us (level)
  no operation moved by 1% of the time
where the time goes in v7:
time: 173 us
  blocking collectives  81.5 us (47%)
  waiting for transfers between devices  39 us (23%)
  matrix products  25 us (14%)
  local copies, waits for them, and re-layouts  15.1 us (9%)
  starting transfers between devices  7.93 us (5%)
  other arithmetic  3.86 us (2%)
    all_to_all x1, blocking collectives, device_body(): lax.all_to_all(fold_rows(packed, experts), 'expert', split_axis=0, concat...  81.5 us
    all_to_all x1, waiting for transfers between devices, device_body(): lax.all_to_all(outgoing_back, 'expert', split_axis=0, concat_axis=0, tile...  38.6 us
    dot_general x4, matrix products, fwd(): return jnp.dot(rows, weight, preferred_element_type=jnp.float32)  10.2 us
    all_to_all x1, starting transfers between devices, device_body(): lax.all_to_all(outgoing_back, 'expert', split_axis=0, concat_axis=0, tile...  7.15 us
    dot_general x4, matrix products, back(): lax.dot_general(grad, weight, (((1,), (1,)), ((), ())), preferred_element...  6.68 us
    reshape x2, local copies, waits for them, and re-layouts, fold_rows(): return rows.reshape(experts, 4, per_expert // 4)  6.05 us
    dot_general x2, matrix products, fwd_t(): lax.dot_general(rows, weight, (((1,), (1,)), ((), ())), preferred_element...  4.87 us
  transfers between devices with their start and end apart: 4, of which 2 were waited for; matrix products, arithmetic and copies ran while one was open for 13% of the time, Pallas kernels for 0%

profile of v7, /device:TPU:32, one launch (start us, length us, event | category | flops | bytes accessed | tf_op | source)
XLA Modules:
  0.0 172.6 jit_solution(12965754980228286558)
XLA Ops:
  0.0 0.8 copy.24
  1.9 0.7 multiply_add_fusion
  2.7 2.1 %convolution_convert_fusion = bf16[384,3584]{1,0:T(8,128)(2,1)S(1)} fusion(bf16[128,1792]{1,0:T(8,128)(2,1)} %param.8, bf16[128,1792]{1,0:T(8,128)(2,1)} %param.7, s32[128,384]{1,0:T(8,128)S(1)} %convert_reduce_fusion), kind=kOutput, calls=%fused_computation | convolution fusion | flops 355581952 | bytes 3866624 | tf_op jit(solution)/shard_map/dot_general | solution.py:52
  4.8 2.9 %reshape.77 = bf16[128,4,2688]{2,1,0:T(4,128)(2,1)} reshape(bf16[384,3584]{1,0:T(8,128)(2,1)S(1)} %convolution_convert_fusion) | data formatting | bytes 5505024 | tf_op jit(solution)/shard_map/reshape | solution.py:9
  7.7 81.5 %all_to_all.10 = bf16[128,4,2688]{2,1,0:T(4,128)(2,1)S(1)} all-to-all(bf16[128,4,2688]{2,1,0:T(4,128)(2,1)} %reshape.77), channel_id=1, replica_groups=mesh['expert'=128,'tensor'=2] {'expert'}, dimensions={0} | all-to-all | bytes 5505024 | tf_op jit(solution)/shard_map/all_to_all | solution.py:55
  89.2 3.0 %reshape.78 = bf16[384,3584]{1,0:T(8,128)(2,1)} reshape(bf16[128,4,2688]{2,1,0:T(4,128)(2,1)S(1)} %all_to_all.10) | data formatting | bytes 5505024 | tf_op jit(solution)/shard_map/reshape | solution.py:58
  92.3 2.3 %constant_dynamic-slice_fusion = (bf16[1,1792,512]{2,1,0:T(8,128)(2,1)S(1)}, bf16[1,1792,512]{2,1,0:T(8,128)(2,1)S(1)}) fusion(bf16[1,3584,512]{2,1,0:T(8,128)(2,1)} %param.11, s32[]{:T(128)S(6)} %select_n.27, bf16[1,3584,512]{2,1,0:T(8,128)(2,1)} %param.12), kind=kLoop, calls=%fused_computation.66 | loop fusion | bytes 7340036 | tf_op jit(solution)/shard_map/dynamic_slice | solution.py:30
  94.6 2.3 %pad_maximum_fusion = bf16[2,1792,512]{2,1,0:T(8,128)(2,1)} fusion(bf16[1,1792,512]{2,1,0:T(8,128)(2,1)S(1)} %get-tuple-element.8, bf16[1,1792,512]{2,1,0:T(8,128)(2,1)S(1)} %get-tuple-element.7), kind=kLoop, calls=%fused_computation.1 | loop fusion | flops 1835008 | bytes 7340032 | tf_op jit(solution)/shard_map/stack | solution.py:28
  97.0 0.5 collective-permute-start.2
  97.5 2.9 %fusion.7 = f32[384,512]{1,0:T(8,128)S(1)} fusion(bf16[1,3584,512]{2,1,0:T(8,128)(2,1)} %param.11, s32[]{:T(128)S(6)} %select_n.25, bf16[384,3584]{1,0:T(8,128)(2,1)} %reshape.78), kind=kOutput, calls=%fused_computation.14 | convolution fusion | flops 704643072 | bytes 3997700 | tf_op jit(solution)/shard_map/dot_general | solution.py:65
  100.5 2.4 %fusion.12 = f32[384,512]{1,0:T(8,128)S(1)} fusion(bf16[1,3584,512]{2,1,0:T(8,128)(2,1)S(1)} %copy-done.3, s32[]{:T(128)S(6)} %select_n.25, bf16[384,3584]{1,0:T(8,128)(2,1)} %reshape.78), kind=kOutput, calls=%fused_computation.19 | convolution fusion | flops 704643072 | bytes 3997700 | tf_op jit(solution)/shard_map/dot_general | solution.py:65
  102.9 2.5 %fusion.16 = f32[384,512]{1,0:T(8,128)S(1)} fusion(bf16[1,512,3584]{2,1,0:T(8,128)(2,1)} %param.13, s32[]{:T(128)S(6)} %select_n.25, bf16[384,3584]{1,0:T(8,128)(2,1)S(1)} %copy-done.4), kind=kOutput, calls=%fused_computation.23 | convolution fusion | flops 704643072 | bytes 3997700 | tf_op jit(solution)/shard_map/dot_general | solution.py:68
  105.4 2.4 %fusion.43 = f32[384,512]{1,0:T(8,128)S(1)} fusion(f32[384,512]{1,0:T(8,128)S(1)} %fusion.7, bf16[1,1792,512]{2,1,0:T(8,128)(2,1)S(1)} %copy-done.1, bf16[384,3584]{1,0:T(8,128)(2,1)} %collective-permute-done), kind=kOutput, calls=%fused_computation.38 | convolution fusion | flops 704839680 | bytes 4784128 | tf_op jit(solution)/shard_map/dot_general | solution.py:65
  107.9 2.3 %multiply_convert_fusion = (bf16[384,512]{1,0:T(8,128)(2,1)S(1)}, f32[384,512]{1,0:T(8,128)S(1)}) fusion(f32[384,512]{1,0:T(8,128)S(1)} %fusion.43, f32[384,512]{1,0:T(8,128)S(1)} %fusion.16, bf16[1,512,3584]{2,1,0:T(8,128)(2,1)S(1)} %copy-done.5, s32[]{:T(128)S(6)} %select_n.27, bf16[384,3584]{1,0:T(8,128)(2,1)} %collective-permute-done), kind=kOutput, calls=%fused_computation.48 | convolution fusion | flops 706019328 | bytes 5963780 | tf_op jit(solution)/shard_map/dot_general | solution.py:68
  110.2 2.5 %fusion.46 = bf16[384,512]{1,0:T(8,128)(2,1)S(1)} fusion(f32[384,512]{1,0:T(8,128)S(1)} %get-tuple-element.6, f32[384,512]{1,0:T(8,128)S(1)} %fusion.12, bf16[1,1792,512]{2,1,0:T(8,128)(2,1)S(1)} %get-tuple-element.8, bf16[384,3584]{1,0:T(8,128)(2,1)} %collective-permute-done, f32[384,512]{1,0:T(8,128)S(1)} %fusion.43), kind=kOutput, calls=%fused_computation.39 | convolution fusion | flops 706805760 | bytes 5963776 | tf_op jit(solution)/shard_map/dot_general | solution.py:65
  113.2 0.9 fusion.5
  114.1 0.9 convolution_add_fusion.1
  115.4 2.4 %fusion.2 = f32[384,1792]{1,0:T(8,128)S(1)} fusion(bf16[2,1792,512]{2,1,0:T(8,128)(2,1)} %collective-permute-done.2, bf16[384,1024]{1,0:T(8,128)(2,1)S(1)} %collective-permute-done.1), kind=kOutput, calls=%fused_computation.8 | convolution fusion | flops 704643072 | bytes 4980736 | tf_op jit(solution)/shard_map/dot_general | solution.py:83
  117.8 2.4 %fusion.1 = bf16[384,1792]{1,0:T(8,128)(2,1)S(1)} fusion(f32[384,1792]{1,0:T(8,128)S(1)} %fusion.2, f32[384,1792]{1,0:T(8,128)S(1)} %convolution_add_fusion.1, bf16[2,1792,512]{2,1,0:T(8,128)(2,1)} %collective-permute-done.2, bf16[384,1024]{1,0:T(8,128)(2,1)S(1)} %collective-permute-done.1), kind=kOutput, calls=%fused_computation.5 | convolution fusion | flops 706707456 | bytes 9109504 | tf_op jit(solution)/shard_map/dot_general | solution.py:83
  120.3 3.1 %reshape.79 = bf16[128,4,1344]{2,1,0:T(4,128)(2,1)} reshape(bf16[384,1792]{1,0:T(8,128)(2,1)S(1)} %fusion.1) | data formatting | bytes 2752512 | tf_op jit(solution)/shard_map/reshape | solution.py:9
  123.4 7.2 %all-to-all-start.1 = ((bf16[128,4,1344]{2,1,0:T(4,128)(2,1)}), bf16[128,4,1344]{2,1,0:T(4,128)(2,1)S(1)}, u32[]{:S(2)}, u32[]{:S(2)}) async-start(bf16[128,4,1344]{2,1,0:T(4,128)(2,1)} %reshape.79), calls=%async_computation.1 | async-start | bytes 2883584 | tf_op jit(solution)/shard_map/all_to_all | solution.py:94
  130.7 38.6 %all-to-all-done.1 = bf16[128,4,1344]{2,1,0:T(4,128)(2,1)S(1)} async-done(((bf16[128,4,1344]{2,1,0:T(4,128)(2,1)}), bf16[128,4,1344]{2,1,0:T(4,128)(2,1)S(1)}, u32[]{:S(2)}, u32[]{:S(2)}) %all-to-all-start.1) | async-done | bytes 1376288 | tf_op jit(solution)/shard_map/all_to_all | solution.py:94
  169.3 2.2 %reshape.80 = bf16[384,1792]{1,0:T(8,128)(2,1)S(1)} reshape(bf16[128,4,1344]{2,1,0:T(4,128)(2,1)S(1)} %all-to-all-done.1) | data formatting | bytes 2752512 | tf_op jit(solution)/shard_map/reshape | solution.py:96
  171.5 1.2 convolution_convert_fusion.1
  (35 shorter events, 2.3 us)
Async XLA Ops:
  92.3 13.2 %collective-permute-start = (bf16[384,3584]{1,0:T(8,128)(2,1)}, bf16[384,3584]{1,0:T(8,128)(2,1)}, u32[]{:S(2)}, u32[]{:S(2)}) collective-permute-start(bf16[384,3584]{1,0:T(8,128)(2,1)} %reshape.78), channel_id=1, source_target_pairs={{0,1},{1,0},{2,3},{3,2},{4,5},{5,4},{6,7},{7,6},{8,9},{9,8},{10,11... | collective-permute-start | bytes 8257544 | tf_op jit(solution)/shard_map/ppermute | solution.py:59
  94.5 2.4 %copy-start = (bf16[1,1792,512]{2,1,0:T(8,128)(2,1)}, bf16[1,1792,512]{2,1,0:T(8,128)(2,1)S(1)}, u32[]{:S(2)}) copy-start(bf16[1,1792,512]{2,1,0:T(8,128)(2,1)S(1)} %get-tuple-element.7) | copy-start | bytes 5505028
  97.0 18.1 %collective-permute-start.2 = (bf16[2,1792,512]{2,1,0:T(8,128)(2,1)}, bf16[2,1792,512]{2,1,0:T(8,128)(2,1)}, u32[]{:S(2)}, u32[]{:S(2)}) collective-permute-start(bf16[2,1792,512]{2,1,0:T(8,128)(2,1)} %pad_maximum_fusion), channel_id=1, source_target_pairs={{0,1},{1,0},{2,3},{3,2},{4,5},{5,4},{6,7},{7,6},{8,9},{9,8},{10,11... | collective-permute-start | bytes 11010056 | tf_op jit(solution)/shard_map/ppermute | solution.py:34
  97.5 3.0 %copy-start.3 = (bf16[1,3584,512]{2,1,0:T(8,128)(2,1)S(1)}, bf16[1,3584,512]{2,1,0:T(8,128)(2,1)}, u32[]{:S(2)}) copy-start(bf16[1,3584,512]{2,1,0:T(8,128)(2,1)} %param.12) | copy-start | bytes 11010052
  100.5 2.4 %copy-start.4 = (bf16[384,3584]{1,0:T(8,128)(2,1)S(1)}, bf16[384,3584]{1,0:T(8,128)(2,1)}, u32[]{:S(2)}) copy-start(bf16[384,3584]{1,0:T(8,128)(2,1)} %reshape.78) | copy-start | bytes 8257540
  102.8 2.6 %copy-start.1 = (bf16[1,1792,512]{2,1,0:T(8,128)(2,1)S(1)}, bf16[1,1792,512]{2,1,0:T(8,128)(2,1)}, u32[]{:S(2)}) copy-start(bf16[1,1792,512]{2,1,0:T(8,128)(2,1)} %copy-done) | copy-start | bytes 5505028
  105.4 2.5 %copy-start.5 = (bf16[1,512,3584]{2,1,0:T(8,128)(2,1)S(1)}, bf16[1,512,3584]{2,1,0:T(8,128)(2,1)}, u32[]{:S(2)}) copy-start(bf16[1,512,3584]{2,1,0:T(8,128)(2,1)} %param.13) | copy-start | bytes 11010052
  110.2 2.9 %copy-start.2 = (bf16[1,3584,512]{2,1,0:T(8,128)(2,1)S(1)}, bf16[1,3584,512]{2,1,0:T(8,128)(2,1)}, u32[]{:S(2)}) copy-start(bf16[1,3584,512]{2,1,0:T(8,128)(2,1)} %param.11) | copy-start | bytes 11010052
  112.9 2.6 %collective-permute-start.1 = (bf16[384,1024]{1,0:T(8,128)(2,1)S(1)}, bf16[384,1024]{1,0:T(8,128)(2,1)S(1)}, u32[]{:S(2)}, u32[]{:S(2)}) collective-permute-start(bf16[384,1024]{1,0:T(8,128)(2,1)S(1)} %pad_maximum_fusion.1), channel_id=1, source_target_pairs={{0,1},{1,0},{2,3},{3,2},{4,5},{5,4},{6,7},{7,6},{8,9},{9,8},{10,11... | collective-permute-start | bytes 2359304 | tf_op jit(solution)/shard_map/ppermute | solution.py:80
  120.3 10.3 %copy-start.6 = (bf16[128,2]{0,1:T(2,128)(2,1)S(1)}, bf16[128,2]{0,1:T(2,128)(2,1)}, u32[]{:S(2)}) copy-start(bf16[128,2]{0,1:T(2,128)(2,1)} %param.10) | copy-start | bytes 1540
  123.4 45.9 %all-to-all-start.1 = ((bf16[128,4,1344]{2,1,0:T(4,128)(2,1)}), bf16[128,4,1344]{2,1,0:T(4,128)(2,1)S(1)}, u32[]{:S(2)}, u32[]{:S(2)}) async-start(bf16[128,4,1344]{2,1,0:T(4,128)(2,1)} %reshape.79), calls=%async_computation.1 | async-start | bytes 2883584 | tf_op jit(solution)/shard_map/all_to_all | solution.py:94

commit v8 on v3

--- a/solution.py
+++ b/solution.py
@@ -4,12 +4,12 @@
 from jax.sharding import PartitionSpec as P
 
 
-def fold_rows(rows, experts, lanes):
+def fold_rows(rows, experts):
     per_expert = rows.size // experts
     return rows.reshape(experts, 4, per_expert // 4)
 
 
-def per_device(features, cotangent, expert_ids, route_weight, gate_weight, up_weight, down_weight):
+def device_body(features, cotangent, expert_ids, route_weight, gate_weight, up_weight, down_weight):
     experts = lax.axis_size("expert")
     parts = lax.axis_size("tensor")
     me = lax.axis_index("tensor")
@@ -51,7 +51,7 @@
     packed = lax.dot_general(
         token_slot, token_rows, (((0,), (0,)), ((), ())), preferred_element_type=jnp.float32
     ).astype(jnp.bfloat16)
-    row_part = fold_rows(packed, experts, 128)
+    row_part = fold_rows(packed, experts)
     weight4 = jnp.pad(slot_weight.reshape(experts, capacity), ((0, 0), (0, 4 - capacity)))
     lane = jnp.arange(128, dtype=jnp.int32)[None, None, :]
     weight_part = jnp.where(lane == 0, weight4[:, :, None], jnp.zeros((), jnp.bfloat16))
@@ -95,7 +95,7 @@
         + back(got_grad[:, :ffh], got_w[0])
         + back(got_grad[:, ffh:], got_w[1])
     )
-    outgoing_back = fold_rows(share.astype(jnp.bfloat16), experts, 128)
+    outgoing_back = fold_rows(share.astype(jnp.bfloat16), experts)
     returned = lax.all_to_all(outgoing_back, "expert", split_axis=0, concat_axis=0, tiled=True)
     summed = jnp.dot(
         token_slot, returned.reshape(total, half), preferred_element_type=jnp.float32
@@ -115,5 +115,5 @@
     )
     out_specs = P("expert", "tensor")
     return jax.shard_map(
-        per_device, mesh=mesh, in_specs=in_specs, out_specs=out_specs, check_vma=False
+        device_body, mesh=mesh, in_specs=in_specs, out_specs=out_specs, check_vma=False
     )

time: 185 us -> 185 us (level)
  no operation moved by 1% of the time
where the time goes in v8:
time: 185 us; the launch traced here: 184 us
  blocking collectives  130 us (70%)
  matrix products  25.1 us (14%)
  local copies, waits for them, and re-layouts  20.7 us (11%)
  other arithmetic  7.46 us (4%)
    all_to_all x1, blocking collectives, device_body(): lax.all_to_all(outgoing, 'expert', split_axis=0, concat_axis=0, tiled=True)  84.2 us
    all_to_all x1, blocking collectives, device_body(): lax.all_to_all(outgoing_back, 'expert', split_axis=0, concat_axis=0, tile...  45.7 us
    dot_general x4, matrix products, fwd(): return jnp.dot(rows, weight, preferred_element_type=jnp.float32)  10.2 us
    dot_general x4, matrix products, back(): lax.dot_general(grad, weight, (((1,), (1,)), ((), ())), preferred_element...  6.68 us
    reshape x2, local copies, waits for them, and re-layouts, fold_rows(): return rows.reshape(experts, 4, per_expert // 4)  5.19 us
    dot_general x2, matrix products, fwd_t(): lax.dot_general(rows, weight, (((1,), (1,)), ((), ())), preferred_element...  5.02 us
    reshape x1, local copies, waits for them, and re-layouts, device_body(): own_rows = received[:, :, :fold].reshape(total, 2 * half)  4.82 us
  transfers between devices with their start and end apart: 3, of which 1 were waited for; matrix products, arithmetic and copies ran while one was open for 12% of the time, Pallas kernels for 0%

profile of v8, /device:TPU:32, one launch (start us, length us, event | category | flops | bytes accessed | tf_op | source)
XLA Modules:
  0.0 184.4 jit_solution(13604582449897069145)
XLA Ops:
  0.0 0.8 copy.44
  4.1 2.1 %convolution_convert_fusion = bf16[384,3584]{1,0:T(8,128)(2,1)S(1)} fusion(bf16[128,1792]{1,0:T(8,128)(2,1)} %param.8, bf16[128,1792]{1,0:T(8,128)(2,1)} %param.7, s32[128,384]{1,0:T(8,128)S(1)} %convert_reduce_fusion), kind=kOutput, calls=%fused_computation | convolution fusion | flops 355581952 | bytes 3866624 | tf_op jit(solution)/shard_map/dot_general | solution.py:51
  6.1 2.9 %reshape.83 = bf16[128,4,2688]{2,1,0:T(4,128)(2,1)} reshape(bf16[384,3584]{1,0:T(8,128)(2,1)S(1)} %convolution_convert_fusion) | data formatting | bytes 5505024 | tf_op jit(solution)/shard_map/reshape | solution.py:9
  9.3 3.1 %pad_maximum_fusion.1 = bf16[128,4,2816]{2,1,0:T(4,128)(2,1)S(1)} fusion(bf16[128,4,128]{2,1,0:T(4,128)(2,1)S(1)} %broadcast_select_fusion, bf16[128,4,2688]{2,1,0:T(4,128)(2,1)} %reshape.83), kind=kLoop, calls=%fused_computation.5 | loop fusion | flops 5767168 | bytes 5767168 | tf_op jit(solution)/shard_map/concatenate | solution.py:58
  12.4 84.2 %all_to_all.10 = bf16[128,4,2816]{2,1,0:T(4,128)(2,1)S(1)} all-to-all(bf16[128,4,2816]{2,1,0:T(4,128)(2,1)S(1)} %pad_maximum_fusion.1), channel_id=1, replica_groups=mesh['expert'=128,'tensor'=2] {'expert'}, dimensions={0} | all-to-all | bytes 5767168 | tf_op jit(solution)/shard_map/all_to_all | solution.py:60
  96.5 2.5 %slice.51 = bf16[128,4,2688]{2,1,0:T(4,128)(2,1)} slice(bf16[128,4,2816]{2,1,0:T(4,128)(2,1)S(1)} %all_to_all.10), slice={[0:128], [0:4], [0:2688]} | slice | bytes 5505024 | tf_op jit(solution)/shard_map/slice | solution.py:62
  99.0 4.8 %reshape.84 = bf16[384,3584]{1,0:T(8,128)(2,1)} reshape(bf16[128,4,2688]{2,1,0:T(4,128)(2,1)} %slice.51) | data formatting | bytes 5505024 | tf_op jit(solution)/shard_map/reshape | solution.py:62
  103.9 1.8 constant_dynamic-slice_fusion
  105.6 0.8 copy-done.5
  106.6 2.4 %pad_maximum_fusion = bf16[2,1792,512]{2,1,0:T(8,128)(2,1)} fusion(bf16[1,1792,512]{2,1,0:T(8,128)(2,1)S(1)} %constant_dynamic-slice_fusion.1, bf16[1,1792,512]{2,1,0:T(8,128)(2,1)S(1)} %constant_dynamic-slice_fusion), kind=kLoop, calls=%fused_computation.1 | loop fusion | flops 1835008 | bytes 7340032 | tf_op jit(solution)/shard_map/stack | solution.py:28
  110.4 2.9 %fusion.7 = f32[384,512]{1,0:T(8,128)S(1)} fusion(bf16[1,3584,512]{2,1,0:T(8,128)(2,1)} %param.11, s32[]{:T(128)S(6)} %select_n.29, bf16[384,3584]{1,0:T(8,128)(2,1)} %reshape.84), kind=kOutput, calls=%fused_computation.15 | convolution fusion | flops 704643072 | bytes 3997700 | tf_op jit(solution)/shard_map/dot_general | solution.py:69
  113.4 2.4 %fusion.12 = f32[384,512]{1,0:T(8,128)S(1)} fusion(bf16[1,3584,512]{2,1,0:T(8,128)(2,1)S(1)} %copy-done.6, s32[]{:T(128)S(6)} %select_n.29, bf16[384,3584]{1,0:T(8,128)(2,1)} %reshape.84), kind=kOutput, calls=%fused_computation.20 | convolution fusion | flops 704643072 | bytes 3997700 | tf_op jit(solution)/shard_map/dot_general | solution.py:69
  115.7 2.5 %fusion.16 = f32[384,512]{1,0:T(8,128)S(1)} fusion(bf16[1,512,3584]{2,1,0:T(8,128)(2,1)} %param.13, s32[]{:T(128)S(6)} %select_n.29, bf16[384,3584]{1,0:T(8,128)(2,1)S(1)} %copy-done.7), kind=kOutput, calls=%fused_computation.24 | convolution fusion | flops 704643072 | bytes 3997700 | tf_op jit(solution)/shard_map/dot_general | solution.py:72
  118.3 2.4 %fusion.43 = f32[384,512]{1,0:T(8,128)S(1)} fusion(f32[384,512]{1,0:T(8,128)S(1)} %fusion.7, bf16[1,1792,512]{2,1,0:T(8,128)(2,1)S(1)} %copy-done.3, bf16[384,3584]{1,0:T(8,128)(2,1)} %collective-permute-done), kind=kOutput, calls=%fused_computation.39 | convolution fusion | flops 704839680 | bytes 4784128 | tf_op jit(solution)/shard_map/dot_general | solution.py:69
  120.7 2.5 %multiply_convert_fusion = (bf16[384,512]{1,0:T(8,128)(2,1)S(1)}, f32[384,512]{1,0:T(8,128)S(1)}) fusion(f32[384,512]{1,0:T(8,128)S(1)} %fusion.43, f32[384]{0:T(512)S(1)} %reshape.88, f32[384,512]{1,0:T(8,128)S(1)} %fusion.16, bf16[1,512,3584]{2,1,0:T(8,128)(2,1)S(1)} %copy-done.8, s32[]{:T(128)S(6)} %select_n.31, bf16[384,3584]{1,0:T(8,128)(2,1)} %collective-permute-done), kind=kOutput, calls=%fused_computation.50 | convolution fusion | flops 706215936 | bytes 5965828 | tf_op jit(solution)/shard_map/dot_general | solution.py:72
  123.3 2.6 %fusion.51 = bf16[384,512]{1,0:T(8,128)(2,1)S(1)} fusion(f32[384,512]{1,0:T(8,128)S(1)} %get-tuple-element.6, f32[384,512]{1,0:T(8,128)S(1)} %fusion.12, bf16[1,1792,512]{2,1,0:T(8,128)(2,1)S(1)} %copy-done.1, bf16[384,3584]{1,0:T(8,128)(2,1)} %collective-permute-done, f32[384,512]{1,0:T(8,128)S(1)} %fusion.43), kind=kOutput, calls=%fused_computation.41 | convolution fusion | flops 706805760 | bytes 5963776 | tf_op jit(solution)/shard_map/dot_general | solution.py:69
  126.0 0.9 fusion.5
  127.0 0.9 convolution_add_fusion.1
  128.3 2.4 %fusion.2 = f32[384,1792]{1,0:T(8,128)S(1)} fusion(bf16[2,1792,512]{2,1,0:T(8,128)(2,1)} %collective-permute-done.2, bf16[384,1024]{1,0:T(8,128)(2,1)S(1)} %collective-permute-done.1), kind=kOutput, calls=%fused_computation.9 | convolution fusion | flops 704643072 | bytes 4980736 | tf_op jit(solution)/shard_map/dot_general | solution.py:88
  130.7 2.4 %fusion.1 = bf16[384,1792]{1,0:T(8,128)(2,1)S(1)} fusion(f32[384,1792]{1,0:T(8,128)S(1)} %fusion.2, f32[384,1792]{1,0:T(8,128)S(1)} %convolution_add_fusion.1, bf16[2,1792,512]{2,1,0:T(8,128)(2,1)} %collective-permute-done.2, bf16[384,1024]{1,0:T(8,128)(2,1)S(1)} %collective-permute-done.1), kind=kOutput, calls=%fused_computation.6 | convolution fusion | flops 706707456 | bytes 9109504 | tf_op jit(solution)/shard_map/dot_general | solution.py:88
  133.1 2.3 %reshape.85 = bf16[128,4,1344]{2,1,0:T(4,128)(2,1)S(1)} reshape(bf16[384,1792]{1,0:T(8,128)(2,1)S(1)} %fusion.1) | data formatting | bytes 2752512 | tf_op jit(solution)/shard_map/reshape | solution.py:9
  135.4 45.7 %all_to_all.11 = bf16[128,4,1344]{2,1,0:T(4,128)(2,1)S(1)} all-to-all(bf16[128,4,1344]{2,1,0:T(4,128)(2,1)S(1)} %reshape.85), channel_id=1, replica_groups=mesh['expert'=128,'tensor'=2] {'expert'}, dimensions={0} | all-to-all | bytes 2752512 | tf_op jit(solution)/shard_map/all_to_all | solution.py:99
  181.0 2.2 %reshape.86 = bf16[384,1792]{1,0:T(8,128)(2,1)S(1)} reshape(bf16[128,4,1344]{2,1,0:T(4,128)(2,1)S(1)} %all_to_all.11) | data formatting | bytes 2752512 | tf_op jit(solution)/shard_map/reshape | solution.py:101
  183.2 1.2 convolution_convert_fusion.1
  (49 shorter events, 5.6 us)
Async XLA Ops:
  103.9 14.4 %collective-permute-start = (bf16[384,3584]{1,0:T(8,128)(2,1)}, bf16[384,3584]{1,0:T(8,128)(2,1)}, u32[]{:S(2)}, u32[]{:S(2)}) collective-permute-start(bf16[384,3584]{1,0:T(8,128)(2,1)} %reshape.84), channel_id=1, source_target_pairs={{0,1},{1,0},{2,3},{3,2},{4,5},{5,4},{6,7},{7,6},{8,9},{9,8},{10,11... | collective-permute-start | bytes 8257544 | tf_op jit(solution)/shard_map/ppermute | solution.py:63
  103.9 2.6 %copy-start.5 = (bf16[1,3584,512]{2,1,0:T(8,128)(2,1)S(1)}, bf16[1,3584,512]{2,1,0:T(8,128)(2,1)}, u32[]{:S(2)}) copy-start(bf16[1,3584,512]{2,1,0:T(8,128)(2,1)} %param.12) | copy-start | bytes 11010052
  106.4 2.5 %copy-start.2 = (bf16[1,1792,512]{2,1,0:T(8,128)(2,1)}, bf16[1,1792,512]{2,1,0:T(8,128)(2,1)S(1)}, u32[]{:S(2)}) copy-start(bf16[1,1792,512]{2,1,0:T(8,128)(2,1)S(1)} %constant_dynamic-slice_fusion) | copy-start | bytes 5505028
  106.6 2.8 %copy-start = (bf16[1,1792,512]{2,1,0:T(8,128)(2,1)}, bf16[1,1792,512]{2,1,0:T(8,128)(2,1)S(1)}, u32[]{:S(2)}) copy-start(bf16[1,1792,512]{2,1,0:T(8,128)(2,1)S(1)} %constant_dynamic-slice_fusion.1) | copy-start | bytes 5505028
  109.4 18.5 %collective-permute-start.2 = (bf16[2,1792,512]{2,1,0:T(8,128)(2,1)}, bf16[2,1792,512]{2,1,0:T(8,128)(2,1)}, u32[]{:S(2)}, u32[]{:S(2)}) collective-permute-start(bf16[2,1792,512]{2,1,0:T(8,128)(2,1)} %pad_maximum_fusion), channel_id=1, source_target_pairs={{0,1},{1,0},{2,3},{3,2},{4,5},{5,4},{6,7},{7,6},{8,9},{9,8},{10,11... | collective-permute-start | bytes 11010056 | tf_op jit(solution)/shard_map/ppermute | solution.py:34
  110.3 3.0 %copy-start.6 = (bf16[1,3584,512]{2,1,0:T(8,128)(2,1)S(1)}, bf16[1,3584,512]{2,1,0:T(8,128)(2,1)}, u32[]{:S(2)}) copy-start(bf16[1,3584,512]{2,1,0:T(8,128)(2,1)} %param.12) | copy-start | bytes 11010052
  113.4 2.4 %copy-start.7 = (bf16[384,3584]{1,0:T(8,128)(2,1)S(1)}, bf16[384,3584]{1,0:T(8,128)(2,1)}, u32[]{:S(2)}) copy-start(bf16[384,3584]{1,0:T(8,128)(2,1)} %reshape.84) | copy-start | bytes 8257540
  115.7 2.6 %copy-start.3 = (bf16[1,1792,512]{2,1,0:T(8,128)(2,1)S(1)}, bf16[1,1792,512]{2,1,0:T(8,128)(2,1)}, u32[]{:S(2)}) copy-start(bf16[1,1792,512]{2,1,0:T(8,128)(2,1)} %copy-done.2) | copy-start | bytes 5505028
  118.3 2.5 %copy-start.8 = (bf16[1,512,3584]{2,1,0:T(8,128)(2,1)S(1)}, bf16[1,512,3584]{2,1,0:T(8,128)(2,1)}, u32[]{:S(2)}) copy-start(bf16[1,512,3584]{2,1,0:T(8,128)(2,1)} %param.13) | copy-start | bytes 11010052
  120.7 2.5 %copy-start.1 = (bf16[1,1792,512]{2,1,0:T(8,128)(2,1)S(1)}, bf16[1,1792,512]{2,1,0:T(8,128)(2,1)}, u32[]{:S(2)}) copy-start(bf16[1,1792,512]{2,1,0:T(8,128)(2,1)} %copy-done) | copy-start | bytes 5505028
  123.2 2.8 %copy-start.4 = (bf16[1,3584,512]{2,1,0:T(8,128)(2,1)S(1)}, bf16[1,3584,512]{2,1,0:T(8,128)(2,1)}, u32[]{:S(2)}) copy-start(bf16[1,3584,512]{2,1,0:T(8,128)(2,1)} %param.11) | copy-start | bytes 11010052
  125.9 2.4 %collective-permute-start.1 = (bf16[384,1024]{1,0:T(8,128)(2,1)S(1)}, bf16[384,1024]{1,0:T(8,128)(2,1)S(1)}, u32[]{:S(2)}, u32[]{:S(2)}) collective-permute-start(bf16[384,1024]{1,0:T(8,128)(2,1)S(1)} %pad_maximum_fusion.2), channel_id=1, source_target_pairs={{0,1},{1,0},{2,3},{3,2},{4,5},{5,4},{6,7},{7,6},{8,9},{9,8},{10,11... | collective-permute-start | bytes 2359304 | tf_op jit(solution)/shard_map/ppermute | solution.py:85

commit v9 on v7

--- a/solution.py
+++ b/solution.py
@@ -4,9 +4,9 @@
 from jax.sharding import PartitionSpec as P
 
 
-def fold_rows(rows, experts):
+def fold_rows(rows, experts, folds):
     per_expert = rows.size // experts
-    return rows.reshape(experts, 4, per_expert // 4)
+    return rows.reshape(experts, folds, per_expert // folds)
 
 
 def device_body(features, cotangent, expert_ids, route_weight, gate_weight, up_weight, down_weight):
@@ -53,7 +53,7 @@
         token_slot, token_rows, (((0,), (0,)), ((), ())), preferred_element_type=jnp.float32
     ).astype(jnp.bfloat16)
     received = lax.all_to_all(
-        fold_rows(packed, experts), "expert", split_axis=0, concat_axis=0, tiled=True
+        fold_rows(packed, experts, 4), "expert", split_axis=0, concat_axis=0, tiled=True
     )
     own_rows = received.reshape(total, 2 * half)
     got_rows = lax.ppermute(own_rows, "tensor", swap)
@@ -90,7 +90,7 @@
         + back(got_grad[:, :ffh], got_w[0])
         + back(got_grad[:, ffh:], got_w[1])
     )
-    outgoing_back = fold_rows(share.astype(jnp.bfloat16), experts)
+    outgoing_back = fold_rows(share.astype(jnp.bfloat16), experts, 2)
     returned = lax.all_to_all(outgoing_back, "expert", split_axis=0, concat_axis=0, tiled=True)
     summed = jnp.dot(
         route_weight_slot, returned.reshape(total, half), preferred_element_type=jnp.float32

time: 173 us -> 169 us (0.977)
  local copies, waits for them, and re-layouts: 15.1 us -> 12.5 us
where the time goes in v9:
time: 169 us
  blocking collectives  81.5 us (48%)
  waiting for transfers between devices  37.6 us (22%)
  matrix products  25 us (15%)
  local copies, waits for them, and re-layouts  12.5 us (7%)
  starting transfers between devices  7.93 us (5%)
  other arithmetic  3.86 us (2%)
    all_to_all x1, blocking collectives, device_body(): lax.all_to_all(fold_rows(packed, experts, 4), 'expert', split_axis=0, con...  81.5 us
    all_to_all x1, waiting for transfers between devices, device_body(): lax.all_to_all(outgoing_back, 'expert', split_axis=0, concat_axis=0, tile...  37.2 us
    dot_general x4, matrix products, fwd(): return jnp.dot(rows, weight, preferred_element_type=jnp.float32)  10.2 us
    all_to_all x1, starting transfers between devices, device_body(): lax.all_to_all(outgoing_back, 'expert', split_axis=0, concat_axis=0, tile...  7.15 us
    dot_general x4, matrix products, back(): lax.dot_general(grad, weight, (((1,), (1,)), ((), ())), preferred_element...  6.68 us
    dot_general x2, matrix products, fwd_t(): lax.dot_general(rows, weight, (((1,), (1,)), ((), ())), preferred_element...  4.87 us
    reshape x2, local copies, waits for them, and re-layouts, fold_rows(): return rows.reshape(experts, folds, per_expert // folds)  4.69 us
  transfers between devices with their start and end apart: 4, of which 2 were waited for; matrix products, arithmetic and copies ran while one was open for 13% of the time, Pallas kernels for 0%

profile of v9, /device:TPU:32, one launch (start us, length us, event | category | flops | bytes accessed | tf_op | source)
XLA Modules:
  0.0 168.6 jit_solution(7160367552485355930)
XLA Ops:
  0.0 0.8 copy.24
  1.9 0.7 multiply_add_fusion
  2.7 2.1 %convolution_convert_fusion = bf16[384,3584]{1,0:T(8,128)(2,1)S(1)} fusion(bf16[128,1792]{1,0:T(8,128)(2,1)} %param.8, bf16[128,1792]{1,0:T(8,128)(2,1)} %param.7, s32[128,384]{1,0:T(8,128)S(1)} %convert_reduce_fusion), kind=kOutput, calls=%fused_computation | convolution fusion | flops 355581952 | bytes 3866624 | tf_op jit(solution)/shard_map/dot_general | solution.py:52
  4.8 2.9 %reshape.77 = bf16[128,4,2688]{2,1,0:T(4,128)(2,1)} reshape(bf16[384,3584]{1,0:T(8,128)(2,1)S(1)} %convolution_convert_fusion) | data formatting | bytes 5505024 | tf_op jit(solution)/shard_map/reshape | solution.py:9
  7.7 81.5 %all_to_all.10 = bf16[128,4,2688]{2,1,0:T(4,128)(2,1)S(1)} all-to-all(bf16[128,4,2688]{2,1,0:T(4,128)(2,1)} %reshape.77), channel_id=1, replica_groups=mesh['expert'=128,'tensor'=2] {'expert'}, dimensions={0} | all-to-all | bytes 5505024 | tf_op jit(solution)/shard_map/all_to_all | solution.py:55
  89.2 3.0 %reshape.78 = bf16[384,3584]{1,0:T(8,128)(2,1)} reshape(bf16[128,4,2688]{2,1,0:T(4,128)(2,1)S(1)} %all_to_all.10) | data formatting | bytes 5505024 | tf_op jit(solution)/shard_map/reshape | solution.py:58
  92.3 2.3 %constant_dynamic-slice_fusion = (bf16[1,1792,512]{2,1,0:T(8,128)(2,1)S(1)}, bf16[1,1792,512]{2,1,0:T(8,128)(2,1)S(1)}) fusion(bf16[1,3584,512]{2,1,0:T(8,128)(2,1)} %param.11, s32[]{:T(128)S(6)} %select_n.27, bf16[1,3584,512]{2,1,0:T(8,128)(2,1)} %param.12), kind=kLoop, calls=%fused_computation.66 | loop fusion | bytes 7340036 | tf_op jit(solution)/shard_map/dynamic_slice | solution.py:30
  94.6 2.3 %pad_maximum_fusion = bf16[2,1792,512]{2,1,0:T(8,128)(2,1)} fusion(bf16[1,1792,512]{2,1,0:T(8,128)(2,1)S(1)} %get-tuple-element.8, bf16[1,1792,512]{2,1,0:T(8,128)(2,1)S(1)} %get-tuple-element.7), kind=kLoop, calls=%fused_computation.1 | loop fusion | flops 1835008 | bytes 7340032 | tf_op jit(solution)/shard_map/stack | solution.py:28
  97.0 0.5 collective-permute-start.2
  97.5 2.9 %fusion.7 = f32[384,512]{1,0:T(8,128)S(1)} fusion(bf16[1,3584,512]{2,1,0:T(8,128)(2,1)} %param.11, s32[]{:T(128)S(6)} %select_n.25, bf16[384,3584]{1,0:T(8,128)(2,1)} %reshape.78), kind=kOutput, calls=%fused_computation.14 | convolution fusion | flops 704643072 | bytes 3997700 | tf_op jit(solution)/shard_map/dot_general | solution.py:65
  100.5 2.4 %fusion.12 = f32[384,512]{1,0:T(8,128)S(1)} fusion(bf16[1,3584,512]{2,1,0:T(8,128)(2,1)S(1)} %copy-done.3, s32[]{:T(128)S(6)} %select_n.25, bf16[384,3584]{1,0:T(8,128)(2,1)} %reshape.78), kind=kOutput, calls=%fused_computation.19 | convolution fusion | flops 704643072 | bytes 3997700 | tf_op jit(solution)/shard_map/dot_general | solution.py:65
  102.9 2.5 %fusion.16 = f32[384,512]{1,0:T(8,128)S(1)} fusion(bf16[1,512,3584]{2,1,0:T(8,128)(2,1)} %param.13, s32[]{:T(128)S(6)} %select_n.25, bf16[384,3584]{1,0:T(8,128)(2,1)S(1)} %copy-done.4), kind=kOutput, calls=%fused_computation.23 | convolution fusion | flops 704643072 | bytes 3997700 | tf_op jit(solution)/shard_map/dot_general | solution.py:68
  105.4 2.4 %fusion.43 = f32[384,512]{1,0:T(8,128)S(1)} fusion(f32[384,512]{1,0:T(8,128)S(1)} %fusion.7, bf16[1,1792,512]{2,1,0:T(8,128)(2,1)S(1)} %copy-done.1, bf16[384,3584]{1,0:T(8,128)(2,1)} %collective-permute-done), kind=kOutput, calls=%fused_computation.38 | convolution fusion | flops 704839680 | bytes 4784128 | tf_op jit(solution)/shard_map/dot_general | solution.py:65
  107.9 2.3 %multiply_convert_fusion = (bf16[384,512]{1,0:T(8,128)(2,1)S(1)}, f32[384,512]{1,0:T(8,128)S(1)}) fusion(f32[384,512]{1,0:T(8,128)S(1)} %fusion.43, f32[384,512]{1,0:T(8,128)S(1)} %fusion.16, bf16[1,512,3584]{2,1,0:T(8,128)(2,1)S(1)} %copy-done.5, s32[]{:T(128)S(6)} %select_n.27, bf16[384,3584]{1,0:T(8,128)(2,1)} %collective-permute-done), kind=kOutput, calls=%fused_computation.48 | convolution fusion | flops 706019328 | bytes 5963780 | tf_op jit(solution)/shard_map/dot_general | solution.py:68
  110.2 2.5 %fusion.46 = bf16[384,512]{1,0:T(8,128)(2,1)S(1)} fusion(f32[384,512]{1,0:T(8,128)S(1)} %get-tuple-element.6, f32[384,512]{1,0:T(8,128)S(1)} %fusion.12, bf16[1,1792,512]{2,1,0:T(8,128)(2,1)S(1)} %get-tuple-element.8, bf16[384,3584]{1,0:T(8,128)(2,1)} %collective-permute-done, f32[384,512]{1,0:T(8,128)S(1)} %fusion.43), kind=kOutput, calls=%fused_computation.39 | convolution fusion | flops 706805760 | bytes 5963776 | tf_op jit(solution)/shard_map/dot_general | solution.py:65
  113.2 0.9 fusion.5
  114.1 0.9 convolution_add_fusion.1
  115.4 2.4 %fusion.2 = f32[384,1792]{1,0:T(8,128)S(1)} fusion(bf16[2,1792,512]{2,1,0:T(8,128)(2,1)} %collective-permute-done.2, bf16[384,1024]{1,0:T(8,128)(2,1)S(1)} %collective-permute-done.1), kind=kOutput, calls=%fused_computation.8 | convolution fusion | flops 704643072 | bytes 4980736 | tf_op jit(solution)/shard_map/dot_general | solution.py:83
  117.8 2.4 %fusion.1 = bf16[384,1792]{1,0:T(8,128)(2,1)S(1)} fusion(f32[384,1792]{1,0:T(8,128)S(1)} %fusion.2, f32[384,1792]{1,0:T(8,128)S(1)} %convolution_add_fusion.1, bf16[2,1792,512]{2,1,0:T(8,128)(2,1)} %collective-permute-done.2, bf16[384,1024]{1,0:T(8,128)(2,1)S(1)} %collective-permute-done.1), kind=kOutput, calls=%fused_computation.5 | convolution fusion | flops 706707456 | bytes 9109504 | tf_op jit(solution)/shard_map/dot_general | solution.py:83
  120.3 1.8 %reshape.79 = bf16[128,2,2688]{2,1,0:T(2,128)(2,1)} reshape(bf16[384,1792]{1,0:T(8,128)(2,1)S(1)} %fusion.1) | data formatting | bytes 2752512 | tf_op jit(solution)/shard_map/reshape | solution.py:9
  122.0 7.2 %all-to-all-start.1 = ((bf16[128,2,2688]{2,1,0:T(2,128)(2,1)}), bf16[128,2,2688]{2,1,0:T(2,128)(2,1)S(1)}, u32[]{:S(2)}, u32[]{:S(2)}) async-start(bf16[128,2,2688]{2,1,0:T(2,128)(2,1)} %reshape.79), calls=%async_computation.1 | async-start | bytes 2752512 | tf_op jit(solution)/shard_map/all_to_all | solution.py:94
  129.3 37.2 %all-to-all-done.1 = bf16[128,2,2688]{2,1,0:T(2,128)(2,1)S(1)} async-done(((bf16[128,2,2688]{2,1,0:T(2,128)(2,1)}), bf16[128,2,2688]{2,1,0:T(2,128)(2,1)S(1)}, u32[]{:S(2)}, u32[]{:S(2)}) %all-to-all-start.1) | async-done | bytes 1376288 | tf_op jit(solution)/shard_map/all_to_all | solution.py:94
  166.5 0.9 reshape.80
  167.4 1.2 convolution_convert_fusion.1
  (35 shorter events, 2.3 us)
Async XLA Ops:
  92.3 13.2 %collective-permute-start = (bf16[384,3584]{1,0:T(8,128)(2,1)}, bf16[384,3584]{1,0:T(8,128)(2,1)}, u32[]{:S(2)}, u32[]{:S(2)}) collective-permute-start(bf16[384,3584]{1,0:T(8,128)(2,1)} %reshape.78), channel_id=1, source_target_pairs={{0,1},{1,0},{2,3},{3,2},{4,5},{5,4},{6,7},{7,6},{8,9},{9,8},{10,11... | collective-permute-start | bytes 8257544 | tf_op jit(solution)/shard_map/ppermute | solution.py:59
  94.5 2.4 %copy-start = (bf16[1,1792,512]{2,1,0:T(8,128)(2,1)}, bf16[1,1792,512]{2,1,0:T(8,128)(2,1)S(1)}, u32[]{:S(2)}) copy-start(bf16[1,1792,512]{2,1,0:T(8,128)(2,1)S(1)} %get-tuple-element.7) | copy-start | bytes 5505028
  97.0 18.1 %collective-permute-start.2 = (bf16[2,1792,512]{2,1,0:T(8,128)(2,1)}, bf16[2,1792,512]{2,1,0:T(8,128)(2,1)}, u32[]{:S(2)}, u32[]{:S(2)}) collective-permute-start(bf16[2,1792,512]{2,1,0:T(8,128)(2,1)} %pad_maximum_fusion), channel_id=1, source_target_pairs={{0,1},{1,0},{2,3},{3,2},{4,5},{5,4},{6,7},{7,6},{8,9},{9,8},{10,11... | collective-permute-start | bytes 11010056 | tf_op jit(solution)/shard_map/ppermute | solution.py:34
  97.5 3.0 %copy-start.3 = (bf16[1,3584,512]{2,1,0:T(8,128)(2,1)S(1)}, bf16[1,3584,512]{2,1,0:T(8,128)(2,1)}, u32[]{:S(2)}) copy-start(bf16[1,3584,512]{2,1,0:T(8,128)(2,1)} %param.12) | copy-start | bytes 11010052
  100.5 2.4 %copy-start.4 = (bf16[384,3584]{1,0:T(8,128)(2,1)S(1)}, bf16[384,3584]{1,0:T(8,128)(2,1)}, u32[]{:S(2)}) copy-start(bf16[384,3584]{1,0:T(8,128)(2,1)} %reshape.78) | copy-start | bytes 8257540
  102.8 2.6 %copy-start.1 = (bf16[1,1792,512]{2,1,0:T(8,128)(2,1)S(1)}, bf16[1,1792,512]{2,1,0:T(8,128)(2,1)}, u32[]{:S(2)}) copy-start(bf16[1,1792,512]{2,1,0:T(8,128)(2,1)} %copy-done) | copy-start | bytes 5505028
  105.4 2.5 %copy-start.5 = (bf16[1,512,3584]{2,1,0:T(8,128)(2,1)S(1)}, bf16[1,512,3584]{2,1,0:T(8,128)(2,1)}, u32[]{:S(2)}) copy-start(bf16[1,512,3584]{2,1,0:T(8,128)(2,1)} %param.13) | copy-start | bytes 11010052
  110.2 2.9 %copy-start.2 = (bf16[1,3584,512]{2,1,0:T(8,128)(2,1)S(1)}, bf16[1,3584,512]{2,1,0:T(8,128)(2,1)}, u32[]{:S(2)}) copy-start(bf16[1,3584,512]{2,1,0:T(8,128)(2,1)} %param.11) | copy-start | bytes 11010052
  112.9 2.6 %collective-permute-start.1 = (bf16[384,1024]{1,0:T(8,128)(2,1)S(1)}, bf16[384,1024]{1,0:T(8,128)(2,1)S(1)}, u32[]{:S(2)}, u32[]{:S(2)}) collective-permute-start(bf16[384,1024]{1,0:T(8,128)(2,1)S(1)} %pad_maximum_fusion.1), channel_id=1, source_target_pairs={{0,1},{1,0},{2,3},{3,2},{4,5},{5,4},{6,7},{7,6},{8,9},{9,8},{10,11... | collective-permute-start | bytes 2359304 | tf_op jit(solution)/shard_map/ppermute | solution.py:80
  120.3 8.9 %copy-start.6 = (bf16[128,2]{0,1:T(2,128)(2,1)S(1)}, bf16[128,2]{0,1:T(2,128)(2,1)}, u32[]{:S(2)}) copy-start(bf16[128,2]{0,1:T(2,128)(2,1)} %param.10) | copy-start | bytes 1540
  122.0 44.5 %all-to-all-start.1 = ((bf16[128,2,2688]{2,1,0:T(2,128)(2,1)}), bf16[128,2,2688]{2,1,0:T(2,128)(2,1)S(1)}, u32[]{:S(2)}, u32[]{:S(2)}) async-start(bf16[128,2,2688]{2,1,0:T(2,128)(2,1)} %reshape.79), calls=%async_computation.1 | async-start | bytes 2752512 | tf_op jit(solution)/shard_map/all_to_all | solution.py:94

commit v10 on v8

--- a/solution.py
+++ b/solution.py
@@ -4,9 +4,9 @@
 from jax.sharding import PartitionSpec as P
 
 
-def fold_rows(rows, experts):
+def fold_rows(rows, experts, folds):
     per_expert = rows.size // experts
-    return rows.reshape(experts, 4, per_expert // 4)
+    return rows.reshape(experts, folds, per_expert // folds)
 
 
 def device_body(features, cotangent, expert_ids, route_weight, gate_weight, up_weight, down_weight):
@@ -51,7 +51,7 @@
     packed = lax.dot_general(
         token_slot, token_rows, (((0,), (0,)), ((), ())), preferred_element_type=jnp.float32
     ).astype(jnp.bfloat16)
-    row_part = fold_rows(packed, experts)
+    row_part = fold_rows(packed, experts, 4)
     weight4 = jnp.pad(slot_weight.reshape(experts, capacity), ((0, 0), (0, 4 - capacity)))
     lane = jnp.arange(128, dtype=jnp.int32)[None, None, :]
     weight_part = jnp.where(lane == 0, weight4[:, :, None], jnp.zeros((), jnp.bfloat16))
@@ -95,7 +95,7 @@
         + back(got_grad[:, :ffh], got_w[0])
         + back(got_grad[:, ffh:], got_w[1])
     )
-    outgoing_back = fold_rows(share.astype(jnp.bfloat16), experts)
+    outgoing_back = fold_rows(share.astype(jnp.bfloat16), experts, 2)
     returned = lax.all_to_all(outgoing_back, "expert", split_axis=0, concat_axis=0, tiled=True)
     summed = jnp.dot(
         token_slot, returned.reshape(total, half), preferred_element_type=jnp.float32

time: 185 us -> 184 us (level)
  no operation moved by 1% of the time
where the time goes in v10:
time: 184 us; the launch traced here: 183 us
  blocking collectives  129 us (70%)
  matrix products  25.1 us (14%)
  local copies, waits for them, and re-layouts  20.7 us (11%)
  other arithmetic  7.47 us (4%)
    all_to_all x1, blocking collectives, device_body(): lax.all_to_all(outgoing, 'expert', split_axis=0, concat_axis=0, tiled=True)  84.2 us
    all_to_all x1, blocking collectives, device_body(): lax.all_to_all(outgoing_back, 'expert', split_axis=0, concat_axis=0, tile...  44.4 us
    dot_general x4, matrix products, fwd(): return jnp.dot(rows, weight, preferred_element_type=jnp.float32)  10.2 us
    dot_general x4, matrix products, back(): lax.dot_general(grad, weight, (((1,), (1,)), ((), ())), preferred_element...  6.65 us
    dot_general x2, matrix products, fwd_t(): lax.dot_general(rows, weight, (((1,), (1,)), ((), ())), preferred_element...  5.03 us
    reshape x1, local copies, waits for them, and re-layouts, device_body(): own_rows = received[:, :, :fold].reshape(total, 2 * half)  4.82 us
    reshape x2, local copies, waits for them, and re-layouts, fold_rows(): return rows.reshape(experts, folds, per_expert // folds)  3.85 us
  transfers between devices with their start and end apart: 3, of which 1 were waited for; matrix products, arithmetic and copies ran while one was open for 12% of the time, Pallas kernels for 0%

profile of v10, /device:TPU:32, one launch (start us, length us, event | category | flops | bytes accessed | tf_op | source)
XLA Modules:
  0.0 183.1 jit_solution(6341526111929864262)
XLA Ops:
  0.0 0.8 copy.44
  4.1 2.1 %convolution_convert_fusion = bf16[384,3584]{1,0:T(8,128)(2,1)S(1)} fusion(bf16[128,1792]{1,0:T(8,128)(2,1)} %param.8, bf16[128,1792]{1,0:T(8,128)(2,1)} %param.7, s32[128,384]{1,0:T(8,128)S(1)} %convert_reduce_fusion), kind=kOutput, calls=%fused_computation | convolution fusion | flops 355581952 | bytes 3866624 | tf_op jit(solution)/shard_map/dot_general | solution.py:51
  6.1 2.9 %reshape.83 = bf16[128,4,2688]{2,1,0:T(4,128)(2,1)} reshape(bf16[384,3584]{1,0:T(8,128)(2,1)S(1)} %convolution_convert_fusion) | data formatting | bytes 5505024 | tf_op jit(solution)/shard_map/reshape | solution.py:9
  9.3 3.1 %pad_maximum_fusion.1 = bf16[128,4,2816]{2,1,0:T(4,128)(2,1)S(1)} fusion(bf16[128,4,128]{2,1,0:T(4,128)(2,1)S(1)} %broadcast_select_fusion, bf16[128,4,2688]{2,1,0:T(4,128)(2,1)} %reshape.83), kind=kLoop, calls=%fused_computation.5 | loop fusion | flops 5767168 | bytes 5767168 | tf_op jit(solution)/shard_map/concatenate | solution.py:58
  12.4 84.2 %all_to_all.10 = bf16[128,4,2816]{2,1,0:T(4,128)(2,1)S(1)} all-to-all(bf16[128,4,2816]{2,1,0:T(4,128)(2,1)S(1)} %pad_maximum_fusion.1), channel_id=1, replica_groups=mesh['expert'=128,'tensor'=2] {'expert'}, dimensions={0} | all-to-all | bytes 5767168 | tf_op jit(solution)/shard_map/all_to_all | solution.py:60
  96.5 2.5 %slice.51 = bf16[128,4,2688]{2,1,0:T(4,128)(2,1)} slice(bf16[128,4,2816]{2,1,0:T(4,128)(2,1)S(1)} %all_to_all.10), slice={[0:128], [0:4], [0:2688]} | slice | bytes 5505024 | tf_op jit(solution)/shard_map/slice | solution.py:62
  99.0 4.8 %reshape.84 = bf16[384,3584]{1,0:T(8,128)(2,1)} reshape(bf16[128,4,2688]{2,1,0:T(4,128)(2,1)} %slice.51) | data formatting | bytes 5505024 | tf_op jit(solution)/shard_map/reshape | solution.py:62
  103.9 1.8 constant_dynamic-slice_fusion
  105.6 0.8 copy-done.5
  106.6 2.4 %pad_maximum_fusion = bf16[2,1792,512]{2,1,0:T(8,128)(2,1)} fusion(bf16[1,1792,512]{2,1,0:T(8,128)(2,1)S(1)} %constant_dynamic-slice_fusion.1, bf16[1,1792,512]{2,1,0:T(8,128)(2,1)S(1)} %constant_dynamic-slice_fusion), kind=kLoop, calls=%fused_computation.1 | loop fusion | flops 1835008 | bytes 7340032 | tf_op jit(solution)/shard_map/stack | solution.py:28
  110.4 2.9 %fusion.7 = f32[384,512]{1,0:T(8,128)S(1)} fusion(bf16[1,3584,512]{2,1,0:T(8,128)(2,1)} %param.11, s32[]{:T(128)S(6)} %select_n.29, bf16[384,3584]{1,0:T(8,128)(2,1)} %reshape.84), kind=kOutput, calls=%fused_computation.15 | convolution fusion | flops 704643072 | bytes 3997700 | tf_op jit(solution)/shard_map/dot_general | solution.py:69
  113.4 2.4 %fusion.12 = f32[384,512]{1,0:T(8,128)S(1)} fusion(bf16[1,3584,512]{2,1,0:T(8,128)(2,1)S(1)} %copy-done.6, s32[]{:T(128)S(6)} %select_n.29, bf16[384,3584]{1,0:T(8,128)(2,1)} %reshape.84), kind=kOutput, calls=%fused_computation.20 | convolution fusion | flops 704643072 | bytes 3997700 | tf_op jit(solution)/shard_map/dot_general | solution.py:69
  115.7 2.5 %fusion.16 = f32[384,512]{1,0:T(8,128)S(1)} fusion(bf16[1,512,3584]{2,1,0:T(8,128)(2,1)} %param.13, s32[]{:T(128)S(6)} %select_n.29, bf16[384,3584]{1,0:T(8,128)(2,1)S(1)} %copy-done.7), kind=kOutput, calls=%fused_computation.24 | convolution fusion | flops 704643072 | bytes 3997700 | tf_op jit(solution)/shard_map/dot_general | solution.py:72
  118.3 2.4 %fusion.43 = f32[384,512]{1,0:T(8,128)S(1)} fusion(f32[384,512]{1,0:T(8,128)S(1)} %fusion.7, bf16[1,1792,512]{2,1,0:T(8,128)(2,1)S(1)} %copy-done.3, bf16[384,3584]{1,0:T(8,128)(2,1)} %collective-permute-done), kind=kOutput, calls=%fused_computation.39 | convolution fusion | flops 704839680 | bytes 4784128 | tf_op jit(solution)/shard_map/dot_general | solution.py:69
  120.7 2.5 %multiply_convert_fusion = (bf16[384,512]{1,0:T(8,128)(2,1)S(1)}, f32[384,512]{1,0:T(8,128)S(1)}) fusion(f32[384,512]{1,0:T(8,128)S(1)} %fusion.43, f32[384]{0:T(512)S(1)} %reshape.88, f32[384,512]{1,0:T(8,128)S(1)} %fusion.16, bf16[1,512,3584]{2,1,0:T(8,128)(2,1)S(1)} %copy-done.8, s32[]{:T(128)S(6)} %select_n.31, bf16[384,3584]{1,0:T(8,128)(2,1)} %collective-permute-done), kind=kOutput, calls=%fused_computation.50 | convolution fusion | flops 706215936 | bytes 5965828 | tf_op jit(solution)/shard_map/dot_general | solution.py:72
  123.3 2.5 %fusion.51 = bf16[384,512]{1,0:T(8,128)(2,1)S(1)} fusion(f32[384,512]{1,0:T(8,128)S(1)} %get-tuple-element.6, f32[384,512]{1,0:T(8,128)S(1)} %fusion.12, bf16[1,1792,512]{2,1,0:T(8,128)(2,1)S(1)} %copy-done.1, bf16[384,3584]{1,0:T(8,128)(2,1)} %collective-permute-done, f32[384,512]{1,0:T(8,128)S(1)} %fusion.43), kind=kOutput, calls=%fused_computation.41 | convolution fusion | flops 706805760 | bytes 5963776 | tf_op jit(solution)/shard_map/dot_general | solution.py:69
  126.0 0.9 fusion.5
  126.9 0.9 convolution_add_fusion.1
  128.3 2.4 %fusion.2 = f32[384,1792]{1,0:T(8,128)S(1)} fusion(bf16[2,1792,512]{2,1,0:T(8,128)(2,1)} %collective-permute-done.2, bf16[384,1024]{1,0:T(8,128)(2,1)S(1)} %collective-permute-done.1), kind=kOutput, calls=%fused_computation.9 | convolution fusion | flops 704643072 | bytes 4980736 | tf_op jit(solution)/shard_map/dot_general | solution.py:88
  130.7 2.4 %fusion.1 = bf16[384,1792]{1,0:T(8,128)(2,1)S(1)} fusion(f32[384,1792]{1,0:T(8,128)S(1)} %fusion.2, f32[384,1792]{1,0:T(8,128)S(1)} %convolution_add_fusion.1, bf16[2,1792,512]{2,1,0:T(8,128)(2,1)} %collective-permute-done.2, bf16[384,1024]{1,0:T(8,128)(2,1)S(1)} %collective-permute-done.1), kind=kOutput, calls=%fused_computation.6 | convolution fusion | flops 706707456 | bytes 9109504 | tf_op jit(solution)/shard_map/dot_general | solution.py:88
  133.1 0.9 reshape.85
  134.1 44.4 %all_to_all.11 = bf16[128,2,2688]{2,1,0:T(2,128)(2,1)} all-to-all(bf16[128,2,2688]{2,1,0:T(2,128)(2,1)S(1)} %reshape.85), channel_id=1, replica_groups=mesh['expert'=128,'tensor'=2] {'expert'}, dimensions={0} | all-to-all | bytes 2752512 | tf_op jit(solution)/shard_map/all_to_all | solution.py:99
  178.4 3.5 %reshape.86 = bf16[384,1792]{1,0:T(8,128)(2,1)S(1)} reshape(bf16[128,2,2688]{2,1,0:T(2,128)(2,1)} %all_to_all.11) | data formatting | bytes 2752512 | tf_op jit(solution)/shard_map/reshape | solution.py:101
  181.9 1.2 convolution_convert_fusion.1
  (49 shorter events, 5.6 us)
Async XLA Ops:
  103.9 14.4 %collective-permute-start = (bf16[384,3584]{1,0:T(8,128)(2,1)}, bf16[384,3584]{1,0:T(8,128)(2,1)}, u32[]{:S(2)}, u32[]{:S(2)}) collective-permute-start(bf16[384,3584]{1,0:T(8,128)(2,1)} %reshape.84), channel_id=1, source_target_pairs={{0,1},{1,0},{2,3},{3,2},{4,5},{5,4},{6,7},{7,6},{8,9},{9,8},{10,11... | collective-permute-start | bytes 8257544 | tf_op jit(solution)/shard_map/ppermute | solution.py:63
  103.9 2.6 %copy-start.5 = (bf16[1,3584,512]{2,1,0:T(8,128)(2,1)S(1)}, bf16[1,3584,512]{2,1,0:T(8,128)(2,1)}, u32[]{:S(2)}) copy-start(bf16[1,3584,512]{2,1,0:T(8,128)(2,1)} %param.12) | copy-start | bytes 11010052
  106.4 2.5 %copy-start.2 = (bf16[1,1792,512]{2,1,0:T(8,128)(2,1)}, bf16[1,1792,512]{2,1,0:T(8,128)(2,1)S(1)}, u32[]{:S(2)}) copy-start(bf16[1,1792,512]{2,1,0:T(8,128)(2,1)S(1)} %constant_dynamic-slice_fusion) | copy-start | bytes 5505028
  106.6 2.8 %copy-start = (bf16[1,1792,512]{2,1,0:T(8,128)(2,1)}, bf16[1,1792,512]{2,1,0:T(8,128)(2,1)S(1)}, u32[]{:S(2)}) copy-start(bf16[1,1792,512]{2,1,0:T(8,128)(2,1)S(1)} %constant_dynamic-slice_fusion.1) | copy-start | bytes 5505028
  109.4 18.5 %collective-permute-start.2 = (bf16[2,1792,512]{2,1,0:T(8,128)(2,1)}, bf16[2,1792,512]{2,1,0:T(8,128)(2,1)}, u32[]{:S(2)}, u32[]{:S(2)}) collective-permute-start(bf16[2,1792,512]{2,1,0:T(8,128)(2,1)} %pad_maximum_fusion), channel_id=1, source_target_pairs={{0,1},{1,0},{2,3},{3,2},{4,5},{5,4},{6,7},{7,6},{8,9},{9,8},{10,11... | collective-permute-start | bytes 11010056 | tf_op jit(solution)/shard_map/ppermute | solution.py:34
  110.3 3.0 %copy-start.6 = (bf16[1,3584,512]{2,1,0:T(8,128)(2,1)S(1)}, bf16[1,3584,512]{2,1,0:T(8,128)(2,1)}, u32[]{:S(2)}) copy-start(bf16[1,3584,512]{2,1,0:T(8,128)(2,1)} %param.12) | copy-start | bytes 11010052
  113.4 2.4 %copy-start.7 = (bf16[384,3584]{1,0:T(8,128)(2,1)S(1)}, bf16[384,3584]{1,0:T(8,128)(2,1)}, u32[]{:S(2)}) copy-start(bf16[384,3584]{1,0:T(8,128)(2,1)} %reshape.84) | copy-start | bytes 8257540
  115.7 2.6 %copy-start.3 = (bf16[1,1792,512]{2,1,0:T(8,128)(2,1)S(1)}, bf16[1,1792,512]{2,1,0:T(8,128)(2,1)}, u32[]{:S(2)}) copy-start(bf16[1,1792,512]{2,1,0:T(8,128)(2,1)} %copy-done.2) | copy-start | bytes 5505028
  118.3 2.5 %copy-start.8 = (bf16[1,512,3584]{2,1,0:T(8,128)(2,1)S(1)}, bf16[1,512,3584]{2,1,0:T(8,128)(2,1)}, u32[]{:S(2)}) copy-start(bf16[1,512,3584]{2,1,0:T(8,128)(2,1)} %param.13) | copy-start | bytes 11010052
  120.7 2.5 %copy-start.1 = (bf16[1,1792,512]{2,1,0:T(8,128)(2,1)S(1)}, bf16[1,1792,512]{2,1,0:T(8,128)(2,1)}, u32[]{:S(2)}) copy-start(bf16[1,1792,512]{2,1,0:T(8,128)(2,1)} %copy-done) | copy-start | bytes 5505028
  123.3 2.8 %copy-start.4 = (bf16[1,3584,512]{2,1,0:T(8,128)(2,1)S(1)}, bf16[1,3584,512]{2,1,0:T(8,128)(2,1)}, u32[]{:S(2)}) copy-start(bf16[1,3584,512]{2,1,0:T(8,128)(2,1)} %param.11) | copy-start | bytes 11010052
  125.9 2.4 %collective-permute-start.1 = (bf16[384,1024]{1,0:T(8,128)(2,1)S(1)}, bf16[384,1024]{1,0:T(8,128)(2,1)S(1)}, u32[]{:S(2)}, u32[]{:S(2)}) collective-permute-start(bf16[384,1024]{1,0:T(8,128)(2,1)S(1)} %pad_maximum_fusion.2), channel_id=1, source_target_pairs={{0,1},{1,0},{2,3},{3,2},{4,5},{5,4},{6,7},{7,6},{8,9},{9,8},{10,11... | collective-permute-start | bytes 2359304 | tf_op jit(solution)/shard_map/ppermute | solution.py:85

commit v11 on v5

--- a/solution.py
+++ b/solution.py
@@ -4,12 +4,12 @@
 from jax.sharding import PartitionSpec as P
 
 
-def fold_rows(rows, experts, lanes):
+def fold_rows(rows, experts, folds):
     per_expert = rows.size // experts
-    return rows.reshape(experts, 4, per_expert // 4)
+    return rows.reshape(experts, folds, per_expert // folds)
 
 
-def per_device(features, cotangent, expert_ids, route_weight, gate_weight, up_weight, down_weight):
+def device_body(features, cotangent, expert_ids, route_weight, gate_weight, up_weight, down_weight):
     experts = lax.axis_size("expert")
     parts = lax.axis_size("tensor")
     me = lax.axis_index("tensor")
@@ -46,24 +46,20 @@
     route_slot = destination[:, None] == jnp.arange(total, dtype=jnp.int32)[None, :]
     token_slot = jnp.sum(route_slot.reshape(tok_rows, top, total).astype(jnp.int32), axis=1)
     token_slot = token_slot.astype(jnp.bfloat16)
-    slot_weight = jnp.sum(
-        jnp.where(route_slot, route_weight.reshape(routes).astype(jnp.float32)[:, None], 0.0),
-        axis=0,
+    route_weight_slot = jnp.sum(
+        jnp.where(route_slot, route_weight.reshape(routes).astype(jnp.float32)[:, None], 0.0)
+        .reshape(tok_rows, top, total),
+        axis=1,
     ).astype(jnp.bfloat16)
 
     token_rows = jnp.concatenate([features, cotangent], axis=1)
     packed = lax.dot_general(
         token_slot, token_rows, (((0,), (0,)), ((), ())), preferred_element_type=jnp.float32
     ).astype(jnp.bfloat16)
-    row_part = fold_rows(packed, experts, 128)
-    weight4 = jnp.pad(slot_weight.reshape(experts, capacity), ((0, 0), (0, 4 - capacity)))
-    lane = jnp.arange(128, dtype=jnp.int32)[None, None, :]
-    weight_part = jnp.where(lane == 0, weight4[:, :, None], jnp.zeros((), jnp.bfloat16))
-    outgoing = jnp.concatenate([row_part, weight_part], axis=2)
-    fold = row_part.shape[2]
-    received = lax.all_to_all(outgoing, "expert", split_axis=0, concat_axis=0, tiled=True)
-    weights = received[:, :capacity, fold].reshape(total)
-    own_rows = received[:, :, :fold].reshape(total, 2 * half)
+    received = lax.all_to_all(
+        fold_rows(packed, experts, 4), "expert", split_axis=0, concat_axis=0, tiled=True
+    )
+    own_rows = received.reshape(total, 2 * half)
     got_rows = lax.ppermute(own_rows, "tensor", swap)
     other_cols = (me + 1) % parts * half
     own_down = lax.dynamic_slice_in_dim(down_w, me * half, half, axis=1)
@@ -81,7 +77,6 @@
     gate_pre = gate_up[:, :ffh]
     up_pre = gate_up[:, ffh:]
     hidden_grad = fwd_t(own_rows[:, half:], own_down) + fwd_t(got_rows[:, half:], other_down)
-    hidden_grad = hidden_grad * weights.astype(jnp.float32)[:, None]
     sigmoid_gate = jax.nn.sigmoid(gate_pre)
     gate_grad = (
         hidden_grad * up_pre * sigmoid_gate * (1.0 + gate_pre * (1.0 - sigmoid_gate))
@@ -90,10 +85,10 @@
     grads = jnp.concatenate([gate_grad, up_grad], axis=1)
     got_grads = lax.ppermute(grads, "tensor", swap)
     share = fwd_t(grads, own_gu) + fwd_t(got_grads, got_gu)
-    outgoing_back = fold_rows(share.astype(jnp.bfloat16), experts, 128)
+    outgoing_back = fold_rows(share.astype(jnp.bfloat16), experts, 2)
     returned = lax.all_to_all(outgoing_back, "expert", split_axis=0, concat_axis=0, tiled=True)
     summed = jnp.dot(
-        token_slot, returned.reshape(total, half), preferred_element_type=jnp.float32
+        route_weight_slot, returned.reshape(total, half), preferred_element_type=jnp.float32
     )
     return summed.astype(jnp.bfloat16)
 
@@ -110,5 +105,5 @@
     )
     out_specs = P("expert", "tensor")
     return jax.shard_map(
-        per_device, mesh=mesh, in_specs=in_specs, out_specs=out_specs, check_vma=False
+        device_body, mesh=mesh, in_specs=in_specs, out_specs=out_specs, check_vma=False
     )

time: 184 us -> 157 us (0.85)
  blocking collectives: 130 us -> 81.5 us
  waiting for transfers between devices: 0.62 us -> 37.7 us
  matrix products: 21.3 us -> 11.8 us
  starting transfers between devices: 0.6 us -> 8.53 us
  local copies, waits for them, and re-layouts: 23.2 us -> 15.3 us
  other arithmetic: 7.66 us -> 2.08 us
    all_to_all x2 -> x1, blocking collectives: 130 us -> 81.5 us  [device_body(): lax.all_to_all(fold_rows(packed, experts, 4), 'expert', split_axis=0, con...]
    all_to_all x0 -> x1, waiting for transfers between devices: none -> 37.5 us  [device_body(): lax.all_to_all(outgoing_back, 'expert', split_axis=0, concat_axis=0, tile...]
    all_to_all x0 -> x1, starting transfers between devices: none -> 7.15 us  [device_body(): lax.all_to_all(outgoing_back, 'expert', split_axis=0, concat_axis=0, tile...]
    dot_general x4, matrix products: 10.8 us -> 5.34 us  [fwd_t(): lax.dot_general(rows, weight, (((1,), (1,)), ((), ())), preferred_element...]
    dot_general x2, matrix products: 7.27 us -> 3.18 us  [fwd(): return jnp.dot(rows, weight, preferred_element_type=jnp.float32)]
    reshape x4, local copies, waits for them, and re-layouts: 12.2 us -> 8.58 us  [the longest x2 4.69 us: fold_rows(): return rows.reshape(experts, folds, per_expert // folds)]
    concatenate x2 -> x1, other arithmetic: 3.19 us -> 0.1 us  [device_body(): grads = jnp.concatenate([gate_grad, up_grad], axis=1)]
    slice x1 -> x0, local copies, waits for them, and re-layouts: 2.5 us -> none  [per_device(): own_rows = received[:, :, :fold].reshape(total, 2 * half)]
  transfers between devices with their start and end apart: 3 -> 4, of which waited for: 1 -> 2; matrix products, arithmetic and copies ran while one was open for 12% -> 7% of each run, Pallas kernels for 0% -> 0%
where the time goes in v11:
time: 157 us
  blocking collectives  81.5 us (52%)
  waiting for transfers between devices  37.7 us (24%)
  local copies, waits for them, and re-layouts  15.3 us (10%)
  matrix products  11.8 us (8%)
  starting transfers between devices  8.53 us (5%)
  other arithmetic  2.08 us (1%)
    all_to_all x1, blocking collectives, device_body(): lax.all_to_all(fold_rows(packed, experts, 4), 'expert', split_axis=0, con...  81.5 us
    all_to_all x1, waiting for transfers between devices, device_body(): lax.all_to_all(outgoing_back, 'expert', split_axis=0, concat_axis=0, tile...  37.5 us
    all_to_all x1, starting transfers between devices, device_body(): lax.all_to_all(outgoing_back, 'expert', split_axis=0, concat_axis=0, tile...  7.15 us
    dot_general x4, matrix products, fwd_t(): lax.dot_general(rows, weight, (((1,), (1,)), ((), ())), preferred_element...  5.34 us
    reshape x2, local copies, waits for them, and re-layouts, fold_rows(): return rows.reshape(experts, folds, per_expert // folds)  4.69 us
    dynamic_slice x1, local copies, waits for them, and re-layouts, rows_of(): lax.dynamic_slice_in_dim(up_w, start, half, axis=0)  3.62 us
    dot_general x2, matrix products, fwd(): return jnp.dot(rows, weight, preferred_element_type=jnp.float32)  3.18 us
  transfers between devices with their start and end apart: 4, of which 2 were waited for; matrix products, arithmetic and copies ran while one was open for 7% of the time, Pallas kernels for 0%

profile of v11, /device:TPU:32, one launch (start us, length us, event | category | flops | bytes accessed | tf_op | source)
XLA Modules:
  0.0 157.1 jit_solution(174443893183621583)
XLA Ops:
  0.0 0.8 copy.24
  1.9 0.7 multiply_add_fusion
  2.7 2.1 %convolution_convert_fusion = bf16[384,3584]{1,0:T(8,128)(2,1)S(1)} fusion(bf16[128,1792]{1,0:T(8,128)(2,1)} %param.8, bf16[128,1792]{1,0:T(8,128)(2,1)} %param.7, s32[128,384]{1,0:T(8,128)S(1)} %convert_reduce_fusion), kind=kOutput, calls=%fused_computation | convolution fusion | flops 355581952 | bytes 3866624 | tf_op jit(solution)/shard_map/dot_general | solution.py:56
  4.8 2.9 %reshape.75 = bf16[128,4,2688]{2,1,0:T(4,128)(2,1)} reshape(bf16[384,3584]{1,0:T(8,128)(2,1)S(1)} %convolution_convert_fusion) | data formatting | bytes 5505024 | tf_op jit(solution)/shard_map/reshape | solution.py:9
  7.7 81.5 %all_to_all.10 = bf16[128,4,2688]{2,1,0:T(4,128)(2,1)S(1)} all-to-all(bf16[128,4,2688]{2,1,0:T(4,128)(2,1)} %reshape.75), channel_id=1, replica_groups=mesh['expert'=128,'tensor'=2] {'expert'}, dimensions={0} | all-to-all | bytes 5505024 | tf_op jit(solution)/shard_map/all_to_all | solution.py:59
  89.2 3.0 %reshape.76 = bf16[384,3584]{1,0:T(8,128)(2,1)} reshape(bf16[128,4,2688]{2,1,0:T(4,128)(2,1)S(1)} %all_to_all.10) | data formatting | bytes 5505024 | tf_op jit(solution)/shard_map/reshape | solution.py:62
  92.2 3.6 %dynamic-slice_bitcast_fusion = (bf16[1792,512]{1,0:T(8,128)(2,1)S(1)}, bf16[1792,512]{1,0:T(8,128)(2,1)S(1)}, bf16[1792,512]{1,0:T(8,128)(2,1)S(1)}, bf16[1792,512]{1,0:T(8,128)(2,1)S(1)}) fusion(bf16[1,3584,512]{2,1,0:T(8,128)(2,1)} %param.12, s32[]{:T(128)S(6)} %select_n.27, s32[]{:T(128)S(6)} %select_n.25, bf16[1,3584,512]{2,1,0:T(8,128)(2,1)} %param.11), kind=kLoop, calls=%fused_computation.12 | loop fusion | bytes 14680072 | tf_op jit(solution)/shard_map/dynamic_slice | solution.py:33
  95.9 0.6 pad_maximum_fusion.1
  96.5 0.6 collective-permute-start.2
  97.1 0.6 copy-done
  97.6 1.1 copy-done.1
  98.7 0.9 fusion.5
  99.7 1.6 %fusion.2 = f32[384,1024]{1,0:T(8,128)S(1)} fusion(bf16[1792,512]{1,0:T(8,128)(2,1)S(1)} %get-tuple-element.8, bf16[1792,512]{1,0:T(8,128)(2,1)S(1)} %get-tuple-element.11, bf16[384,3584]{1,0:T(8,128)(2,1)S(1)} %copy-done), kind=kOutput, calls=%fused_computation.7 | convolution fusion | flops 1416626176 | bytes 6619136 | tf_op jit(solution)/shard_map/dot_general | solution.py:69
  101.2 1.6 %convolution_add_fusion.1 = f32[384,1024]{1,0:T(8,128)S(1)} fusion(f32[384,1024]{1,0:T(8,128)S(1)} %fusion.2, bf16[384,3584]{1,0:T(8,128)(2,1)S(1)} %collective-permute-done, bf16[1792,512]{1,0:T(8,128)(2,1)S(1)} %get-tuple-element.7, bf16[1792,512]{1,0:T(8,128)(2,1)S(1)} %get-tuple-element.12), kind=kOutput, calls=%fused_computation.18 | convolution fusion | flops 1417019392 | bytes 8192000 | tf_op jit(solution)/shard_map/dot_general | solution.py:69
  102.9 1.2 fusion.23
  104.1 0.8 collective-permute-start.1
  104.9 1.6 %fusion.1 = f32[384,1792]{1,0:T(8,128)S(1)} fusion(bf16[1792,512]{1,0:T(8,128)(2,1)S(1)} %get-tuple-element.8, bf16[1792,512]{1,0:T(8,128)(2,1)S(1)} %get-tuple-element.11, bf16[384,512]{1,0:T(8,128)(2,1)S(1)} %get-tuple-element.10, bf16[384,512]{1,0:T(8,128)(2,1)S(1)} %get-tuple-element.9), kind=kOutput, calls=%fused_computation.6 | convolution fusion | flops 1418199040 | bytes 7208960 | tf_op jit(solution)/shard_map/dot_general | solution.py:72
  106.6 0.3 collective-permute-done.1
  106.8 1.7 %fusion = bf16[384,1792]{1,0:T(8,128)(2,1)S(1)} fusion(f32[384,1792]{1,0:T(8,128)S(1)} %fusion.1, bf16[384,1024]{1,0:T(8,128)(2,1)S(1)} %collective-permute-done.1, bf16[1792,1024]{1,0:T(8,128)(2,1)S(1)} %collective-permute-done.2), kind=kOutput, calls=%fused_computation.4 | convolution fusion | flops 1410662400 | bytes 8585216 | tf_op jit(solution)/shard_map/dot_general | solution.py:72
  108.5 1.8 %reshape.77 = bf16[128,2,2688]{2,1,0:T(2,128)(2,1)} reshape(bf16[384,1792]{1,0:T(8,128)(2,1)S(1)} %fusion) | data formatting | bytes 2752512 | tf_op jit(solution)/shard_map/reshape | solution.py:9
  110.3 7.1 %all-to-all-start.1 = ((bf16[128,2,2688]{2,1,0:T(2,128)(2,1)}), bf16[128,2,2688]{2,1,0:T(2,128)(2,1)S(1)}, u32[]{:S(2)}, u32[]{:S(2)}) async-start(bf16[128,2,2688]{2,1,0:T(2,128)(2,1)} %reshape.77), calls=%async_computation.1 | async-start | bytes 2752512 | tf_op jit(solution)/shard_map/all_to_all | solution.py:89
  117.6 37.5 %all-to-all-done.1 = bf16[128,2,2688]{2,1,0:T(2,128)(2,1)S(1)} async-done(((bf16[128,2,2688]{2,1,0:T(2,128)(2,1)}), bf16[128,2,2688]{2,1,0:T(2,128)(2,1)S(1)}, u32[]{:S(2)}, u32[]{:S(2)}) %all-to-all-start.1) | async-done | bytes 1376288 | tf_op jit(solution)/shard_map/all_to_all | solution.py:89
  155.1 0.9 reshape.78
  156.0 1.2 convolution_convert_fusion.1
  (23 shorter events, 1.4 us)
Async XLA Ops:
  92.2 9.0 %collective-permute-start = (bf16[384,3584]{1,0:T(8,128)(2,1)}, bf16[384,3584]{1,0:T(8,128)(2,1)S(1)}, u32[]{:S(2)}, u32[]{:S(2)}) collective-permute-start(bf16[384,3584]{1,0:T(8,128)(2,1)} %reshape.76), channel_id=1, source_target_pairs={{0,1},{1,0},{2,3},{3,2},{4,5},{5,4},{6,7},{7,6},{8,9},{9,8},{10,11... | collective-permute-start | bytes 8257544 | tf_op jit(solution)/shard_map/ppermute | solution.py:63
  95.9 1.8 %copy-start = (bf16[384,3584]{1,0:T(8,128)(2,1)S(1)}, bf16[384,3584]{1,0:T(8,128)(2,1)}, u32[]{:S(2)}) copy-start(bf16[384,3584]{1,0:T(8,128)(2,1)} %reshape.76) | copy-start | bytes 8257540
  95.9 2.9 %copy-start.1 = (bf16[1,512,3584]{2,1,0:T(8,128)(2,1)S(1)}, bf16[1,512,3584]{2,1,0:T(8,128)(2,1)}, u32[]{:S(2)}) copy-start(bf16[1,512,3584]{2,1,0:T(8,128)(2,1)} %param.13) | copy-start | bytes 11010052
  96.5 10.1 %collective-permute-start.2 = (bf16[1792,1024]{1,0:T(8,128)(2,1)S(1)}, bf16[1792,1024]{1,0:T(8,128)(2,1)S(1)}, u32[]{:S(2)}, u32[]{:S(2)}) collective-permute-start(bf16[1792,1024]{1,0:T(8,128)(2,1)S(1)} %pad_maximum_fusion.1), channel_id=1, source_target_pairs={{0,1},{1,0},{2,3},{3,2},{4,5},{5,4},{6,7},{7,6},{8,9},{9,8},{10,11... | collective-permute-start | bytes 11010056 | tf_op jit(solution)/shard_map/ppermute | solution.py:39
  104.1 2.7 %collective-permute-start.1 = (bf16[384,1024]{1,0:T(8,128)(2,1)S(1)}, bf16[384,1024]{1,0:T(8,128)(2,1)S(1)}, u32[]{:S(2)}, u32[]{:S(2)}) collective-permute-start(bf16[384,1024]{1,0:T(8,128)(2,1)S(1)} %pad_maximum_fusion.4), channel_id=1, source_target_pairs={{0,1},{1,0},{2,3},{3,2},{4,5},{5,4},{6,7},{7,6},{8,9},{9,8},{10,11... | collective-permute-start | bytes 2359304 | tf_op jit(solution)/shard_map/ppermute | solution.py:86
  108.5 8.9 %copy-start.2 = (bf16[128,2]{0,1:T(2,128)(2,1)S(1)}, bf16[128,2]{0,1:T(2,128)(2,1)}, u32[]{:S(2)}) copy-start(bf16[128,2]{0,1:T(2,128)(2,1)} %param.10) | copy-start | bytes 1540
  110.3 44.8 %all-to-all-start.1 = ((bf16[128,2,2688]{2,1,0:T(2,128)(2,1)}), bf16[128,2,2688]{2,1,0:T(2,128)(2,1)S(1)}, u32[]{:S(2)}, u32[]{:S(2)}) async-start(bf16[128,2,2688]{2,1,0:T(2,128)(2,1)} %reshape.77), calls=%async_computation.1 | async-start | bytes 2752512 | tf_op jit(solution)/shard_map/all_to_all | solution.py:89

commit v12 on v5

--- a/solution.py
+++ b/solution.py
@@ -4,12 +4,12 @@
 from jax.sharding import PartitionSpec as P
 
 
-def fold_rows(rows, experts, lanes):
+def fold_rows(rows, experts, folds):
     per_expert = rows.size // experts
-    return rows.reshape(experts, 4, per_expert // 4)
+    return rows.reshape(experts, folds, per_expert // folds)
 
 
-def per_device(features, cotangent, expert_ids, route_weight, gate_weight, up_weight, down_weight):
+def device_body(features, cotangent, expert_ids, route_weight, gate_weight, up_weight, down_weight):
     experts = lax.axis_size("expert")
     parts = lax.axis_size("tensor")
     me = lax.axis_index("tensor")
@@ -55,7 +55,7 @@
     packed = lax.dot_general(
         token_slot, token_rows, (((0,), (0,)), ((), ())), preferred_element_type=jnp.float32
     ).astype(jnp.bfloat16)
-    row_part = fold_rows(packed, experts, 128)
+    row_part = fold_rows(packed, experts, 4)
     weight4 = jnp.pad(slot_weight.reshape(experts, capacity), ((0, 0), (0, 4 - capacity)))
     lane = jnp.arange(128, dtype=jnp.int32)[None, None, :]
     weight_part = jnp.where(lane == 0, weight4[:, :, None], jnp.zeros((), jnp.bfloat16))
@@ -90,7 +90,7 @@
     grads = jnp.concatenate([gate_grad, up_grad], axis=1)
     got_grads = lax.ppermute(grads, "tensor", swap)
     share = fwd_t(grads, own_gu) + fwd_t(got_grads, got_gu)
-    outgoing_back = fold_rows(share.astype(jnp.bfloat16), experts, 128)
+    outgoing_back = fold_rows(share.astype(jnp.bfloat16), experts, 2)
     returned = lax.all_to_all(outgoing_back, "expert", split_axis=0, concat_axis=0, tiled=True)
     summed = jnp.dot(
         token_slot, returned.reshape(total, half), preferred_element_type=jnp.float32
@@ -110,5 +110,5 @@
     )
     out_specs = P("expert", "tensor")
     return jax.shard_map(
-        per_device, mesh=mesh, in_specs=in_specs, out_specs=out_specs, check_vma=False
+        device_body, mesh=mesh, in_specs=in_specs, out_specs=out_specs, check_vma=False
     )

time: 184 us -> 180 us (0.978)
  local copies, waits for them, and re-layouts: 23.2 us -> 20.6 us
  blocking collectives: 130 us -> 128 us
    reshape x4, local copies, waits for them, and re-layouts: 12.2 us -> 9.57 us  [the longest x1 4.82 us: device_body(): own_rows = received[:, :, :fold].reshape(total, 2 * half)]
  transfers between devices with their start and end apart: 3 -> 3, of which waited for: 1 -> 1; matrix products, arithmetic and copies ran while one was open for 12% -> 13% of each run, Pallas kernels for 0% -> 0%
where the time goes in v12:
time: 180 us; the launch traced here: 179 us
  blocking collectives  128 us (71%)
  matrix products  21.3 us (12%)
  local copies, waits for them, and re-layouts  20.6 us (11%)
  other arithmetic  7.66 us (4%)
    all_to_all x1, blocking collectives, device_body(): lax.all_to_all(outgoing, 'expert', split_axis=0, concat_axis=0, tiled=True)  84.2 us
    all_to_all x1, blocking collectives, device_body(): lax.all_to_all(outgoing_back, 'expert', split_axis=0, concat_axis=0, tile...  44.3 us
    dot_general x4, matrix products, fwd_t(): lax.dot_general(rows, weight, (((1,), (1,)), ((), ())), preferred_element...  10.8 us
    dot_general x2, matrix products, fwd(): return jnp.dot(rows, weight, preferred_element_type=jnp.float32)  7.27 us
    dynamic_slice x1, local copies, waits for them, and re-layouts, rows_of(): lax.dynamic_slice_in_dim(up_w, start, half, axis=0)  5.41 us
    reshape x1, local copies, waits for them, and re-layouts, device_body(): own_rows = received[:, :, :fold].reshape(total, 2 * half)  4.82 us
    reshape x2, local copies, waits for them, and re-layouts, fold_rows(): return rows.reshape(experts, folds, per_expert // folds)  3.85 us
  transfers between devices with their start and end apart: 3, of which 1 were waited for; matrix products, arithmetic and copies ran while one was open for 13% of the time, Pallas kernels for 0%

profile of v12, /device:TPU:32, one launch (start us, length us, event | category | flops | bytes accessed | tf_op | source)
XLA Modules:
  0.0 179.4 jit_solution(8146739538600927923)
XLA Ops:
  0.0 0.8 copy.44
  1.9 0.7 multiply_add_fusion.1
  2.6 0.8 copy.49
  4.1 2.1 %convolution_convert_fusion = bf16[384,3584]{1,0:T(8,128)(2,1)S(1)} fusion(bf16[128,1792]{1,0:T(8,128)(2,1)} %param.8, bf16[128,1792]{1,0:T(8,128)(2,1)} %param.7, s32[128,384]{1,0:T(8,128)S(1)} %convert_reduce_fusion), kind=kOutput, calls=%fused_computation | convolution fusion | flops 355581952 | bytes 3866624 | tf_op jit(solution)/shard_map/dot_general | solution.py:55
  6.1 2.9 %reshape.81 = bf16[128,4,2688]{2,1,0:T(4,128)(2,1)} reshape(bf16[384,3584]{1,0:T(8,128)(2,1)S(1)} %convolution_convert_fusion) | data formatting | bytes 5505024 | tf_op jit(solution)/shard_map/reshape | solution.py:9
  9.3 3.1 %pad_maximum_fusion.2 = bf16[128,4,2816]{2,1,0:T(4,128)(2,1)S(1)} fusion(bf16[128,4,128]{2,1,0:T(4,128)(2,1)S(1)} %broadcast_select_fusion, bf16[128,4,2688]{2,1,0:T(4,128)(2,1)} %reshape.81), kind=kLoop, calls=%fused_computation.4 | loop fusion | flops 5767168 | bytes 5767168 | tf_op jit(solution)/shard_map/concatenate | solution.py:62
  12.4 84.2 %all_to_all.10 = bf16[128,4,2816]{2,1,0:T(4,128)(2,1)S(1)} all-to-all(bf16[128,4,2816]{2,1,0:T(4,128)(2,1)S(1)} %pad_maximum_fusion.2), channel_id=1, replica_groups=mesh['expert'=128,'tensor'=2] {'expert'}, dimensions={0} | all-to-all | bytes 5767168 | tf_op jit(solution)/shard_map/all_to_all | solution.py:64
  96.5 2.5 %slice.41 = bf16[128,4,2688]{2,1,0:T(4,128)(2,1)} slice(bf16[128,4,2816]{2,1,0:T(4,128)(2,1)S(1)} %all_to_all.10), slice={[0:128], [0:4], [0:2688]} | slice | bytes 5505024 | tf_op jit(solution)/shard_map/slice | solution.py:66
  99.0 4.8 %reshape.82 = bf16[384,3584]{1,0:T(8,128)(2,1)} reshape(bf16[128,4,2688]{2,1,0:T(4,128)(2,1)} %slice.41) | data formatting | bytes 5505024 | tf_op jit(solution)/shard_map/reshape | solution.py:66
  103.9 5.4 %dynamic-slice_bitcast_fusion = (bf16[1792,512]{1,0:T(8,128)(2,1)S(1)}, bf16[1792,512]{1,0:T(8,128)(2,1)}, bf16[1792,512]{1,0:T(8,128)(2,1)}, bf16[1792,512]{1,0:T(8,128)(2,1)S(1)}) fusion(bf16[1,3584,512]{2,1,0:T(8,128)(2,1)} %param.12, s32[]{:T(128)S(6)} %select_n.31, s32[]{:T(128)S(6)} %select_n.29, bf16[1,3584,512]{2,1,0:T(8,128)(2,1)} %param.11), kind=kLoop, calls=%fused_computation.13 | loop fusion | bytes 14680072 | tf_op jit(solution)/shard_map/dynamic_slice | solution.py:33
  109.3 2.6 %pad_maximum_fusion.1 = bf16[1792,1024]{1,0:T(8,128)(2,1)} fusion(bf16[1792,512]{1,0:T(8,128)(2,1)S(1)} %get-tuple-element.7, bf16[1792,512]{1,0:T(8,128)(2,1)S(1)} %get-tuple-element.12), kind=kLoop, calls=%fused_computation.2 | loop fusion | flops 7340032 | bytes 7340032 | tf_op jit(solution)/shard_map/concatenate | solution.py:30
  111.9 0.3 copy-done.2
  112.2 0.5 collective-permute-start.2
  113.1 2.8 %fusion.5 = f32[384,512]{1,0:T(8,128)S(1)} fusion(bf16[1,512,3584]{2,1,0:T(8,128)(2,1)} %param.13, s32[]{:T(128)S(6)} %select_n.29, bf16[384,3584]{1,0:T(8,128)(2,1)} %reshape.82), kind=kOutput, calls=%fused_computation.11 | convolution fusion | flops 704643072 | bytes 3997700 | tf_op jit(solution)/shard_map/dot_general | solution.py:76
  116.0 4.2 %fusion.2 = f32[384,1024]{1,0:T(8,128)S(1)} fusion(bf16[1792,512]{1,0:T(8,128)(2,1)} %get-tuple-element.8, bf16[1792,512]{1,0:T(8,128)(2,1)} %get-tuple-element.11, bf16[384,3584]{1,0:T(8,128)(2,1)} %reshape.82), kind=kOutput, calls=%fused_computation.8 | convolution fusion | flops 1416626176 | bytes 6619136 | tf_op jit(solution)/shard_map/dot_general | solution.py:73
  120.2 3.1 %convolution_add_fusion.1 = f32[384,1024]{1,0:T(8,128)S(1)} fusion(f32[384,1024]{1,0:T(8,128)S(1)} %fusion.2, bf16[384,3584]{1,0:T(8,128)(2,1)} %collective-permute-done, bf16[1792,512]{1,0:T(8,128)(2,1)S(1)} %copy-done.1, bf16[1792,512]{1,0:T(8,128)(2,1)S(1)} %copy-done.3), kind=kOutput, calls=%fused_computation.19 | convolution fusion | flops 1417019392 | bytes 8192000 | tf_op jit(solution)/shard_map/dot_general | solution.py:73
  123.4 2.7 %fusion.28 = (bf16[384,512]{1,0:T(8,128)(2,1)S(1)}, bf16[384,512]{1,0:T(8,128)(2,1)S(1)}) fusion(f32[384,1024]{1,0:T(8,128)S(1)} %convolution_add_fusion.1, f32[384]{0:T(512)S(1)} %reshape.86, f32[384,512]{1,0:T(8,128)S(1)} %fusion.5, bf16[1,512,3584]{2,1,0:T(8,128)(2,1)S(1)} %copy-done.6, s32[]{:T(128)S(6)} %select_n.31, ...), kind=kOutput, calls=%fused_computation.32 | convolution fusion | flops 707592192 | bytes 6359044 | tf_op jit(solution)/shard_map/dot_general | solution.py:76
  126.3 1.6 fusion.1
  127.9 0.6 collective-permute-done.1
  128.5 3.7 %fusion = bf16[384,1792]{1,0:T(8,128)(2,1)S(1)} fusion(f32[384,1792]{1,0:T(8,128)S(1)} %fusion.1, bf16[384,1024]{1,0:T(8,128)(2,1)S(1)} %collective-permute-done.1, bf16[1792,1024]{1,0:T(8,128)(2,1)} %collective-permute-done.2), kind=kOutput, calls=%fused_computation.5 | convolution fusion | flops 1410662400 | bytes 8585216 | tf_op jit(solution)/shard_map/dot_general | solution.py:76
  132.2 0.9 reshape.83
  133.1 44.3 %all_to_all.11 = bf16[128,2,2688]{2,1,0:T(2,128)(2,1)S(1)} all-to-all(bf16[128,2,2688]{2,1,0:T(2,128)(2,1)S(1)} %reshape.83), channel_id=1, replica_groups=mesh['expert'=128,'tensor'=2] {'expert'}, dimensions={0} | all-to-all | bytes 2752512 | tf_op jit(solution)/shard_map/all_to_all | solution.py:94
  177.4 0.9 reshape.84
  178.3 1.2 convolution_convert_fusion.1
  (40 shorter events, 2.6 us)
Async XLA Ops:
  103.9 16.4 %collective-permute-start = (bf16[384,3584]{1,0:T(8,128)(2,1)}, bf16[384,3584]{1,0:T(8,128)(2,1)}, u32[]{:S(2)}, u32[]{:S(2)}) collective-permute-start(bf16[384,3584]{1,0:T(8,128)(2,1)} %reshape.82), channel_id=1, source_target_pairs={{0,1},{1,0},{2,3},{3,2},{4,5},{5,4},{6,7},{7,6},{8,9},{9,8},{10,11... | collective-permute-start | bytes 8257544 | tf_op jit(solution)/shard_map/ppermute | solution.py:67
  109.3 2.6 %copy-start = (bf16[1792,512]{1,0:T(8,128)(2,1)}, bf16[1792,512]{1,0:T(8,128)(2,1)S(1)}, u32[]{:S(2)}) copy-start(bf16[1792,512]{1,0:T(8,128)(2,1)S(1)} %get-tuple-element.7) | copy-start | bytes 5505028
  109.3 2.9 %copy-start.2 = (bf16[1792,512]{1,0:T(8,128)(2,1)}, bf16[1792,512]{1,0:T(8,128)(2,1)S(1)}, u32[]{:S(2)}) copy-start(bf16[1792,512]{1,0:T(8,128)(2,1)S(1)} %get-tuple-element.12) | copy-start | bytes 5505028
  112.2 15.7 %collective-permute-start.2 = (bf16[1792,1024]{1,0:T(8,128)(2,1)}, bf16[1792,1024]{1,0:T(8,128)(2,1)}, u32[]{:S(2)}, u32[]{:S(2)}) collective-permute-start(bf16[1792,1024]{1,0:T(8,128)(2,1)} %pad_maximum_fusion.1), channel_id=1, source_target_pairs={{0,1},{1,0},{2,3},{3,2},{4,5},{5,4},{6,7},{7,6},{8,9},{9,8},{10,11... | collective-permute-start | bytes 11010056 | tf_op jit(solution)/shard_map/ppermute | solution.py:39
  116.0 4.2 %copy-start.1 = (bf16[1792,512]{1,0:T(8,128)(2,1)S(1)}, bf16[1792,512]{1,0:T(8,128)(2,1)}, u32[]{:S(2)}) copy-start(bf16[1792,512]{1,0:T(8,128)(2,1)} %copy-done) | copy-start | bytes 5505028
  116.0 4.2 %copy-start.3 = (bf16[1792,512]{1,0:T(8,128)(2,1)S(1)}, bf16[1792,512]{1,0:T(8,128)(2,1)}, u32[]{:S(2)}) copy-start(bf16[1792,512]{1,0:T(8,128)(2,1)} %copy-done.2) | copy-start | bytes 5505028
  120.2 3.1 %copy-start.6 = (bf16[1,512,3584]{2,1,0:T(8,128)(2,1)S(1)}, bf16[1,512,3584]{2,1,0:T(8,128)(2,1)}, u32[]{:S(2)}) copy-start(bf16[1,512,3584]{2,1,0:T(8,128)(2,1)} %param.13) | copy-start | bytes 11010052
  123.3 2.9 %copy-start.4 = (bf16[1792,512]{1,0:T(8,128)(2,1)S(1)}, bf16[1792,512]{1,0:T(8,128)(2,1)}, u32[]{:S(2)}) copy-start(bf16[1792,512]{1,0:T(8,128)(2,1)} %get-tuple-element.8) | copy-start | bytes 5505028
  123.3 2.9 %copy-start.5 = (bf16[1792,512]{1,0:T(8,128)(2,1)S(1)}, bf16[1792,512]{1,0:T(8,128)(2,1)}, u32[]{:S(2)}) copy-start(bf16[1792,512]{1,0:T(8,128)(2,1)} %get-tuple-element.11) | copy-start | bytes 5505028
  126.1 2.4 %collective-permute-start.1 = (bf16[384,1024]{1,0:T(8,128)(2,1)S(1)}, bf16[384,1024]{1,0:T(8,128)(2,1)S(1)}, u32[]{:S(2)}, u32[]{:S(2)}) collective-permute-start(bf16[384,1024]{1,0:T(8,128)(2,1)S(1)} %pad_maximum_fusion.5), channel_id=1, source_target_pairs={{0,1},{1,0},{2,3},{3,2},{4,5},{5,4},{6,7},{7,6},{8,9},{9,8},{10,11... | collective-permute-start | bytes 2359304 | tf_op jit(solution)/shard_map/ppermute | solution.py:91
